TPU v7x, 128 devices: a whole 4x4x4 slice. The times are simulated.
128 devices in a mesh: req: 8 (over y, core), exp: 16 (over z, x).
Axes of the slice: x: 4, y: 4, z: 4, core: 2. Of those that a mesh axis runs over, the one named last changes fastest.
Arguments:
- hidden: bfloat16 [16384, 2560], P(('req', 'exp')), may hold values from -1.5 to 1.5
- queries: bfloat16 [16384, 1280], P(('req', 'exp')), may hold values from -100 to 100
- suffix_kv: bfloat16 [16384, 512], P(('req', 'exp')), may hold values from -24 to 24
- lengths: int32 [8, 4], P('req'), may hold values from 1 to 1024, 2048 in all within a row
- page_table: int32 [8, 4, 32], P('req'), may hold values from 0 to 55
- page_pool: bfloat16 [56, 128, 512], P('req'), may hold values from -24 to 24
- w_out: bfloat16 [1280, 2560], replicated, may hold values from -0.15625 to 0.15625
- w_router: bfloat16 [2560, 64], replicated, may hold values from -5 to 5
- routes: int32 [16384, 6], P(('req', 'exp')), may hold values from 0 to 63, all different within a row; in each aligned block of 128 rows (0 to 127, 128 to 255, ...) at most 15 rows name the same one
- w_gate: bfloat16 [128, 2560, 768], P(('req', 'exp')), may hold values from -0.125 to 0.125
- w_up: bfloat16 [128, 2560, 768], P(('req', 'exp')), may hold values from -0.125 to 0.125
- w_down: bfloat16 [128, 768, 2560], P(('req', 'exp')), may hold values from -0.4375 to 0.4375
Outputs:
- layer_out: bfloat16 [16384, 2560], P(('req', 'exp'))
Inputs may be any that keep to these rules, and one draw needn't show every extreme that they name: `lengths`: each row sums to 2048; its largest entry is exactly 1024. `page_table`: a page may appear in several prefixes and more than once in one. `routes`: the 6 experts of a token are distinct; among the rows of one device no expert is named more than 15 times, a bound that some block reaches.
All inputs are finite; a program needn't handle non-finite values.
Results may differ from a plain program's by a relative error of at most 0.022.
Values may be sent and summed in bfloat16 or wider, within the bound.
No kernel may reach another device: no remote copies, remote signals or barrier semaphores. Data moves between devices by JAX's collectives and lax.ppermute only.
A program may use at most 192 MiB of HBM per device.

v0:
```python
import math

import jax
import jax.numpy as jnp
from jax import lax
from jax.sharding import PartitionSpec as P

D = 2560
QUERY_HEADS = 10
KEY_VALUE_HEADS = 2
HEAD_SIZE = 128
TOP = 6
PAGE_TOKENS = 128


NEGATIVE_MASK = -1e30
EPS = 1e-06


def fold_scores(carry, query_matrix, key_rows, value_rows, weights):
    scores = jnp.einsum(
        "tgrd,kgd->tgrk", query_matrix, key_rows, preferred_element_type=jnp.float32
    ) * (1.0 / math.sqrt(HEAD_SIZE))
    running_maximum, grand_total, summed_output = carry
    live = weights[:, None, None, :] > 0
    fresh = jnp.maximum(running_maximum, jnp.max(jnp.where(live, scores, NEGATIVE_MASK), axis=-1))
    expo = jnp.where(live, jnp.exp(scores - fresh[..., None]), 0.0) * weights[:, None, None, :]
    decay = jnp.exp(running_maximum - fresh)
    grand_total = decay * grand_total + jnp.sum(expo, axis=-1)
    summed_output = decay[..., None] * summed_output + jnp.einsum(
        "tgrk,kgd->tgrd", expo.astype(jnp.bfloat16), value_rows, preferred_element_type=jnp.float32
    )
    return (fresh, grand_total, summed_output)


def empty_carry(token_count, request_groups):
    return (
        jnp.full((token_count, KEY_VALUE_HEADS, request_groups), NEGATIVE_MASK, jnp.float32),
        jnp.zeros((token_count, KEY_VALUE_HEADS, request_groups), jnp.float32),
        jnp.zeros((token_count, KEY_VALUE_HEADS, request_groups, HEAD_SIZE), jnp.float32),
    )


def on_device(
    hidden,
    queries,
    suffix_kv,
    lengths,
    page_table,
    page_pool,
    w_out,
    w_router,
    routes,
    w_gate,
    w_up,
    w_down,
):
    token_index = hidden.shape[0]
    row_width = KEY_VALUE_HEADS * HEAD_SIZE
    request_groups = QUERY_HEADS // KEY_VALUE_HEADS
    request_count = lax.axis_size("req")
    pool_per_shard = page_pool.shape[0]
    pool_all = pool_per_shard * request_count
    query_matrix = queries.reshape(token_index, KEY_VALUE_HEADS, request_groups, HEAD_SIZE)
    positions = lax.axis_index("exp") * token_index + jnp.arange(token_index, dtype=jnp.int32)
    lens = lengths[0]
    ends = jnp.cumsum(lens)
    starts = ends - lens
    req_of = jnp.sum((positions[:, None] >= ends[None, :]).astype(jnp.int32), axis=1)
    pick = req_of[:, None] == jnp.arange(lens.shape[0], dtype=jnp.int32)[None, :]
    first = jnp.sum(jnp.where(pick, starts[None, :], 0), axis=1)
    counts = jnp.sum(
        (page_table[0][:, :, None] == jnp.arange(pool_all, dtype=jnp.int32)[None, None, :]).astype(
            jnp.float32
        ),
        axis=1,
    )
    query_counts = jnp.dot(pick.astype(jnp.float32), counts, precision=lax.Precision.HIGHEST)
    query_total_set, every_count = (
        lax.all_gather(queries, "req", axis=0, tiled=True),
        lax.all_gather(query_counts.astype(jnp.bfloat16), "req", axis=0, tiled=True),
    )
    query_total_count = query_total_set.shape[0]
    local = lax.dynamic_slice_in_dim(
        every_count, lax.axis_index("req") * pool_per_shard, pool_per_shard, 1
    ).astype(jnp.float32)
    weights = jnp.repeat(local, PAGE_TOKENS, axis=1)
    flattened = page_pool.reshape(pool_per_shard * PAGE_TOKENS, 2 * row_width)
    key_rows = flattened[:, :row_width].reshape(
        pool_per_shard * PAGE_TOKENS, KEY_VALUE_HEADS, HEAD_SIZE
    )
    value_rows = flattened[:, row_width:].reshape(
        pool_per_shard * PAGE_TOKENS, KEY_VALUE_HEADS, HEAD_SIZE
    )
    running_maximum, grand_total, summed_output = fold_scores(
        empty_carry(query_total_count, request_groups),
        query_total_set.reshape(query_total_count, KEY_VALUE_HEADS, request_groups, HEAD_SIZE),
        key_rows,
        value_rows,
        weights,
    )
    peaks, totals, sums = (
        lax.all_to_all(
            running_maximum.reshape(request_count, token_index, KEY_VALUE_HEADS, request_groups),
            "req",
            split_axis=0,
            concat_axis=0,
            tiled=True,
        ),
        lax.all_to_all(
            grand_total.reshape(request_count, token_index, KEY_VALUE_HEADS, request_groups),
            "req",
            split_axis=0,
            concat_axis=0,
            tiled=True,
        ),
        lax.all_to_all(
            summed_output.reshape(
                request_count, token_index, KEY_VALUE_HEADS, request_groups, HEAD_SIZE
            ),
            "req",
            split_axis=0,
            concat_axis=0,
            tiled=True,
        ),
    )
    highest = jnp.max(peaks, axis=0)
    factor = jnp.exp(peaks - highest[None])
    carry = (highest, jnp.sum(factor * totals, axis=0), jnp.sum(factor[..., None] * sums, axis=0))
    segment = lax.all_gather(suffix_kv, "exp", axis=0, tiled=True)
    token_count = segment.shape[0]
    keypos = jnp.arange(token_count, dtype=jnp.int32)
    weights = (
        (keypos[None, :] <= positions[:, None]) & (keypos[None, :] >= first[:, None])
    ).astype(jnp.float32)
    key_rows = segment[:, :row_width].reshape(token_count, KEY_VALUE_HEADS, HEAD_SIZE)
    value_rows = segment[:, row_width:].reshape(token_count, KEY_VALUE_HEADS, HEAD_SIZE)
    running_maximum, grand_total, summed_output = fold_scores(
        carry, query_matrix, key_rows, value_rows, weights
    )
    attended = (
        (summed_output / grand_total[..., None])
        .reshape(token_index, QUERY_HEADS * HEAD_SIZE)
        .astype(jnp.bfloat16)
    )
    projected = jnp.dot(attended, w_out, preferred_element_type=jnp.float32)
    resid = lax.optimization_barrier((hidden.astype(jnp.float32) + projected).astype(jnp.bfloat16))
    resid_f = resid.astype(jnp.float32)
    normed = (resid_f * lax.rsqrt(jnp.mean(resid_f * resid_f, axis=1, keepdims=True) + EPS)).astype(
        jnp.bfloat16
    )
    n_experts = w_router.shape[1]
    logits = jnp.dot(normed, w_router, preferred_element_type=jnp.float32)
    expert_ids = jnp.arange(n_experts, dtype=jnp.int32)
    chosen = jnp.sum(
        jnp.where(routes[:, :, None] == expert_ids[None, None, :], logits[:, None, :], 0.0), axis=2
    )
    gates = jax.nn.softmax(chosen, axis=1)
    capacity = max(2, (5 * token_index * TOP + 4 * n_experts - 1) // (4 * n_experts))
    flat_routes = routes.reshape(-1)
    onehot = (flat_routes[:, None] == expert_ids[None, :]).astype(jnp.int32)
    rank = jnp.sum(jnp.cumsum(onehot, axis=0) * onehot, axis=1) - 1
    slot = flat_routes * capacity + rank
    send = (
        jnp.zeros((n_experts * capacity, D), jnp.bfloat16)
        .at[slot]
        .set(jnp.repeat(normed, TOP, axis=0))
    )
    outgoing = jnp.broadcast_to(
        send.reshape(n_experts, 1, capacity, D), (n_experts, 2, capacity, D)
    ).reshape(2 * n_experts, capacity, D)
    rows = lax.all_to_all(outgoing, ("req", "exp"), split_axis=0, concat_axis=0, tiled=True)
    array_shape = rows.shape
    flat_rows = rows.reshape(-1, D)
    gate_part = jnp.dot(flat_rows, w_gate[0], preferred_element_type=jnp.float32)
    up_part = jnp.dot(flat_rows, w_up[0], preferred_element_type=jnp.float32)
    inner = (jax.nn.silu(gate_part) * up_part).astype(jnp.bfloat16)
    returned = lax.all_to_all(
        jnp.dot(inner, w_down[0], preferred_element_type=jnp.float32)
        .astype(jnp.bfloat16)
        .reshape(array_shape),
        ("req", "exp"),
        split_axis=0,
        concat_axis=0,
        tiled=True,
    )
    halves = jnp.sum(
        returned.reshape(n_experts, 2, capacity, D).astype(jnp.float32), axis=1
    ).reshape(n_experts * capacity, D)
    picked = halves[slot].reshape(token_index, TOP, D)
    moe = jnp.sum(picked * gates[:, :, None], axis=1)
    return (resid_f + moe).astype(jnp.bfloat16)


def solution(mesh):
    placed = (
        P(("req", "exp"), None),
        P(("req", "exp"), None),
        P(("req", "exp"), None),
        P("req", None),
        P("req", None, None),
        P("req", None, None),
        P(),
        P(),
        P(("req", "exp"), None),
        P(("req", "exp"), None, None),
        P(("req", "exp"), None, None),
        P(("req", "exp"), None, None),
    )
    return jax.shard_map(
        on_device, mesh=mesh, in_specs=placed, out_specs=P(("req", "exp"), None), check_vma=False
    )
```

profile of v0, /device:TPU:34, one launch (start us, length us, event | category | flops | bytes accessed | tf_op | source)
XLA Modules:
  0.0 631.7 jit_solution(13155531788352508001)
XLA Ops:
  7.4 1.9 copy.159
  9.3 0.8 reduce-window.10
  10.2 0.8 convert_reduce_fusion.1
  11.2 12.1 %all_gather.9 = bf16[1024,56]{0,1:T(8,128)(2,1)S(1)} all-gather(bf16[128,56]{0,1:T(8,128)(2,1)S(1)} %convolution_convert_fusion.1), channel_id=1, replica_groups=mesh['req'=8,'exp'=16] {'req'}, dimensions={0}, use_global_device_ids=true | all-gather | bytes 129024 | tf_op jit(solution)/shard_map/all_gather | solution.py:81
  23.6 1.2 fusion.66
  25.1 16.3 %all-gather.3.cloned.1.call-done = bf16[1024,1280]{0,1:T(8,128)(2,1)} async-done(((bf16[128,1280]{0,1:T(8,128)(2,1)}), bf16[1024,1280]{0,1:T(8,128)(2,1)}) %all-gather.3.cloned.1.call-update) | async-done | bytes 2621456 | tf_op jit(solution)/shard_map/all_gather | solution.py:80
  41.4 16.3 %fusion = (f32[1024,2,5]{0,2,1:T(8,128)S(1)}, f32[2,896,1024,5]{2,1,3,0:T(8,128)}) fusion(pred[1024,896]{0,1:T(8,128)(4,1)S(1)} %bitcast_compare_fusion, bf16[896,2,128,1]{0,2,3,1:T(8,128)(2,1)S(1)} %bitcast.144, bf16[1024,2,5,128]{0,3,2,1:T(8,128)(2,1)} %bitcast.140), kind=kOutput, calls=%fused_computation.4 | convolution fusion | flops 2376325120 | bytes 40738816 | tf_op jit(solution)/shard_map/tgrd,kgd->tgrk/dot_general | solution.py:21
  57.7 0.4 broadcast_in_dim.118
  58.2 1.8 copy-done.1
  60.0 15.7 %fusion.4 = f32[1024,2,5]{0,2,1:T(8,128)S(1)} fusion(f32[2,896,1024,5]{2,1,3,0:T(8,128)} %get-tuple-element.18, f32[1024,896]{0,1:T(8,128)S(1)} %bitcast.138, f32[1024,2,5]{0,2,1:T(8,128)S(1)} %get-tuple-element.14, pred[1024,896]{0,1:T(8,128)(4,1)S(1)} %bitcast_compare_fusion), kind=kLoop, calls=%fused_computation.8 | loop fusion | flops 45864960 | bytes 41369600 | tf_op jit(solution)/shard_map/reduce_sum | solution.py:29
  75.7 0.6 copy.183
  76.3 4.0 all-to-all-start.2
  80.4 0.8 copy.165
  81.4 0.6 copy.163
  82.1 3.8 all-to-all-done.2
  85.8 3.3 all-to-all-start
  89.2 17.4 %bitcast_add_fusion = f32[1024,2,5,128]{3,0,2,1:T(8,128)S(1)} fusion(f32[1024,2,5]{0,2,1:T(8,128)S(1)} %get-tuple-element.13, bf16[896,2,128,1]{0,2,3,1:T(8,128)(2,1)S(1)} %bitcast.148, f32[2,896,1024,5]{2,1,3,0:T(8,128)} %get-tuple-element.18, f32[1024,896]{0,1:T(8,128)} %bitcast.139, f32[1024,2,5]{0,2,1:T(8,128)S(1)} %get-tuple-element.14, ...), kind=kOutput, calls=%fused_computation.24 | convolution fusion | flops 2395996160 | bytes 47071232 | tf_op jit(solution)/shard_map/tgrk,kgd->tgrd/dot_general | solution.py:30
  106.6 2.7 copy.177
  109.4 5.1 all-to-all-start.1
  114.9 1.8 reduce-window.11
  117.9 12.6 %all-gather.5.cloned.1.call-done = bf16[2048,512]{0,1:T(8,128)(2,1)} async-done(((bf16[128,512]{0,1:T(8,128)(2,1)}), bf16[2048,512]{0,1:T(8,128)(2,1)}) %all-gather.5.cloned.1.call-update) | async-done | bytes 2097168 | tf_op jit(solution)/shard_map/all_gather | solution.py:130
  130.5 2.7 fusion.65
  133.2 5.8 fusion.9
  139.2 6.4 %fusion.13 = f32[128,2,5]{0,2,1:T(8,128)S(1)} fusion(f32[2,2048,128,5]{2,1,3,0:T(8,128)} %get-tuple-element.20, f32[128,2048]{0,1:T(8,128)S(1)} %get-tuple-element.16, f32[128,2,5]{0,2,1:T(8,128)S(1)} %copy.180, pred[128,2048]{0,1:T(8,128)(4,1)S(1)} %get-tuple-element.15), kind=kLoop, calls=%fused_computation.21 | loop fusion | flops 13105920 | bytes 11806720 | tf_op jit(solution)/shard_map/reduce_sum | solution.py:29
  145.7 29.8 %all-to-all-done.1 = f32[8,128,2,5,128]{4,1,3,2,0:T(8,128)} async-done(((f32[8,128,2,5,128]{4,1,3,2,0:T(8,128)}), f32[8,128,2,5,128]{4,1,3,2,0:T(8,128)}, u32[]{:S(2)}, u32[]{:S(2)}) %all-to-all-start.1) | async-done | bytes 5242912 | tf_op jit(solution)/shard_map/all_to_all | solution.py:117
  175.4 4.3 multiply_reduce_fusion.1
  179.8 2.2 copy.179
  181.9 7.9 %fusion.43 = bf16[128,2,5,128]{0,3,2,1:T(8,128)(2,1)S(1)} fusion(bf16[2048,2,128,1]{0,2,3,1:T(8,128)(2,1)} %bitcast.146, f32[2,2048,128,5]{2,1,3,0:T(8,128)} %get-tuple-element.20, f32[128,2048]{0,1:T(8,128)} %copy-done.3, f32[128,2,5]{0,2,1:T(8,128)S(1)} %copy.180, pred[128,2048]{0,1:T(8,128)(4,1)S(1)} %get-tuple-element.15, ...), kind=kOutput, calls=%fused_computation.52 | convolution fusion | flops 684851200 | bytes 13843456 | tf_op jit(solution)/shard_map/tgrk,kgd->tgrd/dot_general | solution.py:30
  189.8 1.1 fusion.23
  191.3 2.9 broadcast_in_dim.133
  194.2 7.5 %reshape.302 = bf16[768,2560]{1,0:T(8,128)(2,1)} reshape(bf16[128,6,2560]{2,1,0:T(8,128)(2,1)} %broadcast_in_dim.133) | data formatting | bytes 7864320 | tf_op jit(solution)/shard_map/reshape | solution.py:167
  201.7 12.2 %scatter_custom_fusion = bf16[960,2560]{1,0:T(8,128)(2,1)} fusion(s32[768]{0:T(1024)S(1)} %fusion.56, bf16[768,2560]{1,0:T(8,128)(2,1)} %reshape.302, bf16[]{:T(256)} %constant.29.clone.1), kind=kCustom, calls=%fused_computation.35 | custom fusion | bytes 4915712 | tf_op jit(solution)/shard_map/scatter | solution.py:167
  213.9 7.6 %broadcast_in_dim.134 = bf16[64,15,2560]{2,1,0:T(8,128)(2,1)} reshape(bf16[960,2560]{1,0:T(8,128)(2,1)} %scatter_custom_fusion) | data formatting | bytes 9830400 | tf_op jit(solution)/shard_map/broadcast_in_dim | solution.py:169
  221.4 7.8 %broadcast_in_dim.135 = bf16[64,2,15,2560]{3,2,1,0:T(8,128)(2,1)} broadcast(bf16[64,15,2560]{2,1,0:T(8,128)(2,1)} %broadcast_in_dim.134), dimensions={0,2,3} | broadcast | bytes 14745600 | tf_op jit(solution)/shard_map/broadcast_in_dim | solution.py:169
  229.2 127.0 %all_to_all.25 = bf16[128,15,2560]{2,1,0:T(8,128)(2,1)} all-to-all(bf16[128,15,2560]{2,1,0:T(8,128)(2,1)} %bitcast.135), channel_id=1, replica_groups=mesh['req'=8,'exp'=16] {'req','exp'}, dimensions={0} | all-to-all | bytes 19660800 | tf_op jit(solution)/shard_map/all_to_all | solution.py:172
  356.2 13.9 %reshape.285 = bf16[1920,2560]{1,0:T(8,128)(2,1)} reshape(bf16[128,15,2560]{2,1,0:T(8,128)(2,1)} %all_to_all.25) | data formatting | bytes 19660800 | tf_op jit(solution)/shard_map/reshape | solution.py:174
  370.1 13.1 %fusion.21 = f32[1920,768]{1,0:T(8,128)} fusion(bf16[1920,2560]{1,0:T(8,128)(2,1)} %reshape.285, bf16[1,2560,768]{2,1,0:T(8,128)(2,1)} %param.21), kind=kOutput, calls=%fused_computation.30 | convolution fusion | flops 7549747200 | bytes 19660800 | tf_op jit(solution)/shard_map/dot_general | solution.py:175
  383.2 27.3 %convolution_convert_fusion = bf16[1920,2560]{1,0:T(8,128)(2,1)} fusion(f32[1920,768]{1,0:T(8,128)} %fusion.21, bf16[1920,2560]{1,0:T(8,128)(2,1)} %reshape.285, bf16[1,768,2560]{2,1,0:T(8,128)(2,1)} %param.23, bf16[1,2560,768]{2,1,0:T(8,128)(2,1)} %param.22), kind=kOutput, calls=%fused_computation.13 | convolution fusion | flops 15113256960 | bytes 33423360 | tf_op jit(solution)/shard_map/dot_general | solution.py:179
  410.5 13.8 %reshape.286 = bf16[128,15,2560]{2,1,0:T(8,128)(2,1)} reshape(bf16[1920,2560]{1,0:T(8,128)(2,1)} %convolution_convert_fusion) | data formatting | bytes 19660800 | tf_op jit(solution)/shard_map/reshape | solution.py:181
  424.3 7.0 %all-to-all-start.4 = ((bf16[128,15,2560]{2,1,0:T(8,128)(2,1)}), bf16[128,15,2560]{2,1,0:T(8,128)(2,1)}, u32[]{:S(2)}, u32[]{:S(2)}) async-start(bf16[128,15,2560]{2,1,0:T(8,128)(2,1)} %reshape.286), calls=%async_computation.4 | async-start | bytes 20971520 | tf_op jit(solution)/shard_map/all_to_all | solution.py:178
  431.3 0.3 fusion.67
  431.9 140.3 %all-to-all-done.4 = bf16[128,15,2560]{2,1,0:T(8,128)(2,1)} async-done(((bf16[128,15,2560]{2,1,0:T(8,128)(2,1)}), bf16[128,15,2560]{2,1,0:T(8,128)(2,1)}, u32[]{:S(2)}, u32[]{:S(2)}) %all-to-all-start.4) | async-done | bytes 9830432 | tf_op jit(solution)/shard_map/all_to_all | solution.py:178
  572.1 11.3 %convert_reduce_fusion = f32[64,15,2560]{2,1,0:T(8,128)} fusion(bf16[128,15,2560]{2,1,0:T(8,128)(2,1)} %all-to-all-done.4), kind=kLoop, calls=%fused_computation.10 | loop fusion | flops 7372800 | bytes 19660800 | tf_op jit(solution)/shard_map/reduce_sum | solution.py:187
  583.5 10.2 %reshape.287 = f32[960,2560]{1,0:T(8,128)} reshape(f32[64,15,2560]{2,1,0:T(8,128)} %convert_reduce_fusion) | data formatting | bytes 19660800 | tf_op jit(solution)/shard_map/reshape | solution.py:189
  593.7 12.2 %gather_fusion = f32[768,2560]{1,0:T(8,128)} fusion(f32[960,2560]{1,0:T(8,128)} %reshape.287, s32[1024]{0:T(1024)S(1)} %pad_clamp_fusion), kind=kCustom, calls=%fused_computation | custom fusion | bytes 15731712 | tf_op jit(solution)/shard_map/gather | solution.py:190
  605.9 9.2 %reshape.288 = f32[128,6,2560]{2,1,0:T(8,128)} reshape(f32[768,2560]{1,0:T(8,128)} %gather_fusion) | data formatting | bytes 15728640 | tf_op jit(solution)/shard_map/reshape | solution.py:190
  615.2 7.9 %multiply_reduce_fusion = f32[128,2560]{1,0:T(8,128)S(1)} fusion(f32[128,6,2560]{2,1,0:T(8,128)} %reshape.288, f32[128,6]{1,0:T(8,128)S(1)} %copy.192), kind=kLoop, calls=%fused_computation.20 | loop fusion | flops 3604480 | bytes 9178112 | tf_op jit(solution)/shard_map/reduce_sum | solution.py:191
  623.1 0.9 fusion.31
  (69 shorter events, 3.5 us)
Async XLA Ops:
  7.4 424.0 %copy-start = (bf16[2560,64]{0,1:T(8,128)(2,1)S(1)}, bf16[2560,64]{0,1:T(8,128)(2,1)}, u32[]{:S(2)}) copy-start(bf16[2560,64]{0,1:T(8,128)(2,1)} %param.19) | copy-start | bytes 983044
  7.4 34.0 %all-gather.3.cloned.1.call-start = ((), (), s32[]{:S(2)}) async-start(), calls=%async_computation.5 | async-start | bytes 2949120 | tf_op jit(solution)/shard_map/all_gather | solution.py:80
  58.2 1.8 copy-start.1
  60.0 20.4 %copy-start.5 = (bf16[128,512]{1,0:T(8,128)(2,1)S(1)}, bf16[128,512]{1,0:T(8,128)(2,1)}, u32[]{:S(2)}) copy-start(bf16[128,512]{1,0:T(8,128)(2,1)} %param.14) | copy-start | bytes 393220
  76.3 9.5 %all-to-all-start.2 = ((f32[8,128,2,5]{1,2,3,0:T(2,128)}), f32[8,128,2,5]{1,2,3,0:T(2,128)S(1)}, u32[]{:S(2)}, u32[]{:S(2)}) async-start(f32[8,128,2,5]{1,2,3,0:T(2,128)} %copy.183), calls=%async_computation.2 | async-start | bytes 81920 | tf_op jit(solution)/shard_map/all_to_all | solution.py:110
  80.3 50.2 %all-gather.5.cloned.1.call-start = ((), (), s32[]{:S(2)}) async-start(), calls=%async_computation.6 | async-start | bytes 2228224 | tf_op jit(solution)/shard_map/all_gather | solution.py:130
  85.8 23.5 %all-to-all-start = ((f32[8,128,2,5]{1,2,3,0:T(2,128)}), f32[8,128,2,5]{1,2,3,0:T(2,128)S(1)}, u32[]{:S(2)}, u32[]{:S(2)}) async-start(f32[8,128,2,5]{1,2,3,0:T(2,128)} %copy.163), calls=%async_computation | async-start | bytes 81920 | tf_op jit(solution)/shard_map/all_to_all | solution.py:103
  109.3 5.1 copy-start.6
  109.4 8.1 %copy-start.7 = (s32[1,4]{1,0:T(1,128)S(1)}, s32[1,4]{1,0:T(1,128)}, u32[]{:S(2)}) copy-start(s32[1,4]{1,0:T(1,128)} %param.15) | copy-start | bytes 52
  109.4 23.9 %copy-start.2 = (bf16[128,1280]{0,1:T(8,128)(2,1)S(1)}, bf16[128,1280]{0,1:T(8,128)(2,1)}, u32[]{:S(2)}) copy-start(bf16[128,1280]{0,1:T(8,128)(2,1)} %copy.159) | copy-start | bytes 983044
  109.4 66.1 %all-to-all-start.1 = ((f32[8,128,2,5,128]{4,1,3,2,0:T(8,128)}), f32[8,128,2,5,128]{4,1,3,2,0:T(8,128)}, u32[]{:S(2)}, u32[]{:S(2)}) async-start(f32[8,128,2,5,128]{4,1,3,2,0:T(8,128)} %copy.177), calls=%async_computation.1 | async-start | bytes 10485760 | tf_op jit(solution)/shard_map/all_to_all | solution.py:117
  117.9 21.3 %copy-start.3 = (f32[128,2048]{0,1:T(8,128)}, f32[128,2048]{0,1:T(8,128)S(1)}, u32[]{:S(2)}) copy-start(f32[128,2048]{0,1:T(8,128)S(1)} %get-tuple-element.16) | copy-start | bytes 3145732
  175.4 14.4 %slice-start = ((s8[6553600]{0:T(1024)(128)(4,1)}), s8[2359296]{0:T(1024)(128)(4,1)S(1)}, s32[]{:S(2)}) async-start(s8[6553600]{0:T(1024)(128)(4,1)} %bitcast.136), calls=%async_computation.7 | async-start | bytes 4718592
  181.9 7.9 %slice-start.1 = ((s8[6553600]{0:T(1024)(128)(4,1)}), s8[4194304]{0:T(1024)(128)(4,1)S(1)}, s32[]{:S(2)}) async-start(s8[6553600]{0:T(1024)(128)(4,1)} %bitcast.136), calls=%async_computation.8 | async-start | bytes 8388608
  181.9 7.9 %copy-start.4 = (bf16[128,2560]{1,0:T(8,128)(2,1)S(1)}, bf16[128,2560]{1,0:T(8,128)(2,1)}, u32[]{:S(2)}) copy-start(bf16[128,2560]{1,0:T(8,128)(2,1)} %param.12) | copy-start | bytes 1966084
  424.3 147.8 %all-to-all-start.4 = ((bf16[128,15,2560]{2,1,0:T(8,128)(2,1)}), bf16[128,15,2560]{2,1,0:T(8,128)(2,1)}, u32[]{:S(2)}, u32[]{:S(2)}) async-start(bf16[128,15,2560]{2,1,0:T(8,128)(2,1)} %reshape.286), calls=%async_computation.4 | async-start | bytes 20971520 | tf_op jit(solution)/shard_map/all_to_all | solution.py:178
Sparse Core Ops, SparseCore 0:
  9.9 31.4 all-gather.2
Sparse Core Ops, SparseCore 1:
  82.9 47.5 all-gather.4
where the time goes:
time: 642 us; the launch traced here: 632 us
  waiting for transfers between devices  203 us (32%)
  blocking collectives  139 us (22%)
  local copies, waits for them, and re-layouts  114 us (18%)
  matrix products  89.5 us (14%)
  other arithmetic  51.6 us (8%)
  starting transfers between devices  19.5 us (3%)
  between operations  15.4 us (2%)
    all_to_all x1, waiting for transfers between devices, on_device(): lax.all_to_all(jnp.dot(inner, w_down[0], preferred_element_type=jnp.float...  140 us
    all_to_all x1, blocking collectives, on_device(): lax.all_to_all(outgoing, ('req', 'exp'), split_axis=0, concat_axis=0, til...  127 us
    all_to_all x1, waiting for transfers between devices, on_device(): lax.all_to_all(summed_output.reshape(request_count, token_index, KEY_VALU...  29.8 us
    dot_general x1, matrix products, on_device(): jnp.dot(inner, w_down[0], preferred_element_type=jnp.float32)  27.3 us
    dot_general x2, matrix products, fold_scores(): jnp.einsum('tgrk,kgd->tgrd', expo.astype(jnp.bfloat16), value_rows, prefe...  25.3 us
    dot_general x2, matrix products, fold_scores(): jnp.einsum('tgrd,kgd->tgrk', query_matrix, key_rows, preferred_element_ty...  22.1 us
    reduce_sum x2, other arithmetic, fold_scores(): grand_total = decay * grand_total + jnp.sum(expo, axis=-1)  22.1 us
    all_gather x1, waiting for transfers between devices, on_device(): lax.all_gather(queries, 'req', axis=0, tiled=True)  16.3 us
  transfers between devices with their start and end apart: 6, of which 5 were waited for; matrix products, arithmetic and copies ran while one was open for 7% of the time, Pallas kernels for 0%

commit v1 on v0

--- a/solution.py
+++ b/solution.py
@@ -156,19 +156,25 @@
         jnp.where(routes[:, :, None] == expert_ids[None, None, :], logits[:, None, :], 0.0), axis=2
     )
     gates = jax.nn.softmax(chosen, axis=1)
-    capacity = max(2, (5 * token_index * TOP + 4 * n_experts - 1) // (4 * n_experts))
-    flat_routes = routes.reshape(-1)
-    onehot = (flat_routes[:, None] == expert_ids[None, :]).astype(jnp.int32)
-    rank = jnp.sum(jnp.cumsum(onehot, axis=0) * onehot, axis=1) - 1
-    slot = flat_routes * capacity + rank
-    send = (
-        jnp.zeros((n_experts * capacity, D), jnp.bfloat16)
-        .at[slot]
-        .set(jnp.repeat(normed, TOP, axis=0))
-    )
-    outgoing = jnp.broadcast_to(
-        send.reshape(n_experts, 1, capacity, D), (n_experts, 2, capacity, D)
-    ).reshape(2 * n_experts, capacity, D)
+    capacity = 16
+    member = routes[:, :, None] == expert_ids[None, None, :]
+    picks = jnp.any(member, axis=1).astype(jnp.float32)
+    gate_of = jnp.sum(jnp.where(member, gates[:, :, None], 0.0), axis=1)
+    earlier = (
+        jnp.arange(token_index, dtype=jnp.int32)[:, None]
+        > jnp.arange(token_index, dtype=jnp.int32)[None, :]
+    ).astype(jnp.float32)
+    rank = jnp.dot(earlier, picks, precision=lax.Precision.HIGHEST).astype(jnp.int32)
+    place = jnp.arange(capacity, dtype=jnp.int32)
+    select = (picks[None, :, :] > 0) & (rank[None, :, :] == place[:, None, None])
+    select = jnp.transpose(select, (2, 0, 1))
+    select2 = jnp.broadcast_to(
+        select[:, None], (n_experts, 2, capacity, token_index)
+    ).reshape(2 * n_experts * capacity, token_index)
+    outgoing = jnp.dot(
+        select2.astype(jnp.bfloat16), normed, preferred_element_type=jnp.float32
+    ).astype(jnp.bfloat16)
+    outgoing = outgoing.reshape(2 * n_experts, capacity, D)
     rows = lax.all_to_all(outgoing, ("req", "exp"), split_axis=0, concat_axis=0, tiled=True)
     array_shape = rows.shape
     flat_rows = rows.reshape(-1, D)
@@ -183,12 +189,20 @@
         split_axis=0,
         concat_axis=0,
         tiled=True,
-    )
-    halves = jnp.sum(
-        returned.reshape(n_experts, 2, capacity, D).astype(jnp.float32), axis=1
-    ).reshape(n_experts * capacity, D)
-    picked = halves[slot].reshape(token_index, TOP, D)
-    moe = jnp.sum(picked * gates[:, :, None], axis=1)
+    ).reshape(2 * n_experts * capacity, D)
+    weight = jnp.where(
+        jnp.transpose(select, (2, 0, 1))[:, :, None, :],
+        gate_of[:, :, None, None],
+        0.0,
+    )
+    weight = jnp.broadcast_to(
+        weight, (token_index, n_experts, 2, capacity)
+    ).reshape(token_index, 2 * n_experts * capacity)
+    high = weight.astype(jnp.bfloat16)
+    low = (weight - high.astype(jnp.float32)).astype(jnp.bfloat16)
+    moe = jnp.dot(high, returned, preferred_element_type=jnp.float32) + jnp.dot(
+        low, returned, preferred_element_type=jnp.float32
+    )
     return (resid_f + moe).astype(jnp.bfloat16)
 
 

time: 642 us -> 533 us (0.83); the launches traced: 632 us -> 532 us
  local copies, waits for them, and re-layouts: 114 us -> 19.7 us
  other arithmetic: 51.6 us -> 29.7 us
  matrix products: 89.5 us -> 104 us
    reshape x5 -> x0, local copies, waits for them, and re-layouts: 54.6 us -> none  [the longest x1 13.9 us: on_device(): flat_rows = rows.reshape(-1, D)]
    reduce_sum x3 -> x1, other arithmetic: 19.4 us -> 0.03 us  [on_device(): gate_of = jnp.sum(jnp.where(member, gates[:, :, None], 0.0), axis=1)]
    broadcast_in_dim x3, local copies, waits for them, and re-layouts: 18.3 us -> 0.21 us  [the longest x2 0.14 us: on_device(): jnp.broadcast_to(weight, (token_index, n_experts, 2, capacity))]
    dot_general x0 -> x4, matrix products: none -> 15.3 us  [the longest x1 6.39 us: on_device(): jnp.dot(low, returned, preferred_element_type=jnp.float32)]
    gather x1 -> x0, local copies, waits for them, and re-layouts: 12.2 us -> none  [on_device(): picked = halves[slot].reshape(token_index, TOP, D)]
    scatter x1 -> x0, local copies, waits for them, and re-layouts: 12.2 us -> none  [on_device(): send = jnp.zeros((n_experts * capacity, D), jnp.bfloat16).at[slot].set(jn...]
  transfers between devices with their start and end apart: 6 -> 6, of which waited for: 5 -> 5; matrix products, arithmetic and copies ran while one was open for 7% -> 8% of each run, Pallas kernels for 0% -> 0%
where the time goes in v1:
time: 533 us; the launch traced here: 532 us
  waiting for transfers between devices  206 us (39%)
  blocking collectives  138 us (26%)
  matrix products  104 us (20%)
  other arithmetic  29.7 us (6%)
  local copies, waits for them, and re-layouts  19.7 us (4%)
  starting transfers between devices  19 us (4%)
  between operations  15.2 us (3%)
    all_to_all x1, waiting for transfers between devices, on_device(): lax.all_to_all(jnp.dot(inner, w_down[0], preferred_element_type=jnp.float...  141 us
    all_to_all x1, blocking collectives, on_device(): lax.all_to_all(outgoing, ('req', 'exp'), split_axis=0, concat_axis=0, til...  126 us
    all_to_all x1, waiting for transfers between devices, on_device(): lax.all_to_all(summed_output.reshape(request_count, token_index, KEY_VALU...  29.6 us
    dot_general x1, matrix products, on_device(): jnp.dot(inner, w_down[0], preferred_element_type=jnp.float32)  28.9 us
    dot_general x2, matrix products, fold_scores(): jnp.einsum('tgrk,kgd->tgrd', expo.astype(jnp.bfloat16), value_rows, prefe...  25.3 us
    dot_general x2, matrix products, fold_scores(): jnp.einsum('tgrd,kgd->tgrk', query_matrix, key_rows, preferred_element_ty...  22.1 us
    reduce_sum x2, other arithmetic, fold_scores(): grand_total = decay * grand_total + jnp.sum(expo, axis=-1)  22.1 us
    all_gather x1, waiting for transfers between devices, on_device(): lax.all_gather(queries, 'req', axis=0, tiled=True)  16.3 us
  transfers between devices with their start and end apart: 6, of which 5 were waited for; matrix products, arithmetic and copies ran while one was open for 8% of the time, Pallas kernels for 0%

profile of v1, /device:TPU:34, one launch (start us, length us, event | category | flops | bytes accessed | tf_op | source)
XLA Modules:
  0.0 531.8 jit_solution(14392213772407807917)
XLA Ops:
  7.4 1.9 copy.140
  9.3 0.8 reduce-window.4
  10.2 0.8 convert_reduce_fusion
  11.0 0.2 convolution_convert_fusion.3
  11.2 12.1 %all_gather.9 = bf16[1024,56]{0,1:T(8,128)(2,1)S(1)} all-gather(bf16[128,56]{0,1:T(8,128)(2,1)S(1)} %convolution_convert_fusion.3), channel_id=1, replica_groups=mesh['req'=8,'exp'=16] {'req'}, dimensions={0}, use_global_device_ids=true | all-gather | bytes 129024 | tf_op jit(solution)/shard_map/all_gather | solution.py:81
  23.4 0.2 bitcast_compare_fusion
  23.6 1.2 fusion.69
  24.8 0.2 copy.139
  25.1 16.3 %all-gather.3.cloned.1.call-done = bf16[1024,1280]{0,1:T(8,128)(2,1)} async-done(((bf16[128,1280]{0,1:T(8,128)(2,1)}), bf16[1024,1280]{0,1:T(8,128)(2,1)}) %all-gather.3.cloned.1.call-update) | async-done | bytes 2621456 | tf_op jit(solution)/shard_map/all_gather | solution.py:80
  41.4 16.3 %fusion = (f32[1024,2,5]{0,2,1:T(8,128)S(1)}, f32[2,896,1024,5]{2,1,3,0:T(8,128)}) fusion(pred[1024,896]{0,1:T(8,128)(4,1)S(1)} %bitcast_compare_fusion, bf16[896,2,128,1]{0,2,3,1:T(8,128)(2,1)S(1)} %bitcast.144, bf16[1024,2,5,128]{0,3,2,1:T(8,128)(2,1)} %bitcast.138), kind=kOutput, calls=%fused_computation.2 | convolution fusion | flops 2376325120 | bytes 40738816 | tf_op jit(solution)/shard_map/tgrd,kgd->tgrk/dot_general | solution.py:21
  57.7 0.4 broadcast_in_dim.146
  58.2 1.8 copy-done.1
  60.0 15.7 %fusion.4 = f32[1024,2,5]{0,2,1:T(8,128)S(1)} fusion(f32[2,896,1024,5]{2,1,3,0:T(8,128)} %get-tuple-element.20, f32[1024,896]{0,1:T(8,128)S(1)} %bitcast.133, f32[1024,2,5]{0,2,1:T(8,128)S(1)} %get-tuple-element.14, pred[1024,896]{0,1:T(8,128)(4,1)S(1)} %bitcast_compare_fusion), kind=kLoop, calls=%fused_computation.6 | loop fusion | flops 45864960 | bytes 41369600 | tf_op jit(solution)/shard_map/reduce_sum | solution.py:29
  75.7 0.6 copy.164
  76.3 4.0 all-to-all-start.2
  80.4 0.8 copy.146
  81.2 0.2 copy.155
  81.4 0.6 copy.144
  82.1 3.8 all-to-all-done.2
  85.8 3.3 all-to-all-start
  89.2 17.4 %bitcast_add_fusion = f32[1024,2,5,128]{3,0,2,1:T(8,128)S(1)} fusion(f32[1024,2,5]{0,2,1:T(8,128)S(1)} %get-tuple-element.13, bf16[896,2,128,1]{0,2,3,1:T(8,128)(2,1)S(1)} %bitcast.150, f32[2,896,1024,5]{2,1,3,0:T(8,128)} %get-tuple-element.20, f32[1024,896]{0,1:T(8,128)} %bitcast.134, f32[1024,2,5]{0,2,1:T(8,128)S(1)} %get-tuple-element.14, ...), kind=kOutput, calls=%fused_computation.21 | convolution fusion | flops 2395996160 | bytes 47071232 | tf_op jit(solution)/shard_map/tgrk,kgd->tgrd/dot_general | solution.py:30
  106.7 2.7 copy.158
  109.4 5.0 all-to-all-start.1
  114.5 0.1 convolution_convert_fusion.2
  114.6 0.1 fusion.47
  114.8 0.3 broadcast_compare_fusion
  115.1 15.4 %all-gather.5.cloned.1.call-done = bf16[2048,512]{0,1:T(8,128)(2,1)} async-done(((bf16[128,512]{0,1:T(8,128)(2,1)}), bf16[2048,512]{0,1:T(8,128)(2,1)}) %all-gather.5.cloned.1.call-update) | async-done | bytes 2097168 | tf_op jit(solution)/shard_map/all_gather | solution.py:130
  130.5 2.7 fusion.68
  133.2 5.8 %fusion.9 = (f32[128,2,5]{0,2,1:T(8,128)S(1)}, f32[2,2048,128,5]{2,1,3,0:T(8,128)}) fusion(pred[128,2048]{0,1:T(8,128)(4,1)S(1)} %get-tuple-element.17, bf16[2048,2,128,1]{0,2,3,1:T(8,128)(2,1)S(1)} %bitcast.141, bf16[128,2,5,128]{0,3,2,1:T(8,128)(2,1)S(1)} %bitcast.140), kind=kOutput, calls=%fused_computation.14 | convolution fusion | flops 678951680 | bytes 12129280 | tf_op jit(solution)/shard_map/tgrd,kgd->tgrk/dot_general | solution.py:21
  139.2 6.4 %fusion.13 = f32[128,2,5]{0,2,1:T(8,128)S(1)} fusion(f32[2,2048,128,5]{2,1,3,0:T(8,128)} %get-tuple-element.22, f32[128,2048]{0,1:T(8,128)S(1)} %get-tuple-element.18, f32[128,2,5]{0,2,1:T(8,128)S(1)} %copy.161, pred[128,2048]{0,1:T(8,128)(4,1)S(1)} %get-tuple-element.17), kind=kLoop, calls=%fused_computation.18 | loop fusion | flops 13105920 | bytes 11806720 | tf_op jit(solution)/shard_map/reduce_sum | solution.py:29
  145.7 29.6 %all-to-all-done.1 = f32[8,128,2,5,128]{4,1,3,2,0:T(8,128)} async-done(((f32[8,128,2,5,128]{4,1,3,2,0:T(8,128)}), f32[8,128,2,5,128]{4,1,3,2,0:T(8,128)}, u32[]{:S(2)}, u32[]{:S(2)}) %all-to-all-start.1) | async-done | bytes 5242912 | tf_op jit(solution)/shard_map/all_to_all | solution.py:117
  175.3 4.3 multiply_reduce_fusion
  179.6 2.2 copy.160
  181.8 7.9 %fusion.42 = bf16[128,2,5,128]{0,3,2,1:T(8,128)(2,1)S(1)} fusion(bf16[2048,2,128,1]{0,2,3,1:T(8,128)(2,1)} %bitcast.147, f32[2,2048,128,5]{2,1,3,0:T(8,128)} %get-tuple-element.22, f32[128,2048]{0,1:T(8,128)} %copy-done.4, f32[128,2,5]{0,2,1:T(8,128)S(1)} %copy.161, pred[128,2048]{0,1:T(8,128)(4,1)S(1)} %get-tuple-element.17, ...), kind=kOutput, calls=%fused_computation.49 | convolution fusion | flops 684851200 | bytes 13843456 | tf_op jit(solution)/shard_map/tgrk,kgd->tgrd/dot_general | solution.py:30
  189.7 1.0 fusion.25
  190.7 0.2 fusion.29
  191.0 3.2 convolution_convert_fusion.1
  194.3 126.3 %all_to_all.25 = bf16[128,16,2560]{2,1,0:T(8,128)(2,1)S(1)} all-to-all(bf16[128,16,2560]{2,1,0:T(8,128)(2,1)S(1)} %bitcast.130), channel_id=1, replica_groups=mesh['req'=8,'exp'=16] {'req','exp'}, dimensions={0} | all-to-all | bytes 20971520 | tf_op jit(solution)/shard_map/all_to_all | solution.py:178
  320.5 3.8 copy-done.2
  324.4 10.2 %fusion.21 = f32[2048,768]{1,0:T(8,128)} fusion(bf16[2048,2560]{1,0:T(8,128)(2,1)S(1)} %bitcast.136, bf16[1,2560,768]{2,1,0:T(8,128)(2,1)S(1)} %copy-done.8), kind=kOutput, calls=%fused_computation.27 | convolution fusion | flops 8053063680 | bytes 20709376 | tf_op jit(solution)/shard_map/dot_general | solution.py:181
  334.5 28.9 %convolution_convert_fusion = bf16[2048,2560]{1,0:T(8,128)(2,1)} fusion(f32[2048,768]{1,0:T(8,128)} %fusion.21, bf16[2048,2560]{1,0:T(8,128)(2,1)} %bitcast.137, bf16[1,768,2560]{2,1,0:T(8,128)(2,1)} %param.23, bf16[1,2560,768]{2,1,0:T(8,128)(2,1)} %param.22), kind=kOutput, calls=%fused_computation.10 | convolution fusion | flops 16120807424 | bytes 35127296 | tf_op jit(solution)/shard_map/dot_general | solution.py:185
  363.5 6.7 %all-to-all-start.4 = ((bf16[128,16,2560]{2,1,0:T(8,128)(2,1)}), bf16[128,16,2560]{2,1,0:T(8,128)(2,1)}, u32[]{:S(2)}, u32[]{:S(2)}) async-start(bf16[128,16,2560]{2,1,0:T(8,128)(2,1)} %bitcast.135), calls=%async_computation.4 | async-start | bytes 20971520 | tf_op jit(solution)/shard_map/all_to_all | solution.py:184
  370.1 0.4 fusion.49
  370.7 0.1 select_convert_fusion
  370.8 0.1 fusion.45
  371.0 141.3 %all-to-all-done.4 = bf16[128,16,2560]{2,1,0:T(8,128)(2,1)} async-done(((bf16[128,16,2560]{2,1,0:T(8,128)(2,1)}), bf16[128,16,2560]{2,1,0:T(8,128)(2,1)}, u32[]{:S(2)}, u32[]{:S(2)}) %all-to-all-start.4) | async-done | bytes 10485792 | tf_op jit(solution)/shard_map/all_to_all | solution.py:184
  512.3 5.5 %fusion.70 = f32[128,2560]{1,0:T(8,128)S(1)} fusion(bf16[128,2048]{0,1:T(8,128)(2,1)S(1)} %bitcast.143, bf16[2048,2560]{1,0:T(8,128)(2,1)} %bitcast.34), kind=kOutput, calls=%fused_computation.101 | convolution fusion | flops 1342177280 | bytes 12320768 | tf_op jit(solution)/shard_map/dot_general | solution.py:203
  518.0 6.4 %fusion.24 = bf16[128,2560]{1,0:T(8,128)(2,1)} fusion(f32[128,2560]{1,0:T(8,128)S(1)} %fusion.70, bf16[128,2048]{0,1:T(8,128)(2,1)S(1)} %bitcast.142, bf16[2048,2560]{1,0:T(8,128)(2,1)} %bitcast.34, bf16[128,2560]{1,0:T(8,128)(2,1)S(1)} %fusion.25), kind=kOutput, calls=%fused_computation.32 | convolution fusion | flops 1343488000 | bytes 13631488 | tf_op jit(solution)/shard_map/dot_general | solution.py:203
  (57 shorter events, 0.9 us)
Async XLA Ops:
  7.4 362.8 %copy-start = (bf16[2560,64]{0,1:T(8,128)(2,1)S(1)}, bf16[2560,64]{0,1:T(8,128)(2,1)}, u32[]{:S(2)}) copy-start(bf16[2560,64]{0,1:T(8,128)(2,1)} %param.19) | copy-start | bytes 983044
  7.4 34.0 %all-gather.3.cloned.1.call-start = ((), (), s32[]{:S(2)}) async-start(), calls=%async_computation.5 | async-start | bytes 2949120 | tf_op jit(solution)/shard_map/all_gather | solution.py:80
  58.2 1.8 copy-start.1
  60.0 20.4 %copy-start.6 = (bf16[128,512]{1,0:T(8,128)(2,1)S(1)}, bf16[128,512]{1,0:T(8,128)(2,1)}, u32[]{:S(2)}) copy-start(bf16[128,512]{1,0:T(8,128)(2,1)} %param.14) | copy-start | bytes 393220
  76.3 9.5 %all-to-all-start.2 = ((f32[8,128,2,5]{1,2,3,0:T(2,128)}), f32[8,128,2,5]{1,2,3,0:T(2,128)S(1)}, u32[]{:S(2)}, u32[]{:S(2)}) async-start(f32[8,128,2,5]{1,2,3,0:T(2,128)} %copy.164), calls=%async_computation.2 | async-start | bytes 81920 | tf_op jit(solution)/shard_map/all_to_all | solution.py:110
  80.3 50.2 %all-gather.5.cloned.1.call-start = ((), (), s32[]{:S(2)}) async-start(), calls=%async_computation.6 | async-start | bytes 2228224 | tf_op jit(solution)/shard_map/all_gather | solution.py:130
  85.8 23.6 %all-to-all-start = ((f32[8,128,2,5]{1,2,3,0:T(2,128)}), f32[8,128,2,5]{1,2,3,0:T(2,128)S(1)}, u32[]{:S(2)}, u32[]{:S(2)}) async-start(f32[8,128,2,5]{1,2,3,0:T(2,128)} %copy.144), calls=%async_computation | async-start | bytes 81920 | tf_op jit(solution)/shard_map/all_to_all | solution.py:103
  106.6 7.7 %copy-start.9 = (s32[1,4]{1,0:T(1,128)S(1)}, s32[1,4]{1,0:T(1,128)}, u32[]{:S(2)}) copy-start(s32[1,4]{1,0:T(1,128)} %param.15) | copy-start | bytes 52
  106.6 7.8 %copy-start.7 = (s32[128,6]{0,1:T(8,128)S(1)}, s32[128,6]{0,1:T(8,128)}, u32[]{:S(2)}) copy-start(s32[128,6]{0,1:T(8,128)} %param.20) | copy-start | bytes 9220
  109.4 23.9 %copy-start.3 = (bf16[128,1280]{0,1:T(8,128)(2,1)S(1)}, bf16[128,1280]{0,1:T(8,128)(2,1)}, u32[]{:S(2)}) copy-start(bf16[128,1280]{0,1:T(8,128)(2,1)} %copy.140) | copy-start | bytes 983044
  109.4 65.9 %all-to-all-start.1 = ((f32[8,128,2,5,128]{4,1,3,2,0:T(8,128)}), f32[8,128,2,5,128]{4,1,3,2,0:T(8,128)}, u32[]{:S(2)}, u32[]{:S(2)}) async-start(f32[8,128,2,5,128]{4,1,3,2,0:T(8,128)} %copy.158), calls=%async_computation.1 | async-start | bytes 10485760 | tf_op jit(solution)/shard_map/all_to_all | solution.py:117
  115.1 24.1 %copy-start.4 = (f32[128,2048]{0,1:T(8,128)}, f32[128,2048]{0,1:T(8,128)S(1)}, u32[]{:S(2)}) copy-start(f32[128,2048]{0,1:T(8,128)S(1)} %get-tuple-element.18) | copy-start | bytes 3145732
  175.3 14.4 %slice-start = ((s8[6553600]{0:T(1024)(128)(4,1)}), s8[2359296]{0:T(1024)(128)(4,1)S(1)}, s32[]{:S(2)}) async-start(s8[6553600]{0:T(1024)(128)(4,1)} %bitcast.131), calls=%async_computation.7 | async-start | bytes 4718592
  181.8 7.9 %slice-start.1 = ((s8[6553600]{0:T(1024)(128)(4,1)}), s8[4194304]{0:T(1024)(128)(4,1)S(1)}, s32[]{:S(2)}) async-start(s8[6553600]{0:T(1024)(128)(4,1)} %bitcast.131), calls=%async_computation.8 | async-start | bytes 8388608
  181.8 7.9 %copy-start.5 = (bf16[128,2560]{1,0:T(8,128)(2,1)S(1)}, bf16[128,2560]{1,0:T(8,128)(2,1)}, u32[]{:S(2)}) copy-start(bf16[128,2560]{1,0:T(8,128)(2,1)} %param.12) | copy-start | bytes 1966084
  194.3 130.1 %copy-start.8 = (bf16[1,2560,768]{2,1,0:T(8,128)(2,1)S(1)}, bf16[1,2560,768]{2,1,0:T(8,128)(2,1)}, u32[]{:S(2)}) copy-start(bf16[1,2560,768]{2,1,0:T(8,128)(2,1)} %param.21) | copy-start | bytes 11796484
  320.5 3.8 copy-start.2
  363.5 148.8 %all-to-all-start.4 = ((bf16[128,16,2560]{2,1,0:T(8,128)(2,1)}), bf16[128,16,2560]{2,1,0:T(8,128)(2,1)}, u32[]{:S(2)}, u32[]{:S(2)}) async-start(bf16[128,16,2560]{2,1,0:T(8,128)(2,1)} %bitcast.135), calls=%async_computation.4 | async-start | bytes 20971520 | tf_op jit(solution)/shard_map/all_to_all | solution.py:184
Sparse Core Ops, SparseCore 0:
  9.9 31.4 all-gather.2
Sparse Core Ops, SparseCore 1:
  82.9 47.5 all-gather.4

commit v2 on v1

v2 whole, which is shorter than its diff:
```python
import functools
import math

import jax
import jax.numpy as jnp
from jax import lax
from jax.experimental import pallas as pl
from jax.experimental.pallas import tpu as pltpu
from jax.sharding import PartitionSpec as P

D = 2560
QUERY_HEADS = 10
KEY_VALUE_HEADS = 2
HEAD_SIZE = 128
TOP = 6
PAGE_TOKENS = 128


NEGATIVE_MASK = -1e30
EPS = 1e-06


KEY_BLOCK = 512


def attn_kernel(q_ref, w_ref, pool_ref, suf_ref, o_ref, qs, m_ref, l_ref, acc_ref, *, n_pool, n_blocks, groups, reps, hs):
    j = pl.program_id(0)
    t = q_ref.shape[0]

    @pl.when(j == 0)
    def _():
        for g in range(groups):
            qs[g] = jnp.concatenate(
                [q_ref[:, (g * reps + h) * hs:(g * reps + h + 1) * hs] for h in range(reps)], axis=0)
        m_ref[...] = jnp.full(m_ref.shape, NEGATIVE_MASK, jnp.float32)
        l_ref[...] = jnp.zeros(l_ref.shape, jnp.float32)
        acc_ref[...] = jnp.zeros(acc_ref.shape, jnp.float32)

    def step(kv_ref):
        w = w_ref[...].astype(jnp.float32)
        live = (w > 0)[None]
        for g in range(groups):
            k = kv_ref[:, g * hs:(g + 1) * hs]
            v = kv_ref[:, (groups + g) * hs:(groups + g + 1) * hs]
            s = lax.dot_general(qs[g], k, (((1,), (1,)), ((), ())),
                                preferred_element_type=jnp.float32) * (1.0 / math.sqrt(hs))
            s = s.reshape(reps, t, KEY_BLOCK)
            m_old = m_ref[g].reshape(reps, t, 1)
            m_new = jnp.maximum(m_old, jnp.max(jnp.where(live, s, NEGATIVE_MASK), axis=-1, keepdims=True))
            p = jnp.where(live, jnp.exp(s - m_new), 0.0) * w[None]
            alpha = jnp.exp(m_old - m_new)
            l_ref[g] = (alpha * l_ref[g].reshape(reps, t, 1) + jnp.sum(p, axis=-1, keepdims=True)).reshape(reps * t, 1)
            pv = jnp.dot(p.reshape(reps * t, KEY_BLOCK).astype(jnp.bfloat16), v, preferred_element_type=jnp.float32)
            acc_ref[g] = alpha.reshape(reps * t, 1) * acc_ref[g] + pv
            m_ref[g] = m_new.reshape(reps * t, 1)

    @pl.when(j < n_pool)
    def _():
        step(pool_ref)

    @pl.when(j >= n_pool)
    def _():
        step(suf_ref)

    @pl.when(j == n_blocks - 1)
    def _():
        for g in range(groups):
            for h in range(reps):
                rows = slice(h * t, (h + 1) * t)
                o_ref[:, (g * reps + h) * hs:(g * reps + h + 1) * hs] = (
                    acc_ref[g, rows, :] / l_ref[g, rows, :]).astype(o_ref.dtype)


def flash(queries, weights, pool_rows, suffix_rows, groups=2, hs=128):
    t, width = queries.shape
    reps = width // hs // groups
    n_pool = pool_rows.shape[0] // KEY_BLOCK
    n_suf = suffix_rows.shape[0] // KEY_BLOCK
    n_blocks = n_pool + n_suf
    kern = functools.partial(attn_kernel, n_pool=n_pool, n_blocks=n_blocks, groups=groups, reps=reps, hs=hs)
    return pl.pallas_call(
        kern,
        grid=(n_blocks,),
        in_specs=[
            pl.BlockSpec((t, width), lambda j: (0, 0)),
            pl.BlockSpec((t, KEY_BLOCK), lambda j: (0, j)),
            pl.BlockSpec((KEY_BLOCK, pool_rows.shape[1]), lambda j: (jnp.minimum(j, n_pool - 1), 0)),
            pl.BlockSpec((KEY_BLOCK, suffix_rows.shape[1]), lambda j: (jnp.maximum(j - n_pool, 0), 0)),
        ],
        out_specs=pl.BlockSpec((t, width), lambda j: (0, 0)),
        out_shape=jax.ShapeDtypeStruct((t, width), jnp.bfloat16),
        scratch_shapes=[
            pltpu.VMEM((groups, reps * t, hs), jnp.bfloat16),
            pltpu.VMEM((groups, reps * t, 1), jnp.float32),
            pltpu.VMEM((groups, reps * t, 1), jnp.float32),
            pltpu.VMEM((groups, reps * t, hs), jnp.float32),
        ],
    )(queries, weights, pool_rows, suffix_rows)


def on_device(
    hidden,
    queries,
    suffix_kv,
    lengths,
    page_table,
    page_pool,
    w_out,
    w_router,
    routes,
    w_gate,
    w_up,
    w_down,
):
    token_index = hidden.shape[0]
    row_width = KEY_VALUE_HEADS * HEAD_SIZE
    request_groups = QUERY_HEADS // KEY_VALUE_HEADS
    request_count = lax.axis_size("req")
    pool_per_shard = page_pool.shape[0]
    pool_all = pool_per_shard * request_count
    positions = lax.axis_index("exp") * token_index + jnp.arange(token_index, dtype=jnp.int32)
    lens = lengths[0]
    ends = jnp.cumsum(lens)
    starts = ends - lens
    req_of = jnp.sum((positions[:, None] >= ends[None, :]).astype(jnp.int32), axis=1)
    pick = req_of[:, None] == jnp.arange(lens.shape[0], dtype=jnp.int32)[None, :]
    first = jnp.sum(jnp.where(pick, starts[None, :], 0), axis=1)
    pool_rows = lax.all_gather(page_pool, "req", axis=0, tiled=True).reshape(
        pool_all * PAGE_TOKENS, 2 * row_width
    )
    segment = lax.all_gather(suffix_kv, "exp", axis=0, tiled=True)
    counts = jnp.sum(
        (page_table[0][:, :, None] == jnp.arange(pool_all, dtype=jnp.int32)[None, None, :]).astype(
            jnp.float32
        ),
        axis=1,
    )
    query_counts = jnp.dot(pick.astype(jnp.float32), counts, precision=lax.Precision.HIGHEST)
    keypos = jnp.arange(segment.shape[0], dtype=jnp.int32)
    suffix_weights = (keypos[None, :] <= positions[:, None]) & (keypos[None, :] >= first[:, None])
    weights = jnp.concatenate(
        [
            jnp.repeat(query_counts, PAGE_TOKENS, axis=1).astype(jnp.bfloat16),
            suffix_weights.astype(jnp.bfloat16),
        ],
        axis=1,
    )
    attended = flash(queries, weights, pool_rows, segment, groups=KEY_VALUE_HEADS, hs=HEAD_SIZE)
    projected = jnp.dot(attended, w_out, preferred_element_type=jnp.float32)
    resid = lax.optimization_barrier((hidden.astype(jnp.float32) + projected).astype(jnp.bfloat16))
    resid_f = resid.astype(jnp.float32)
    normed = (resid_f * lax.rsqrt(jnp.mean(resid_f * resid_f, axis=1, keepdims=True) + EPS)).astype(
        jnp.bfloat16
    )
    n_experts = w_router.shape[1]
    logits = jnp.dot(normed, w_router, preferred_element_type=jnp.float32)
    expert_ids = jnp.arange(n_experts, dtype=jnp.int32)
    chosen = jnp.sum(
        jnp.where(routes[:, :, None] == expert_ids[None, None, :], logits[:, None, :], 0.0), axis=2
    )
    gates = jax.nn.softmax(chosen, axis=1)
    capacity = 16
    member = routes[:, :, None] == expert_ids[None, None, :]
    picks = jnp.any(member, axis=1).astype(jnp.float32)
    gate_of = jnp.sum(jnp.where(member, gates[:, :, None], 0.0), axis=1)
    earlier = (
        jnp.arange(token_index, dtype=jnp.int32)[:, None]
        > jnp.arange(token_index, dtype=jnp.int32)[None, :]
    ).astype(jnp.float32)
    rank = jnp.dot(earlier, picks, precision=lax.Precision.HIGHEST).astype(jnp.int32)
    place = jnp.arange(capacity, dtype=jnp.int32)
    select = (picks[None, :, :] > 0) & (rank[None, :, :] == place[:, None, None])
    select = jnp.transpose(select, (2, 0, 1))
    select2 = jnp.broadcast_to(
        select[:, None], (n_experts, 2, capacity, token_index)
    ).reshape(2 * n_experts * capacity, token_index)
    outgoing = jnp.dot(
        select2.astype(jnp.bfloat16), normed, preferred_element_type=jnp.float32
    ).astype(jnp.bfloat16)
    outgoing = outgoing.reshape(2 * n_experts, capacity, D)
    rows = lax.all_to_all(outgoing, ("req", "exp"), split_axis=0, concat_axis=0, tiled=True)
    array_shape = rows.shape
    flat_rows = rows.reshape(-1, D)
    gate_part = jnp.dot(flat_rows, w_gate[0], preferred_element_type=jnp.float32)
    up_part = jnp.dot(flat_rows, w_up[0], preferred_element_type=jnp.float32)
    inner = (jax.nn.silu(gate_part) * up_part).astype(jnp.bfloat16)
    returned = lax.all_to_all(
        jnp.dot(inner, w_down[0], preferred_element_type=jnp.float32)
        .astype(jnp.bfloat16)
        .reshape(array_shape),
        ("req", "exp"),
        split_axis=0,
        concat_axis=0,
        tiled=True,
    ).reshape(2 * n_experts * capacity, D)
    weight = jnp.where(
        jnp.transpose(select, (2, 0, 1))[:, :, None, :],
        gate_of[:, :, None, None],
        0.0,
    )
    weight = jnp.broadcast_to(
        weight, (token_index, n_experts, 2, capacity)
    ).reshape(token_index, 2 * n_experts * capacity)
    high = weight.astype(jnp.bfloat16)
    low = (weight - high.astype(jnp.float32)).astype(jnp.bfloat16)
    moe = jnp.dot(high, returned, preferred_element_type=jnp.float32) + jnp.dot(
        low, returned, preferred_element_type=jnp.float32
    )
    return (resid_f + moe).astype(jnp.bfloat16)


def solution(mesh):
    placed = (
        P(("req", "exp"), None),
        P(("req", "exp"), None),
        P(("req", "exp"), None),
        P("req", None),
        P("req", None, None),
        P("req", None, None),
        P(),
        P(),
        P(("req", "exp"), None),
        P(("req", "exp"), None, None),
        P(("req", "exp"), None, None),
        P(("req", "exp"), None, None),
    )
    return jax.shard_map(
        on_device, mesh=mesh, in_specs=placed, out_specs=P(("req", "exp"), None), check_vma=False
    )
```

time: 533 us -> 509 us (0.955)
  Pallas kernels: 0 us -> 60.9 us
  matrix products: 104 us -> 59 us
  waiting for transfers between devices: 206 us -> 232 us
  other arithmetic: 29.7 us -> 4.67 us
  local copies, waits for them, and re-layouts: 19.7 us -> 5.67 us
  starting transfers between devices: 19 us -> 6.69 us
  blocking collectives: 138 us -> 127 us
    pallas_call x0 -> x1, Pallas kernels: none -> 60.9 us  [flash(): pl.pallas_call(kern, grid=(n_blocks,), in_specs=[pl.BlockSpec((t, width),...]
    dot_general x4 -> x0, matrix products: 47.5 us -> none  [the longest x2 25.3 us: fold_scores(): jnp.einsum('tgrk,kgd->tgrd', expo.astype(jnp.bfloat16), value_rows, prefe...]
    all_to_all x3 -> x0, waiting for transfers between devices: 33.3 us -> none  [the longest x1 29.6 us: on_device(): lax.all_to_all(summed_output.reshape(request_count, token_index, KEY_VALU...]
    all_gather x1, waiting for transfers between devices: 16.3 us -> 47.9 us  [on_device(): lax.all_gather(page_pool, 'req', axis=0, tiled=True)]
    reduce_sum x4 -> x0, other arithmetic: 26.5 us -> none  [the longest x2 22.1 us: fold_scores(): grand_total = decay * grand_total + jnp.sum(expo, axis=-1)]
    all_gather x1, waiting for transfers between devices: 15.4 us -> 41.1 us  [on_device(): segment = lax.all_gather(suffix_kv, 'exp', axis=0, tiled=True)]
    all_to_all x3 -> x0, starting transfers between devices: 12.3 us -> none  [the longest x1 4.95 us: on_device(): lax.all_to_all(summed_output.reshape(request_count, token_index, KEY_VALU...]
    all_gather x1 -> x0, blocking collectives: 12.1 us -> none  [on_device(): lax.all_gather(query_counts.astype(jnp.bfloat16), 'req', axis=0, tiled=True)]
  transfers between devices with their start and end apart: 6 -> 3, of which waited for: 5 -> 3; matrix products, arithmetic and copies ran while one was open for 8% -> 1% of each run, Pallas kernels for 0% -> 0%
where the time goes in v2:
time: 509 us
  waiting for transfers between devices  232 us (46%)
  blocking collectives  127 us (25%)
  Pallas kernels  60.9 us (12%)
  matrix products  59 us (12%)
  between operations  13.6 us (3%)
  starting transfers between devices  6.69 us (1%)
  local copies, waits for them, and re-layouts  5.67 us (1%)
    all_to_all x1, waiting for transfers between devices, on_device(): lax.all_to_all(jnp.dot(inner, w_down[0], preferred_element_type=jnp.float...  141 us
    all_to_all x1, blocking collectives, on_device(): lax.all_to_all(outgoing, ('req', 'exp'), split_axis=0, concat_axis=0, til...  127 us
    pallas_call x1, Pallas kernels, flash(): pl.pallas_call(kern, grid=(n_blocks,), in_specs=[pl.BlockSpec((t, width),...  60.9 us
    all_gather x1, waiting for transfers between devices, on_device(): lax.all_gather(page_pool, 'req', axis=0, tiled=True)  47.9 us
    all_gather x1, waiting for transfers between devices, on_device(): segment = lax.all_gather(suffix_kv, 'exp', axis=0, tiled=True)  41.1 us
    dot_general x1, matrix products, on_device(): jnp.dot(inner, w_down[0], preferred_element_type=jnp.float32)  28.9 us
  transfers between devices with their start and end apart: 3, of which 3 were waited for; matrix products, arithmetic and copies ran while one was open for 1% of the time, Pallas kernels for 0%

profile of v2, /device:TPU:34, one launch (start us, length us, event | category | flops | bytes accessed | tf_op | source)
XLA Modules:
  0.0 509.1 jit_solution(11866366885765962663)
XLA Ops:
  6.5 0.0 copy-start
  6.5 0.0 copy-start.5
  6.5 0.0 copy-start.3
  6.5 0.0 all-gather.5.cloned.1.call-start
  6.5 0.7 all-gather.5.cloned.1.call-update
  7.3 0.0 all-gather.3.cloned.1.call-start
  7.3 0.7 all-gather.3.cloned.1.call-update
  8.0 0.8 reduce-window.4
  8.8 0.1 convert_reduce_fusion.1
  8.9 0.8 convert_reduce_fusion
  9.7 0.2 convolution_convert_fusion.3
  9.9 0.1 copy.24
  10.1 1.1 broadcast_in_dim.52
  11.2 0.4 copy.27
  11.6 0.0 copy-done.5
  11.6 0.1 select_reduce_fusion.2
  11.7 0.0 copy-done.3
  11.7 0.1 convolution_convert_fusion.2
  11.9 0.1 fusion.15
  12.0 0.4 fusion.12
  12.5 1.6 pad_maximum_fusion.w_ref
  14.1 41.1 %all-gather.5.cloned.1.call-done.suf_ref = bf16[2048,512]{1,0:T(8,128)(2,1)} async-done(((bf16[128,512]{1,0:T(8,128)(2,1)}), bf16[2048,512]{1,0:T(8,128)(2,1)}) %all-gather.5.cloned.1.call-update) | async-done | bytes 2097168 | tf_op jit(solution)/shard_map/all_gather | solution.py:131
  55.2 47.9 %all-gather.3.cloned.1.call-done = bf16[56,128,512]{2,1,0:T(8,128)(2,1)} async-done(((bf16[7,128,512]{2,1,0:T(8,128)(2,1)}), bf16[56,128,512]{2,1,0:T(8,128)(2,1)}) %all-gather.3.cloned.1.call-update) | async-done | bytes 7340048 | tf_op jit(solution)/shard_map/all_gather | solution.py:128
  103.1 0.0 copy-start.2
  103.1 60.9 %shard_map.118 = bf16[128,1280]{1,0:T(8,128)(2,1)} custom-call(bf16[128,1280]{1,0:T(8,128)(2,1)} %q_ref.1, bf16[128,9216]{1,0:T(8,128)(2,1)} %pad_maximum_fusion.w_ref, bf16[7168,512]{1,0:T(8,128)(2,1)} %bitcast.52, bf16[2048,512]{1,0:T(8,128)(2,1)} %all-gather.5.cloned.1.call-done.suf_ref), custom_call_target="tpu_custom_call" | custom-call | tf_op jit(solution)/shard_map/pallas_call | solution.py:81
  164.1 0.0 copy-done.2
  164.1 4.0 fusion.7
  168.1 0.2 fusion.9
  168.3 0.1 broadcast_in_dim.100
  168.4 3.2 convolution_convert_fusion.1
  171.6 0.0 copy-start.4
  171.6 126.9 %all_to_all.10 = bf16[128,16,2560]{2,1,0:T(8,128)(2,1)S(1)} all-to-all(bf16[128,16,2560]{2,1,0:T(8,128)(2,1)S(1)} %bitcast.46), channel_id=1, replica_groups=mesh['req'=8,'exp'=16] {'req','exp'}, dimensions={0} | all-to-all | bytes 20971520 | tf_op jit(solution)/shard_map/all_to_all | solution.py:181
  298.5 0.0 copy-start.1
  298.5 3.8 copy-done.1
  302.3 0.0 copy-done.4
  302.3 10.2 %fusion.3 = f32[2048,768]{1,0:T(8,128)} fusion(bf16[2048,2560]{1,0:T(8,128)(2,1)S(1)} %bitcast.48, bf16[1,2560,768]{2,1,0:T(8,128)(2,1)S(1)} %copy-done.4), kind=kOutput, calls=%fused_computation.5 | convolution fusion | flops 8053063680 | bytes 20709376 | tf_op jit(solution)/shard_map/dot_general | solution.py:184
  312.5 28.9 %convolution_convert_fusion = bf16[2048,2560]{1,0:T(8,128)(2,1)} fusion(f32[2048,768]{1,0:T(8,128)} %fusion.3, bf16[2048,2560]{1,0:T(8,128)(2,1)} %bitcast.49, bf16[1,768,2560]{2,1,0:T(8,128)(2,1)} %param.23, bf16[1,2560,768]{2,1,0:T(8,128)(2,1)} %param.22), kind=kOutput, calls=%fused_computation | convolution fusion | flops 16120807424 | bytes 35127296 | tf_op jit(solution)/shard_map/dot_general | solution.py:188
  341.4 6.6 %all-to-all-start.1 = ((bf16[128,16,2560]{2,1,0:T(8,128)(2,1)}), bf16[128,16,2560]{2,1,0:T(8,128)(2,1)}, u32[]{:S(2)}, u32[]{:S(2)}) async-start(bf16[128,16,2560]{2,1,0:T(8,128)(2,1)} %bitcast.47), calls=%async_computation.1 | async-start | bytes 20971520 | tf_op jit(solution)/shard_map/all_to_all | solution.py:187
  348.1 0.0 copy-done
  348.1 0.4 fusion.17
  348.6 0.1 select_convert_fusion
  348.8 0.1 fusion.13
  348.9 141.3 %all-to-all-done.1 = bf16[128,16,2560]{2,1,0:T(8,128)(2,1)} async-done(((bf16[128,16,2560]{2,1,0:T(8,128)(2,1)}), bf16[128,16,2560]{2,1,0:T(8,128)(2,1)}, u32[]{:S(2)}, u32[]{:S(2)}) %all-to-all-start.1) | async-done | bytes 10485792 | tf_op jit(solution)/shard_map/all_to_all | solution.py:187
  490.2 0.1 broadcast_in_dim.65
  490.3 5.5 %fusion.26 = f32[128,2560]{1,0:T(8,128)S(1)} fusion(bf16[128,2048]{0,1:T(8,128)(2,1)S(1)} %bitcast.54, bf16[2048,2560]{1,0:T(8,128)(2,1)} %bitcast.16), kind=kOutput, calls=%fused_computation.54 | convolution fusion | flops 1342177280 | bytes 12320768 | tf_op jit(solution)/shard_map/dot_general | solution.py:206
  495.8 0.1 broadcast_in_dim.101
  495.9 6.4 %fusion.6 = bf16[128,2560]{1,0:T(8,128)(2,1)} fusion(f32[128,2560]{1,0:T(8,128)S(1)} %fusion.26, bf16[128,2048]{0,1:T(8,128)(2,1)S(1)} %bitcast.53, bf16[2048,2560]{1,0:T(8,128)(2,1)} %bitcast.16, bf16[128,2560]{1,0:T(8,128)(2,1)S(1)} %fusion.7), kind=kOutput, calls=%fused_computation.10 | convolution fusion | flops 1343488000 | bytes 13631488 | tf_op jit(solution)/shard_map/dot_general | solution.py:206
  (10 shorter events, 0.2 us)
Async XLA Ops:
  6.5 341.5 %copy-start = (bf16[2560,64]{0,1:T(8,128)(2,1)S(1)}, bf16[2560,64]{0,1:T(8,128)(2,1)}, u32[]{:S(2)}) copy-start(bf16[2560,64]{0,1:T(8,128)(2,1)} %param.19) | copy-start | bytes 983044
  6.5 5.0 copy-start.5
  6.5 5.1 %copy-start.3 = (s32[128,6]{0,1:T(8,128)S(1)}, s32[128,6]{0,1:T(8,128)}, u32[]{:S(2)}) copy-start(s32[128,6]{0,1:T(8,128)} %param.20) | copy-start | bytes 9220
  6.5 48.7 %all-gather.5.cloned.1.call-start = ((), (), s32[]{:S(2)}) async-start(), calls=%async_computation.3 | async-start | bytes 2228224 | tf_op jit(solution)/shard_map/all_gather | solution.py:131
  7.3 95.8 %all-gather.3.cloned.1.call-start = ((), (), s32[]{:S(2)}) async-start(), calls=%async_computation.2 | async-start | bytes 8257536 | tf_op jit(solution)/shard_map/all_gather | solution.py:128
  103.1 60.9 %copy-start.2 = (bf16[128,2560]{1,0:T(8,128)(2,1)S(1)}, bf16[128,2560]{1,0:T(8,128)(2,1)}, u32[]{:S(2)}) copy-start(bf16[128,2560]{1,0:T(8,128)(2,1)} %param.12) | copy-start | bytes 1966084
  171.6 130.7 %copy-start.4 = (bf16[1,2560,768]{2,1,0:T(8,128)(2,1)S(1)}, bf16[1,2560,768]{2,1,0:T(8,128)(2,1)}, u32[]{:S(2)}) copy-start(bf16[1,2560,768]{2,1,0:T(8,128)(2,1)} %param.21) | copy-start | bytes 11796484
  298.5 3.8 copy-start.1
  341.4 148.8 %all-to-all-start.1 = ((bf16[128,16,2560]{2,1,0:T(8,128)(2,1)}), bf16[128,16,2560]{2,1,0:T(8,128)(2,1)}, u32[]{:S(2)}, u32[]{:S(2)}) async-start(bf16[128,16,2560]{2,1,0:T(8,128)(2,1)} %bitcast.47), calls=%async_computation.1 | async-start | bytes 20971520 | tf_op jit(solution)/shard_map/all_to_all | solution.py:187
Sparse Core Ops, SparseCore 0:
  9.5 45.6 all-gather.4
  56.9 46.1 all-gather.2

commit v3 on v2

--- a/solution.py
+++ b/solution.py
@@ -23,20 +23,31 @@
 KEY_BLOCK = 512
 
 
-def attn_kernel(q_ref, w_ref, pool_ref, suf_ref, o_ref, qs, m_ref, l_ref, acc_ref, *, n_pool, n_blocks, groups, reps, hs):
+def attn_kernel(flags_ref, q_ref, w_ref, kv_ref, m_in, l_in, acc_in, *refs, first_call, last_call, groups, reps, hs):
+    if last_call:
+        o_ref, qs, m_ref, l_ref, acc_ref = refs
+    else:
+        m_out, l_out, acc_out, qs, m_ref, l_ref, acc_ref = refs
     j = pl.program_id(0)
     t = q_ref.shape[0]
+    key_block = kv_ref.shape[0]
 
     @pl.when(j == 0)
     def _():
         for g in range(groups):
             qs[g] = jnp.concatenate(
                 [q_ref[:, (g * reps + h) * hs:(g * reps + h + 1) * hs] for h in range(reps)], axis=0)
-        m_ref[...] = jnp.full(m_ref.shape, NEGATIVE_MASK, jnp.float32)
-        l_ref[...] = jnp.zeros(l_ref.shape, jnp.float32)
-        acc_ref[...] = jnp.zeros(acc_ref.shape, jnp.float32)
-
-    def step(kv_ref):
+        if first_call:
+            m_ref[...] = jnp.full(m_ref.shape, NEGATIVE_MASK, jnp.float32)
+            l_ref[...] = jnp.zeros(l_ref.shape, jnp.float32)
+            acc_ref[...] = jnp.zeros(acc_ref.shape, jnp.float32)
+        else:
+            m_ref[...] = m_in[...]
+            l_ref[...] = l_in[...]
+            acc_ref[...] = acc_in[...]
+
+    @pl.when(flags_ref[j] > 0)
+    def _():
         w = w_ref[...].astype(jnp.float32)
         live = (w > 0)[None]
         for g in range(groups):
@@ -44,58 +55,72 @@
             v = kv_ref[:, (groups + g) * hs:(groups + g + 1) * hs]
             s = lax.dot_general(qs[g], k, (((1,), (1,)), ((), ())),
                                 preferred_element_type=jnp.float32) * (1.0 / math.sqrt(hs))
-            s = s.reshape(reps, t, KEY_BLOCK)
+            s = jnp.where(live, s.reshape(reps, t, key_block), NEGATIVE_MASK)
             m_old = m_ref[g].reshape(reps, t, 1)
-            m_new = jnp.maximum(m_old, jnp.max(jnp.where(live, s, NEGATIVE_MASK), axis=-1, keepdims=True))
-            p = jnp.where(live, jnp.exp(s - m_new), 0.0) * w[None]
+            m_new = jnp.maximum(m_old, jnp.max(s, axis=-1, keepdims=True))
+            p = jnp.exp(s - m_new) * w[None]
             alpha = jnp.exp(m_old - m_new)
             l_ref[g] = (alpha * l_ref[g].reshape(reps, t, 1) + jnp.sum(p, axis=-1, keepdims=True)).reshape(reps * t, 1)
-            pv = jnp.dot(p.reshape(reps * t, KEY_BLOCK).astype(jnp.bfloat16), v, preferred_element_type=jnp.float32)
+            pv = jnp.dot(p.reshape(reps * t, key_block).astype(jnp.bfloat16), v, preferred_element_type=jnp.float32)
             acc_ref[g] = alpha.reshape(reps * t, 1) * acc_ref[g] + pv
             m_ref[g] = m_new.reshape(reps * t, 1)
 
-    @pl.when(j < n_pool)
+    @pl.when(j == pl.num_programs(0) - 1)
     def _():
-        step(pool_ref)
-
-    @pl.when(j >= n_pool)
-    def _():
-        step(suf_ref)
-
-    @pl.when(j == n_blocks - 1)
-    def _():
-        for g in range(groups):
-            for h in range(reps):
-                rows = slice(h * t, (h + 1) * t)
-                o_ref[:, (g * reps + h) * hs:(g * reps + h + 1) * hs] = (
-                    acc_ref[g, rows, :] / l_ref[g, rows, :]).astype(o_ref.dtype)
-
-
-def flash(queries, weights, pool_rows, suffix_rows, groups=2, hs=128):
+        if last_call:
+            for g in range(groups):
+                for h in range(reps):
+                    rows = slice(h * t, (h + 1) * t)
+                    o_ref[:, (g * reps + h) * hs:(g * reps + h + 1) * hs] = (
+                        acc_ref[g, rows, :] / l_ref[g, rows, :]).astype(o_ref.dtype)
+        else:
+            m_out[...] = m_ref[...]
+            l_out[...] = l_ref[...]
+            acc_out[...] = acc_ref[...]
+
+
+def flash(queries, weights, kv_rows, carry, first_call, last_call, groups, hs):
     t, width = queries.shape
     reps = width // hs // groups
-    n_pool = pool_rows.shape[0] // KEY_BLOCK
-    n_suf = suffix_rows.shape[0] // KEY_BLOCK
-    n_blocks = n_pool + n_suf
-    kern = functools.partial(attn_kernel, n_pool=n_pool, n_blocks=n_blocks, groups=groups, reps=reps, hs=hs)
-    return pl.pallas_call(
-        kern,
+    n_blocks = kv_rows.shape[0] // KEY_BLOCK
+    flags = (jnp.max(weights.reshape(t, n_blocks, KEY_BLOCK), axis=(0, 2)) > 0).astype(jnp.int32)
+    kern = functools.partial(attn_kernel, first_call=first_call, last_call=last_call,
+                             groups=groups, reps=reps, hs=hs)
+    state = [
+        jax.ShapeDtypeStruct((groups, reps * t, 1), jnp.float32),
+        jax.ShapeDtypeStruct((groups, reps * t, 1), jnp.float32),
+        jax.ShapeDtypeStruct((groups, reps * t, hs), jnp.float32),
+    ]
+    state_specs = [
+        pl.BlockSpec((groups, reps * t, 1), lambda j, f: (0, 0, 0)),
+        pl.BlockSpec((groups, reps * t, 1), lambda j, f: (0, 0, 0)),
+        pl.BlockSpec((groups, reps * t, hs), lambda j, f: (0, 0, 0)),
+    ]
+    if last_call:
+        out_shape = jax.ShapeDtypeStruct((t, width), jnp.bfloat16)
+        out_specs = pl.BlockSpec((t, width), lambda j, f: (0, 0))
+    else:
+        out_shape, out_specs = state, state_specs
+    grid_spec = pltpu.PrefetchScalarGridSpec(
+        num_scalar_prefetch=1,
         grid=(n_blocks,),
         in_specs=[
-            pl.BlockSpec((t, width), lambda j: (0, 0)),
-            pl.BlockSpec((t, KEY_BLOCK), lambda j: (0, j)),
-            pl.BlockSpec((KEY_BLOCK, pool_rows.shape[1]), lambda j: (jnp.minimum(j, n_pool - 1), 0)),
-            pl.BlockSpec((KEY_BLOCK, suffix_rows.shape[1]), lambda j: (jnp.maximum(j - n_pool, 0), 0)),
-        ],
-        out_specs=pl.BlockSpec((t, width), lambda j: (0, 0)),
-        out_shape=jax.ShapeDtypeStruct((t, width), jnp.bfloat16),
+            pl.BlockSpec((t, width), lambda j, f: (0, 0)),
+            pl.BlockSpec((t, KEY_BLOCK), lambda j, f: (0, j)),
+            pl.BlockSpec((KEY_BLOCK, kv_rows.shape[1]), lambda j, f: (j, 0)),
+        ] + state_specs,
+        out_specs=out_specs,
         scratch_shapes=[
             pltpu.VMEM((groups, reps * t, hs), jnp.bfloat16),
             pltpu.VMEM((groups, reps * t, 1), jnp.float32),
             pltpu.VMEM((groups, reps * t, 1), jnp.float32),
             pltpu.VMEM((groups, reps * t, hs), jnp.float32),
         ],
-    )(queries, weights, pool_rows, suffix_rows)
+    )
+    if carry is None:
+        carry = tuple(jnp.zeros(s.shape, s.dtype) for s in state)
+    return pl.pallas_call(kern, grid_spec=grid_spec, out_shape=out_shape)(
+        flags, queries, weights, kv_rows, *carry)
 
 
 def on_device(
@@ -128,7 +153,8 @@
     pool_rows = lax.all_gather(page_pool, "req", axis=0, tiled=True).reshape(
         pool_all * PAGE_TOKENS, 2 * row_width
     )
-    segment = lax.all_gather(suffix_kv, "exp", axis=0, tiled=True)
+    pool_rows, suffix_after = lax.optimization_barrier((pool_rows, suffix_kv))
+    segment = lax.all_gather(suffix_after, "exp", axis=0, tiled=True)
     counts = jnp.sum(
         (page_table[0][:, :, None] == jnp.arange(pool_all, dtype=jnp.int32)[None, None, :]).astype(
             jnp.float32
@@ -138,14 +164,18 @@
     query_counts = jnp.dot(pick.astype(jnp.float32), counts, precision=lax.Precision.HIGHEST)
     keypos = jnp.arange(segment.shape[0], dtype=jnp.int32)
     suffix_weights = (keypos[None, :] <= positions[:, None]) & (keypos[None, :] >= first[:, None])
-    weights = jnp.concatenate(
-        [
-            jnp.repeat(query_counts, PAGE_TOKENS, axis=1).astype(jnp.bfloat16),
-            suffix_weights.astype(jnp.bfloat16),
-        ],
-        axis=1,
-    )
-    attended = flash(queries, weights, pool_rows, segment, groups=KEY_VALUE_HEADS, hs=HEAD_SIZE)
+    pool_weights = jnp.repeat(query_counts, PAGE_TOKENS, axis=1).astype(jnp.bfloat16)
+    carry = flash(queries, pool_weights, pool_rows, None, True, False, KEY_VALUE_HEADS, HEAD_SIZE)
+    attended = flash(
+        queries,
+        suffix_weights.astype(jnp.bfloat16),
+        segment,
+        carry,
+        False,
+        True,
+        KEY_VALUE_HEADS,
+        HEAD_SIZE,
+    )
     projected = jnp.dot(attended, w_out, preferred_element_type=jnp.float32)
     resid = lax.optimization_barrier((hidden.astype(jnp.float32) + projected).astype(jnp.bfloat16))
     resid_f = resid.astype(jnp.float32)

time: 509 us -> 475 us (0.933)
  waiting for transfers between devices: 232 us -> 191 us
    all_gather x1, waiting for transfers between devices: 41.1 us -> 0.01 us  [on_device(): segment = lax.all_gather(suffix_after, 'exp', axis=0, tiled=True)]
    pallas_call x1 -> x2, Pallas kernels: 60.9 us -> 57.5 us  [flash(): pl.pallas_call(kern, grid_spec=grid_spec, out_shape=out_shape)]
  transfers between devices with their start and end apart: 3 -> 3, of which waited for: 3 -> 2; matrix products, arithmetic and copies ran while one was open for 1% -> 3% of each run, Pallas kernels for 0% -> 10%
where the time goes in v3:
time: 475 us; the launch traced here: 474 us
  waiting for transfers between devices  191 us (40%)
  blocking collectives  131 us (28%)
  matrix products  59 us (12%)
  Pallas kernels  57.5 us (12%)
  between operations  13.6 us (3%)
  local copies, waits for them, and re-layouts  8.74 us (2%)
  starting transfers between devices  6.69 us (1%)
  other arithmetic  6.69 us (1%)
    all_to_all x1, waiting for transfers between devices, on_device(): lax.all_to_all(jnp.dot(inner, w_down[0], preferred_element_type=jnp.float...  141 us
    all_to_all x1, blocking collectives, on_device(): lax.all_to_all(outgoing, ('req', 'exp'), split_axis=0, concat_axis=0, til...  131 us
    pallas_call x2, Pallas kernels, flash(): pl.pallas_call(kern, grid_spec=grid_spec, out_shape=out_shape)  57.5 us
    all_gather x1, waiting for transfers between devices, on_device(): lax.all_gather(page_pool, 'req', axis=0, tiled=True)  49.1 us
    dot_general x1, matrix products, on_device(): jnp.dot(inner, w_down[0], preferred_element_type=jnp.float32)  28.9 us
    dot_general x1, matrix products, on_device(): jnp.dot(flat_rows, w_gate[0], preferred_element_type=jnp.float32)  10.2 us
  transfers between devices with their start and end apart: 3, of which 2 were waited for; matrix products, arithmetic and copies ran while one was open for 3% of the time, Pallas kernels for 10%

profile of v3, /device:TPU:34, one launch (start us, length us, event | category | flops | bytes accessed | tf_op | source)
XLA Modules:
  0.0 474.3 jit_solution(13413397170687321258)
XLA Ops:
  6.5 0.0 copy-start
  6.5 0.0 all-gather.3.cloned.1.call-start
  6.5 0.7 all-gather.3.cloned.1.call-update
  7.3 0.0 all-gather.5.cloned.1.call-start
  7.3 49.1 %all-gather.3.cloned.1.call-done = bf16[56,128,512]{2,1,0:T(8,128)(2,1)} async-done(((bf16[7,128,512]{2,1,0:T(8,128)(2,1)}), bf16[56,128,512]{2,1,0:T(8,128)(2,1)}) %all-gather.3.cloned.1.call-update) | async-done | bytes 7340048 | tf_op jit(solution)/shard_map/all_gather | solution.py:153
  56.4 0.0 all-gather.5.cloned.1.call-update
  56.4 0.8 reduce-window.4
  57.3 0.1 convert_reduce_fusion.1
  57.4 0.8 convert_reduce_fusion
  58.1 0.2 convolution_convert_fusion.3
  58.4 0.1 copy.24
  58.5 1.1 broadcast_in_dim.57
  59.6 1.6 copy.27
  61.2 1.2 broadcast_reduce_fusion
  62.4 0.1 reduce_max.36
  62.5 0.1 reduce_max.37
  62.6 0.0 copy-done.5
  62.6 0.1 select_reduce_fusion.2
  62.7 0.0 copy-done.3
  62.7 0.3 fusion.14
  63.1 0.6 compare_convert_fusion.flags_ref
  63.7 0.6 compare_convert_fusion.1.flags_ref
  64.3 0.1 convolution_convert_fusion.2
  64.4 0.1 fusion.16
  64.6 1.3 fusion.12.w_ref
  65.8 0.9 broadcast_6_m_in_l_in.2.m_in.l_in
  66.7 0.9 broadcast_in_dim.58.acc_in
  67.6 46.3 %shard_map.118 = (f32[2,640,1]{2,1,0:T(8,128)}, f32[2,640,1]{2,1,0:T(8,128)}, f32[2,640,128]{2,1,0:T(8,128)}) custom-call(s32[14]{0:T(128)} %compare_convert_fusion.flags_ref, bf16[128,1280]{1,0:T(8,128)(2,1)} %q_ref.3, bf16[128,7168]{1,0:T(8,128)(2,1)} %bitcast.52, bf16[7168,512]{1,0:T(8,128)(2,1)} %bitcast.51, ...), custom_call_target="tpu_custom_call" | custom-call | tf_op jit(solution)/shard_map/pallas_call | solution.py:122
  113.9 11.2 %shard_map.119 = bf16[128,1280]{1,0:T(8,128)(2,1)} custom-call(s32[4]{0:T(128)} %compare_convert_fusion.1.flags_ref, bf16[128,1280]{1,0:T(8,128)(2,1)} %q_ref.3, bf16[128,2048]{1,0:T(8,128)(2,1)} %fusion.12.w_ref, bf16[2048,512]{1,0:T(8,128)(2,1)} %all-gather.5.cloned.1.call-done.kv_ref, f32[2,640,1]{2,1,0:T(8,128)} %get-tuple-element.12.m_in, ...), custom_call_target="tpu_custom_call" | custom-call | tf_op jit(solution)/shard_map/pallas_call | solution.py:122
  125.1 0.0 copy-done.2
  125.1 4.0 fusion.7
  129.1 0.2 fusion.9
  129.3 0.1 broadcast_in_dim.104
  129.4 3.2 convolution_convert_fusion.1
  132.6 0.0 copy-start.4
  132.6 131.0 %all_to_all.10 = bf16[128,16,2560]{2,1,0:T(8,128)(2,1)S(1)} all-to-all(bf16[128,16,2560]{2,1,0:T(8,128)(2,1)S(1)} %bitcast.46), channel_id=1, replica_groups=mesh['req'=8,'exp'=16] {'req','exp'}, dimensions={0} | all-to-all | bytes 20971520 | tf_op jit(solution)/shard_map/all_to_all | solution.py:211
  263.6 3.8 copy-done.1
  267.5 10.2 %fusion.3 = f32[2048,768]{1,0:T(8,128)} fusion(bf16[2048,2560]{1,0:T(8,128)(2,1)S(1)} %bitcast.48, bf16[1,2560,768]{2,1,0:T(8,128)(2,1)S(1)} %copy-done.4), kind=kOutput, calls=%fused_computation.5 | convolution fusion | flops 8053063680 | bytes 20709376 | tf_op jit(solution)/shard_map/dot_general | solution.py:214
  277.6 28.9 %convolution_convert_fusion = bf16[2048,2560]{1,0:T(8,128)(2,1)} fusion(f32[2048,768]{1,0:T(8,128)} %fusion.3, bf16[2048,2560]{1,0:T(8,128)(2,1)} %bitcast.49, bf16[1,768,2560]{2,1,0:T(8,128)(2,1)} %param.23, bf16[1,2560,768]{2,1,0:T(8,128)(2,1)} %param.22), kind=kOutput, calls=%fused_computation | convolution fusion | flops 16120807424 | bytes 35127296 | tf_op jit(solution)/shard_map/dot_general | solution.py:218
  306.6 6.6 %all-to-all-start.1 = ((bf16[128,16,2560]{2,1,0:T(8,128)(2,1)}), bf16[128,16,2560]{2,1,0:T(8,128)(2,1)}, u32[]{:S(2)}, u32[]{:S(2)}) async-start(bf16[128,16,2560]{2,1,0:T(8,128)(2,1)} %bitcast.47), calls=%async_computation.1 | async-start | bytes 20971520 | tf_op jit(solution)/shard_map/all_to_all | solution.py:217
  313.2 0.4 fusion.18
  313.8 0.1 select_convert_fusion
  313.9 0.1 fusion.13
  314.1 141.3 %all-to-all-done.1 = bf16[128,16,2560]{2,1,0:T(8,128)(2,1)} async-done(((bf16[128,16,2560]{2,1,0:T(8,128)(2,1)}), bf16[128,16,2560]{2,1,0:T(8,128)(2,1)}, u32[]{:S(2)}, u32[]{:S(2)}) %all-to-all-start.1) | async-done | bytes 10485792 | tf_op jit(solution)/shard_map/all_to_all | solution.py:217
  455.3 0.1 broadcast_in_dim.103
  455.4 5.5 %fusion.27 = f32[128,2560]{1,0:T(8,128)S(1)} fusion(bf16[128,2048]{0,1:T(8,128)(2,1)S(1)} %bitcast.54, bf16[2048,2560]{1,0:T(8,128)(2,1)} %bitcast.16), kind=kOutput, calls=%fused_computation.59 | convolution fusion | flops 1342177280 | bytes 12320768 | tf_op jit(solution)/shard_map/dot_general | solution.py:236
  461.0 0.1 broadcast_in_dim.105
  461.1 6.4 %fusion.6 = bf16[128,2560]{1,0:T(8,128)(2,1)} fusion(f32[128,2560]{1,0:T(8,128)S(1)} %fusion.27, bf16[128,2048]{0,1:T(8,128)(2,1)S(1)} %bitcast.53, bf16[2048,2560]{1,0:T(8,128)(2,1)} %bitcast.16, bf16[128,2560]{1,0:T(8,128)(2,1)S(1)} %fusion.7), kind=kOutput, calls=%fused_computation.10 | convolution fusion | flops 1343488000 | bytes 13631488 | tf_op jit(solution)/shard_map/dot_general | solution.py:236
  (18 shorter events, 0.2 us)
Async XLA Ops:
  6.5 306.7 %copy-start = (bf16[2560,64]{0,1:T(8,128)(2,1)S(1)}, bf16[2560,64]{0,1:T(8,128)(2,1)}, u32[]{:S(2)}) copy-start(bf16[2560,64]{0,1:T(8,128)(2,1)} %param.19) | copy-start | bytes 983044
  6.5 56.1 %copy-start.5 = (s32[1,4]{1,0:T(1,128)S(1)}, s32[1,4]{1,0:T(1,128)}, u32[]{:S(2)}) copy-start(s32[1,4]{1,0:T(1,128)} %param.15) | copy-start | bytes 52
  6.5 56.2 %copy-start.3 = (s32[128,6]{0,1:T(8,128)S(1)}, s32[128,6]{0,1:T(8,128)}, u32[]{:S(2)}) copy-start(s32[128,6]{0,1:T(8,128)} %param.20) | copy-start | bytes 9220
  6.5 49.9 %all-gather.3.cloned.1.call-start = ((), (), s32[]{:S(2)}) async-start(), calls=%async_computation.2 | async-start | bytes 8257536 | tf_op jit(solution)/shard_map/all_gather | solution.py:153
  7.3 106.6 %all-gather.5.cloned.1.call-start = ((), (), s32[]{:S(2)}) async-start(), calls=%async_computation.3 | async-start | bytes 2228224 | tf_op jit(solution)/shard_map/all_gather | solution.py:157
  67.6 57.5 %copy-start.2 = (bf16[128,2560]{1,0:T(8,128)(2,1)S(1)}, bf16[128,2560]{1,0:T(8,128)(2,1)}, u32[]{:S(2)}) copy-start(bf16[128,2560]{1,0:T(8,128)(2,1)} %param.12) | copy-start | bytes 1966084
  132.6 134.8 %copy-start.4 = (bf16[1,2560,768]{2,1,0:T(8,128)(2,1)S(1)}, bf16[1,2560,768]{2,1,0:T(8,128)(2,1)}, u32[]{:S(2)}) copy-start(bf16[1,2560,768]{2,1,0:T(8,128)(2,1)} %param.21) | copy-start | bytes 11796484
  263.6 3.8 copy-start.1
  306.6 148.8 %all-to-all-start.1 = ((bf16[128,16,2560]{2,1,0:T(8,128)(2,1)}), bf16[128,16,2560]{2,1,0:T(8,128)(2,1)}, u32[]{:S(2)}, u32[]{:S(2)}) async-start(bf16[128,16,2560]{2,1,0:T(8,128)(2,1)} %bitcast.47), calls=%async_computation.1 | async-start | bytes 20971520 | tf_op jit(solution)/shard_map/all_to_all | solution.py:217
Sparse Core Ops, SparseCore 0:
  9.1 47.3 all-gather.2
  58.5 43.7 all-gather.4

commit v4 on v3

--- a/solution.py
+++ b/solution.py
@@ -204,39 +204,45 @@
     select2 = jnp.broadcast_to(
         select[:, None], (n_experts, 2, capacity, token_index)
     ).reshape(2 * n_experts * capacity, token_index)
-    outgoing = jnp.dot(
-        select2.astype(jnp.bfloat16), normed, preferred_element_type=jnp.float32
-    ).astype(jnp.bfloat16)
-    outgoing = outgoing.reshape(2 * n_experts, capacity, D)
-    rows = lax.all_to_all(outgoing, ("req", "exp"), split_axis=0, concat_axis=0, tiled=True)
-    array_shape = rows.shape
-    flat_rows = rows.reshape(-1, D)
-    gate_part = jnp.dot(flat_rows, w_gate[0], preferred_element_type=jnp.float32)
-    up_part = jnp.dot(flat_rows, w_up[0], preferred_element_type=jnp.float32)
-    inner = (jax.nn.silu(gate_part) * up_part).astype(jnp.bfloat16)
-    returned = lax.all_to_all(
-        jnp.dot(inner, w_down[0], preferred_element_type=jnp.float32)
-        .astype(jnp.bfloat16)
-        .reshape(array_shape),
-        ("req", "exp"),
-        split_axis=0,
-        concat_axis=0,
-        tiled=True,
-    ).reshape(2 * n_experts * capacity, D)
     weight = jnp.where(
         jnp.transpose(select, (2, 0, 1))[:, :, None, :],
         gate_of[:, :, None, None],
         0.0,
     )
-    weight = jnp.broadcast_to(
-        weight, (token_index, n_experts, 2, capacity)
-    ).reshape(token_index, 2 * n_experts * capacity)
-    high = weight.astype(jnp.bfloat16)
-    low = (weight - high.astype(jnp.float32)).astype(jnp.bfloat16)
-    moe = jnp.dot(high, returned, preferred_element_type=jnp.float32) + jnp.dot(
-        low, returned, preferred_element_type=jnp.float32
-    )
-    return (resid_f + moe).astype(jnp.bfloat16)
+    weight = jnp.broadcast_to(weight, (token_index, n_experts, 2, capacity))
+    chunks = 2
+    part = capacity // chunks
+    select2 = select2.reshape(2 * n_experts, capacity, token_index)
+    moe = resid_f
+    for c in range(chunks):
+        picked_rows = select2[:, c * part:(c + 1) * part].reshape(-1, token_index)
+        outgoing = jnp.dot(
+            picked_rows.astype(jnp.bfloat16), normed, preferred_element_type=jnp.float32
+        ).astype(jnp.bfloat16)
+        outgoing = outgoing.reshape(2 * n_experts, part, D)
+        rows = lax.all_to_all(outgoing, ("req", "exp"), split_axis=0, concat_axis=0, tiled=True)
+        flat_rows = rows.reshape(-1, D)
+        gate_part = jnp.dot(flat_rows, w_gate[0], preferred_element_type=jnp.float32)
+        up_part = jnp.dot(flat_rows, w_up[0], preferred_element_type=jnp.float32)
+        inner = (jax.nn.silu(gate_part) * up_part).astype(jnp.bfloat16)
+        returned = lax.all_to_all(
+            jnp.dot(inner, w_down[0], preferred_element_type=jnp.float32)
+            .astype(jnp.bfloat16)
+            .reshape(rows.shape),
+            ("req", "exp"),
+            split_axis=0,
+            concat_axis=0,
+            tiled=True,
+        ).reshape(-1, D)
+        chunk_weight = weight[:, :, :, c * part:(c + 1) * part].reshape(token_index, -1)
+        high = chunk_weight.astype(jnp.bfloat16)
+        low = (chunk_weight - high.astype(jnp.float32)).astype(jnp.bfloat16)
+        moe = (
+            moe
+            + jnp.dot(high, returned, preferred_element_type=jnp.float32)
+            + jnp.dot(low, returned, preferred_element_type=jnp.float32)
+        )
+    return moe.astype(jnp.bfloat16)
 
 
 def solution(mesh):

time: 475 us -> 431 us (0.907)
  blocking collectives: 131 us -> 0 us
  waiting for transfers between devices: 191 us -> 245 us
  starting transfers between devices: 6.69 us -> 32.1 us
  matrix products: 59 us -> 68.3 us
    all_to_all x1 -> x0, blocking collectives: 131 us -> none  [on_device(): lax.all_to_all(outgoing, ('req', 'exp'), split_axis=0, concat_axis=0, til...]
    all_to_all x0 -> x2, waiting for transfers between devices: none -> 99.6 us  [on_device(): lax.all_to_all(outgoing, ('req', 'exp'), split_axis=0, concat_axis=0, til...]
    all_to_all x1 -> x2, waiting for transfers between devices: 141 us -> 95.8 us  [on_device(): lax.all_to_all(jnp.dot(inner, w_down[0], preferred_element_type=jnp.float...]
    dot_general x1 -> x4, matrix products: 3.23 us -> 22.8 us  [the longest x2 14.9 us: on_device(): up_part = jnp.dot(flat_rows, w_up[0], preferred_element_type=jnp.float32)]
    all_to_all x0 -> x2, starting transfers between devices: none -> 18.9 us  [on_device(): lax.all_to_all(outgoing, ('req', 'exp'), split_axis=0, concat_axis=0, til...]
    dot_general x1 -> x2, matrix products: 28.9 us -> 12 us  [on_device(): jnp.dot(inner, w_down[0], preferred_element_type=jnp.float32)]
    all_to_all x1 -> x2, starting transfers between devices: 6.65 us -> 13.1 us  [on_device(): lax.all_to_all(jnp.dot(inner, w_down[0], preferred_element_type=jnp.float...]
    dot_general x1 -> x2, matrix products: 10.2 us -> 14.4 us  [on_device(): jnp.dot(flat_rows, w_gate[0], preferred_element_type=jnp.float32)]
  transfers between devices with their start and end apart: 3 -> 6, of which waited for: 2 -> 5; matrix products, arithmetic and copies ran while one was open for 3% -> 15% of each run, Pallas kernels for 10% -> 11%
where the time goes in v4:
time: 431 us; the launch traced here: 427 us
  waiting for transfers between devices  245 us (57%)
  matrix products  68.3 us (16%)
  Pallas kernels  56.4 us (13%)
  starting transfers between devices  32.1 us (7%)
  between operations  13.7 us (3%)
  other arithmetic  6.61 us (2%)
  local copies, waits for them, and re-layouts  4.93 us (1%)
    all_to_all x2, waiting for transfers between devices, on_device(): lax.all_to_all(outgoing, ('req', 'exp'), split_axis=0, concat_axis=0, til...  99.6 us
    all_to_all x2, waiting for transfers between devices, on_device(): lax.all_to_all(jnp.dot(inner, w_down[0], preferred_element_type=jnp.float...  95.8 us
    pallas_call x2, Pallas kernels, flash(): pl.pallas_call(kern, grid_spec=grid_spec, out_shape=out_shape)  56.4 us
    all_gather x1, waiting for transfers between devices, on_device(): lax.all_gather(page_pool, 'req', axis=0, tiled=True)  49.1 us
    all_to_all x2, starting transfers between devices, on_device(): lax.all_to_all(outgoing, ('req', 'exp'), split_axis=0, concat_axis=0, til...  18.9 us
    dot_general x2, matrix products, on_device(): up_part = jnp.dot(flat_rows, w_up[0], preferred_element_type=jnp.float32)  14.9 us
    dot_general x2, matrix products, on_device(): jnp.dot(flat_rows, w_gate[0], preferred_element_type=jnp.float32)  14.4 us
    all_to_all x2, starting transfers between devices, on_device(): lax.all_to_all(jnp.dot(inner, w_down[0], preferred_element_type=jnp.float...  13.1 us
  transfers between devices with their start and end apart: 6, of which 5 were waited for; matrix products, arithmetic and copies ran while one was open for 15% of the time, Pallas kernels for 11%

profile of v4, /device:TPU:34, one launch (start us, length us, event | category | flops | bytes accessed | tf_op | source)
XLA Modules:
  0.0 427.4 jit_solution(6205725677891243100)
XLA Ops:
  6.5 0.7 all-gather.3.cloned.1.call-update
  7.3 49.1 %all-gather.3.cloned.1.call-done = bf16[56,128,512]{2,1,0:T(8,128)(2,1)} async-done(((bf16[7,128,512]{2,1,0:T(8,128)(2,1)}), bf16[56,128,512]{2,1,0:T(8,128)(2,1)}) %all-gather.3.cloned.1.call-update) | async-done | bytes 7340048 | tf_op jit(solution)/shard_map/all_gather | solution.py:153
  56.4 0.8 reduce-window.4
  57.3 0.1 convert_reduce_fusion.1
  57.4 0.8 convert_reduce_fusion
  58.1 0.2 convolution_convert_fusion.5
  58.4 0.1 copy.24
  58.5 1.2 broadcast_reduce_fusion
  59.7 0.1 reduce_max.36
  59.8 1.1 broadcast_in_dim.65
  60.9 1.6 copy.27
  62.5 0.1 reduce_max.37
  62.6 0.1 select_reduce_fusion.2
  62.7 0.3 fusion.54
  63.1 0.6 compare_convert_fusion.1.flags_ref
  63.7 0.6 compare_convert_fusion.flags_ref
  64.3 0.1 convolution_convert_fusion.4
  64.4 0.1 fusion.57
  64.6 1.3 fusion.53.w_ref
  65.8 0.9 broadcast_6_m_in_l_in.2.m_in.l_in
  66.7 0.9 broadcast_in_dim.66.acc_in
  67.6 45.1 %shard_map.118 = (f32[2,640,1]{2,1,0:T(8,128)}, f32[2,640,1]{2,1,0:T(8,128)}, f32[2,640,128]{2,1,0:T(8,128)}) custom-call(s32[14]{0:T(128)} %compare_convert_fusion.flags_ref, bf16[128,1280]{1,0:T(8,128)(2,1)} %q_ref.3, bf16[128,7168]{1,0:T(8,128)(2,1)} %bitcast.102, bf16[7168,512]{1,0:T(8,128)(2,1)} %bitcast.101, ...), custom_call_target="tpu_custom_call" | custom-call | tf_op jit(solution)/shard_map/pallas_call | solution.py:122
  112.7 11.3 %shard_map.119 = bf16[128,1280]{1,0:T(8,128)(2,1)} custom-call(s32[4]{0:T(128)} %compare_convert_fusion.1.flags_ref, bf16[128,1280]{1,0:T(8,128)(2,1)} %q_ref.3, bf16[128,2048]{1,0:T(8,128)(2,1)} %fusion.53.w_ref, bf16[2048,512]{1,0:T(8,128)(2,1)} %all-gather.5.cloned.1.call-done.kv_ref, f32[2,640,1]{2,1,0:T(8,128)} %get-tuple-element.12.m_in, ...), custom_call_target="tpu_custom_call" | custom-call | tf_op jit(solution)/shard_map/pallas_call | solution.py:122
  124.0 4.0 fusion.38
  128.0 0.2 fusion.50
  128.3 0.1 broadcast_in_dim.108
  128.3 3.9 fusion.16
  132.3 12.4 %all-to-all-start = ((bf16[128,8,2560]{2,1,0:T(8,128)(2,1)}), bf16[128,8,2560]{2,1,0:T(8,128)(2,1)}, u32[]{:S(2)}, u32[]{:S(2)}) async-start(bf16[128,8,2560]{2,1,0:T(8,128)(2,1)} %fusion.16), calls=%async_computation | async-start | bytes 10485760 | tf_op jit(solution)/shard_map/all_to_all | solution.py:223
  144.7 3.9 fusion.17
  148.6 58.2 %all-to-all-done = bf16[128,8,2560]{2,1,0:T(8,128)(2,1)} async-done(((bf16[128,8,2560]{2,1,0:T(8,128)(2,1)}), bf16[128,8,2560]{2,1,0:T(8,128)(2,1)}, u32[]{:S(2)}, u32[]{:S(2)}) %all-to-all-start) | async-done | bytes 5242912 | tf_op jit(solution)/shard_map/all_to_all | solution.py:223
  206.8 6.5 %all-to-all-start.2 = ((bf16[128,8,2560]{2,1,0:T(8,128)(2,1)}), bf16[128,8,2560]{2,1,0:T(8,128)(2,1)}, u32[]{:S(2)}, u32[]{:S(2)}) async-start(bf16[128,8,2560]{2,1,0:T(8,128)(2,1)} %fusion.17), calls=%async_computation.2 | async-start | bytes 10485760 | tf_op jit(solution)/shard_map/all_to_all | solution.py:223
  213.4 7.5 %fusion.12 = f32[1024,768]{1,0:T(8,128)S(1)} fusion(bf16[128,8,2560]{2,1,0:T(8,128)(2,1)} %all-to-all-done, bf16[1,2560,768]{2,1,0:T(8,128)(2,1)} %param.22), kind=kOutput, calls=%fused_computation.16 | convolution fusion | flops 4026531840 | bytes 12320768 | tf_op jit(solution)/shard_map/dot_general | solution.py:226
  220.9 7.2 %multiply_convert_fusion.1 = bf16[1024,768]{1,0:T(8,128)(2,1)S(1)} fusion(f32[1024,768]{1,0:T(8,128)S(1)} %fusion.12, bf16[1,2560,768]{2,1,0:T(8,128)(2,1)S(1)} %copy-done.3, bf16[128,8,2560]{2,1,0:T(8,128)(2,1)} %all-to-all-done), kind=kOutput, calls=%fused_computation.38 | convolution fusion | flops 4031250432 | bytes 13893632 | tf_op jit(solution)/shard_map/dot_general | solution.py:225
  228.1 6.0 %fusion.18 = bf16[128,8,2560]{2,1,0:T(8,128)(2,1)} fusion(bf16[1024,768]{1,0:T(8,128)(2,1)S(1)} %multiply_convert_fusion.1, bf16[1,768,2560]{2,1,0:T(8,128)(2,1)S(1)} %copy-done.5), kind=kOutput, calls=%fused_computation.22 | convolution fusion | flops 4029153280 | bytes 10747904 | tf_op jit(solution)/shard_map/dot_general | solution.py:229
  234.1 41.4 %all-to-all-done.2 = bf16[128,8,2560]{2,1,0:T(8,128)(2,1)} async-done(((bf16[128,8,2560]{2,1,0:T(8,128)(2,1)}), bf16[128,8,2560]{2,1,0:T(8,128)(2,1)}, u32[]{:S(2)}, u32[]{:S(2)}) %all-to-all-start.2) | async-done | bytes 5242912 | tf_op jit(solution)/shard_map/all_to_all | solution.py:223
  275.5 6.6 %all-to-all-start.1 = ((bf16[128,8,2560]{2,1,0:T(8,128)(2,1)}), bf16[128,8,2560]{2,1,0:T(8,128)(2,1)}, u32[]{:S(2)}, u32[]{:S(2)}) async-start(bf16[128,8,2560]{2,1,0:T(8,128)(2,1)} %fusion.18), calls=%async_computation.1 | async-start | bytes 10485760 | tf_op jit(solution)/shard_map/all_to_all | solution.py:228
  282.1 7.5 %fusion.4 = f32[1024,768]{1,0:T(8,128)S(1)} fusion(bf16[128,8,2560]{2,1,0:T(8,128)(2,1)} %all-to-all-done.2, bf16[1,2560,768]{2,1,0:T(8,128)(2,1)} %param.22), kind=kOutput, calls=%fused_computation.8 | convolution fusion | flops 4026531840 | bytes 12320768 | tf_op jit(solution)/shard_map/dot_general | solution.py:226
  289.6 7.2 %multiply_convert_fusion = bf16[1024,768]{1,0:T(8,128)(2,1)S(1)} fusion(f32[1024,768]{1,0:T(8,128)S(1)} %fusion.4, bf16[1,2560,768]{2,1,0:T(8,128)(2,1)S(1)} %copy-done.4, bf16[128,8,2560]{2,1,0:T(8,128)(2,1)} %all-to-all-done.2), kind=kOutput, calls=%fused_computation.37 | convolution fusion | flops 4031250432 | bytes 13893632 | tf_op jit(solution)/shard_map/dot_general | solution.py:225
  296.8 6.0 %fusion.19 = bf16[128,8,2560]{2,1,0:T(8,128)(2,1)} fusion(bf16[1024,768]{1,0:T(8,128)(2,1)S(1)} %multiply_convert_fusion, bf16[1,768,2560]{2,1,0:T(8,128)(2,1)S(1)} %copy-done.6), kind=kOutput, calls=%fused_computation.23 | convolution fusion | flops 4029153280 | bytes 10747904 | tf_op jit(solution)/shard_map/dot_general | solution.py:229
  302.8 41.4 %all-to-all-done.1 = bf16[128,8,2560]{2,1,0:T(8,128)(2,1)} async-done(((bf16[128,8,2560]{2,1,0:T(8,128)(2,1)}), bf16[128,8,2560]{2,1,0:T(8,128)(2,1)}, u32[]{:S(2)}, u32[]{:S(2)}) %all-to-all-start.1) | async-done | bytes 5242912 | tf_op jit(solution)/shard_map/all_to_all | solution.py:228
  344.2 6.5 %all-to-all-start.3 = ((bf16[128,8,2560]{2,1,0:T(8,128)(2,1)}), bf16[128,8,2560]{2,1,0:T(8,128)(2,1)}, u32[]{:S(2)}, u32[]{:S(2)}) async-start(bf16[128,8,2560]{2,1,0:T(8,128)(2,1)} %fusion.19), calls=%async_computation.3 | async-start | bytes 10485760 | tf_op jit(solution)/shard_map/all_to_all | solution.py:228
  350.7 0.4 fusion.66
  351.3 0.1 fusion.56
  351.5 3.4 fusion.26
  355.0 3.4 fusion.29
  358.4 54.5 %all-to-all-done.3 = bf16[128,8,2560]{2,1,0:T(8,128)(2,1)} async-done(((bf16[128,8,2560]{2,1,0:T(8,128)(2,1)}), bf16[128,8,2560]{2,1,0:T(8,128)(2,1)}, u32[]{:S(2)}, u32[]{:S(2)}) %all-to-all-start.3) | async-done | bytes 5242912 | tf_op jit(solution)/shard_map/all_to_all | solution.py:228
  412.9 3.4 fusion.32
  416.3 4.2 fusion.39
  (36 shorter events, 0.5 us)
Async XLA Ops:
  6.5 344.2 %copy-start = (bf16[2560,64]{0,1:T(8,128)(2,1)S(1)}, bf16[2560,64]{0,1:T(8,128)(2,1)}, u32[]{:S(2)}) copy-start(bf16[2560,64]{0,1:T(8,128)(2,1)} %param.19) | copy-start | bytes 983044
  6.5 56.1 %copy-start.7 = (s32[1,4]{1,0:T(1,128)S(1)}, s32[1,4]{1,0:T(1,128)}, u32[]{:S(2)}) copy-start(s32[1,4]{1,0:T(1,128)} %param.15) | copy-start | bytes 52
  6.5 56.2 %copy-start.2 = (s32[128,6]{0,1:T(8,128)S(1)}, s32[128,6]{0,1:T(8,128)}, u32[]{:S(2)}) copy-start(s32[128,6]{0,1:T(8,128)} %param.20) | copy-start | bytes 9220
  6.5 49.9 %all-gather.3.cloned.1.call-start = ((), (), s32[]{:S(2)}) async-start(), calls=%async_computation.4 | async-start | bytes 8257536 | tf_op jit(solution)/shard_map/all_gather | solution.py:153
  7.3 105.4 %all-gather.5.cloned.1.call-start = ((), (), s32[]{:S(2)}) async-start(), calls=%async_computation.5 | async-start | bytes 2228224 | tf_op jit(solution)/shard_map/all_gather | solution.py:157
  112.7 11.3 %copy-start.1 = (bf16[128,2560]{1,0:T(8,128)(2,1)S(1)}, bf16[128,2560]{1,0:T(8,128)(2,1)}, u32[]{:S(2)}) copy-start(bf16[128,2560]{1,0:T(8,128)(2,1)} %param.12) | copy-start | bytes 1966084
  132.3 74.5 %all-to-all-start = ((bf16[128,8,2560]{2,1,0:T(8,128)(2,1)}), bf16[128,8,2560]{2,1,0:T(8,128)(2,1)}, u32[]{:S(2)}, u32[]{:S(2)}) async-start(bf16[128,8,2560]{2,1,0:T(8,128)(2,1)} %fusion.16), calls=%async_computation | async-start | bytes 10485760 | tf_op jit(solution)/shard_map/all_to_all | solution.py:223
  206.8 68.7 %all-to-all-start.2 = ((bf16[128,8,2560]{2,1,0:T(8,128)(2,1)}), bf16[128,8,2560]{2,1,0:T(8,128)(2,1)}, u32[]{:S(2)}, u32[]{:S(2)}) async-start(bf16[128,8,2560]{2,1,0:T(8,128)(2,1)} %fusion.17), calls=%async_computation.2 | async-start | bytes 10485760 | tf_op jit(solution)/shard_map/all_to_all | solution.py:223
  213.3 7.5 %copy-start.3 = (bf16[1,2560,768]{2,1,0:T(8,128)(2,1)S(1)}, bf16[1,2560,768]{2,1,0:T(8,128)(2,1)}, u32[]{:S(2)}) copy-start(bf16[1,2560,768]{2,1,0:T(8,128)(2,1)} %param.21) | copy-start | bytes 11796484
  220.8 7.2 %copy-start.5 = (bf16[1,768,2560]{2,1,0:T(8,128)(2,1)S(1)}, bf16[1,768,2560]{2,1,0:T(8,128)(2,1)}, u32[]{:S(2)}) copy-start(bf16[1,768,2560]{2,1,0:T(8,128)(2,1)} %param.23) | copy-start | bytes 11796484
  275.5 68.7 %all-to-all-start.1 = ((bf16[128,8,2560]{2,1,0:T(8,128)(2,1)}), bf16[128,8,2560]{2,1,0:T(8,128)(2,1)}, u32[]{:S(2)}, u32[]{:S(2)}) async-start(bf16[128,8,2560]{2,1,0:T(8,128)(2,1)} %fusion.18), calls=%async_computation.1 | async-start | bytes 10485760 | tf_op jit(solution)/shard_map/all_to_all | solution.py:228
  282.1 7.5 %copy-start.4 = (bf16[1,2560,768]{2,1,0:T(8,128)(2,1)S(1)}, bf16[1,2560,768]{2,1,0:T(8,128)(2,1)}, u32[]{:S(2)}) copy-start(bf16[1,2560,768]{2,1,0:T(8,128)(2,1)} %param.21) | copy-start | bytes 11796484
  289.6 7.2 %copy-start.6 = (bf16[1,768,2560]{2,1,0:T(8,128)(2,1)S(1)}, bf16[1,768,2560]{2,1,0:T(8,128)(2,1)}, u32[]{:S(2)}) copy-start(bf16[1,768,2560]{2,1,0:T(8,128)(2,1)} %param.23) | copy-start | bytes 11796484
  344.2 68.7 %all-to-all-start.3 = ((bf16[128,8,2560]{2,1,0:T(8,128)(2,1)}), bf16[128,8,2560]{2,1,0:T(8,128)(2,1)}, u32[]{:S(2)}, u32[]{:S(2)}) async-start(bf16[128,8,2560]{2,1,0:T(8,128)(2,1)} %fusion.19), calls=%async_computation.3 | async-start | bytes 10485760 | tf_op jit(solution)/shard_map/all_to_all | solution.py:228
Sparse Core Ops, SparseCore 0:
  9.1 47.3 all-gather.2
  58.5 43.7 all-gather.4

commit v5 on v4

--- a/solution.py
+++ b/solution.py
@@ -150,10 +150,12 @@
     req_of = jnp.sum((positions[:, None] >= ends[None, :]).astype(jnp.int32), axis=1)
     pick = req_of[:, None] == jnp.arange(lens.shape[0], dtype=jnp.int32)[None, :]
     first = jnp.sum(jnp.where(pick, starts[None, :], 0), axis=1)
-    pool_rows = lax.all_gather(page_pool, "req", axis=0, tiled=True).reshape(
-        pool_all * PAGE_TOKENS, 2 * row_width
-    )
-    pool_rows, suffix_after = lax.optimization_barrier((pool_rows, suffix_kv))
+    split = (pool_per_shard + 1) // 2
+    pool_first = lax.all_gather(page_pool[:split], "req", axis=0, tiled=True)
+    pool_first, pool_later, suffix_after = lax.optimization_barrier(
+        (pool_first, page_pool[split:], suffix_kv)
+    )
+    pool_second = lax.all_gather(pool_later, "req", axis=0, tiled=True)
     segment = lax.all_gather(suffix_after, "exp", axis=0, tiled=True)
     counts = jnp.sum(
         (page_table[0][:, :, None] == jnp.arange(pool_all, dtype=jnp.int32)[None, None, :]).astype(
@@ -164,8 +166,25 @@
     query_counts = jnp.dot(pick.astype(jnp.float32), counts, precision=lax.Precision.HIGHEST)
     keypos = jnp.arange(segment.shape[0], dtype=jnp.int32)
     suffix_weights = (keypos[None, :] <= positions[:, None]) & (keypos[None, :] >= first[:, None])
-    pool_weights = jnp.repeat(query_counts, PAGE_TOKENS, axis=1).astype(jnp.bfloat16)
-    carry = flash(queries, pool_weights, pool_rows, None, True, False, KEY_VALUE_HEADS, HEAD_SIZE)
+    shard_counts = query_counts.reshape(token_index, request_count, pool_per_shard)
+    carry = None
+    for pages, rows in (
+        (shard_counts[:, :, :split], pool_first),
+        (shard_counts[:, :, split:], pool_second),
+    ):
+        page_weights = jnp.repeat(
+            pages.reshape(token_index, -1), PAGE_TOKENS, axis=1
+        ).astype(jnp.bfloat16)
+        carry = flash(
+            queries,
+            page_weights,
+            rows.reshape(-1, 2 * row_width),
+            carry,
+            carry is None,
+            False,
+            KEY_VALUE_HEADS,
+            HEAD_SIZE,
+        )
     attended = flash(
         queries,
         suffix_weights.astype(jnp.bfloat16),

time: 431 us -> 433 us (level)
  Pallas kernels: 56.4 us -> 62.6 us
  waiting for transfers between devices: 245 us -> 239 us
  local copies, waits for them, and re-layouts: 4.93 us -> 9.89 us
    all_gather x1 -> x2, waiting for transfers between devices: 49.1 us -> 32.9 us  [the longest x1 32.9 us: on_device(): pool_first = lax.all_gather(page_pool[:split], 'req', axis=0, tiled=True)]
    all_gather x1, waiting for transfers between devices: 0.01 us -> 9.97 us  [on_device(): segment = lax.all_gather(suffix_after, 'exp', axis=0, tiled=True)]
    pallas_call x2 -> x3, Pallas kernels: 56.4 us -> 62.6 us  [flash(): pl.pallas_call(kern, grid_spec=grid_spec, out_shape=out_shape)]
  transfers between devices with their start and end apart: 6 -> 7, of which waited for: 5 -> 6; matrix products, arithmetic and copies ran while one was open for 15% -> 16% of each run, Pallas kernels for 11% -> 12%
where the time goes in v5:
time: 433 us; the launch traced here: 430 us
  waiting for transfers between devices  239 us (55%)
  matrix products  68.3 us (16%)
  Pallas kernels  62.6 us (14%)
  starting transfers between devices  29.6 us (7%)
  between operations  13.4 us (3%)
  local copies, waits for them, and re-layouts  9.89 us (2%)
  other arithmetic  7.39 us (2%)
    all_to_all x2, waiting for transfers between devices, on_device(): lax.all_to_all(outgoing, ('req', 'exp'), split_axis=0, concat_axis=0, til...  99.7 us
    all_to_all x2, waiting for transfers between devices, on_device(): lax.all_to_all(jnp.dot(inner, w_down[0], preferred_element_type=jnp.float...  95.8 us
    pallas_call x3, Pallas kernels, flash(): pl.pallas_call(kern, grid_spec=grid_spec, out_shape=out_shape)  62.6 us
    all_gather x1, waiting for transfers between devices, on_device(): pool_first = lax.all_gather(page_pool[:split], 'req', axis=0, tiled=True)  32.9 us
    all_to_all x2, starting transfers between devices, on_device(): lax.all_to_all(outgoing, ('req', 'exp'), split_axis=0, concat_axis=0, til...  16.4 us
    dot_general x2, matrix products, on_device(): up_part = jnp.dot(flat_rows, w_up[0], preferred_element_type=jnp.float32)  14.9 us
    dot_general x2, matrix products, on_device(): jnp.dot(flat_rows, w_gate[0], preferred_element_type=jnp.float32)  14.4 us
    all_to_all x2, starting transfers between devices, on_device(): lax.all_to_all(jnp.dot(inner, w_down[0], preferred_element_type=jnp.float...  13.1 us
  transfers between devices with their start and end apart: 7, of which 6 were waited for; matrix products, arithmetic and copies ran while one was open for 16% of the time, Pallas kernels for 12%

profile of v5, /device:TPU:34, one launch (start us, length us, event | category | flops | bytes accessed | tf_op | source)
XLA Modules:
  0.0 430.3 jit_solution(17568224205432573373)
XLA Ops:
  6.5 1.9 slice.26
  8.5 1.8 slice.27
  10.3 32.9 %all-gather.4.cloned.1.call-done = bf16[32,128,512]{2,1,0:T(8,128)(2,1)} async-done(((bf16[4,128,512]{2,1,0:T(8,128)(2,1)}), bf16[32,128,512]{2,1,0:T(8,128)(2,1)}) %all-gather.4.cloned.1.call-update) | async-done | bytes 4194320 | tf_op jit(solution)/shard_map/all_gather | solution.py:154
  43.3 0.7 all-gather.6.cloned.1.call-update
  44.0 0.8 convert_reduce_fusion
  45.0 0.8 reduce-window.4
  45.9 0.2 fusion.62
  46.3 0.6 broadcast_reduce_fusion.1
  46.9 0.5 broadcast_in_dim.67
  47.4 1.0 copy.41
  48.6 0.7 broadcast_reduce_fusion
  49.6 0.6 broadcast_in_dim.104
  50.3 1.4 copy.40
  51.8 0.3 fusion.54
  52.1 0.6 compare_convert_fusion.2.flags_ref
  52.7 0.6 compare_convert_fusion.1.flags_ref
  53.3 0.6 compare_convert_fusion.flags_ref
  53.9 0.1 convolution_convert_fusion.4
  54.2 1.3 fusion.53.w_ref
  55.4 0.9 broadcast_8_m_in_l_in.2.m_in.l_in
  56.3 0.9 broadcast_in_dim.105.acc_in
  57.2 28.0 %shard_map.118 = (f32[2,640,1]{2,1,0:T(8,128)}, f32[2,640,1]{2,1,0:T(8,128)}, f32[2,640,128]{2,1,0:T(8,128)}) custom-call(s32[8]{0:T(128)} %compare_convert_fusion.flags_ref, bf16[128,1280]{1,0:T(8,128)(2,1)} %q_ref.5, bf16[128,4096]{1,0:T(8,128)(2,1)} %bitcast.116, bf16[4096,512]{1,0:T(8,128)(2,1)} %bitcast.114, ...), custom_call_target="tpu_custom_call" | custom-call | tf_op jit(solution)/shard_map/pallas_call | solution.py:122
  85.3 23.4 %shard_map.119 = (f32[2,640,1]{2,1,0:T(8,128)}, f32[2,640,1]{2,1,0:T(8,128)}, f32[2,640,128]{2,1,0:T(8,128)}) custom-call(s32[6]{0:T(128)} %compare_convert_fusion.1.flags_ref, bf16[128,1280]{1,0:T(8,128)(2,1)} %q_ref.5, bf16[128,3072]{1,0:T(8,128)(2,1)} %bitcast.117, bf16[3072,512]{1,0:T(8,128)(2,1)} %bitcast.118, f32[2,640,1]{2,1,0:T(8,128)} %get-tuple-element.17.m_in, ...), custom_call_target="tpu_custom_call" | custom-call | tf_op jit(solution)/shard_map/pallas_call | solution.py:122
  108.6 10.0 %all-gather.6.cloned.1.call-done.kv_ref = bf16[2048,512]{1,0:T(8,128)(2,1)} async-done(((bf16[128,512]{1,0:T(8,128)(2,1)}), bf16[2048,512]{1,0:T(8,128)(2,1)}) %all-gather.6.cloned.1.call-update) | async-done | bytes 2097168 | tf_op jit(solution)/shard_map/all_gather | solution.py:159
  118.6 11.2 %shard_map.120 = bf16[128,1280]{1,0:T(8,128)(2,1)} custom-call(s32[4]{0:T(128)} %compare_convert_fusion.2.flags_ref, bf16[128,1280]{1,0:T(8,128)(2,1)} %q_ref.5, bf16[128,2048]{1,0:T(8,128)(2,1)} %fusion.53.w_ref, bf16[2048,512]{1,0:T(8,128)(2,1)} %all-gather.6.cloned.1.call-done.kv_ref, f32[2,640,1]{2,1,0:T(8,128)} %get-tuple-element.20.m_in, ...), custom_call_target="tpu_custom_call" | custom-call | tf_op jit(solution)/shard_map/pallas_call | solution.py:122
  129.8 4.0 fusion.38
  133.8 0.2 fusion.50
  134.1 3.9 fusion.16
  138.1 9.8 %all-to-all-start = ((bf16[128,8,2560]{2,1,0:T(8,128)(2,1)}), bf16[128,8,2560]{2,1,0:T(8,128)(2,1)}, u32[]{:S(2)}, u32[]{:S(2)}) async-start(bf16[128,8,2560]{2,1,0:T(8,128)(2,1)} %fusion.16), calls=%async_computation | async-start | bytes 10485760 | tf_op jit(solution)/shard_map/all_to_all | solution.py:242
  147.9 3.9 fusion.17
  151.8 58.2 %all-to-all-done = bf16[128,8,2560]{2,1,0:T(8,128)(2,1)} async-done(((bf16[128,8,2560]{2,1,0:T(8,128)(2,1)}), bf16[128,8,2560]{2,1,0:T(8,128)(2,1)}, u32[]{:S(2)}, u32[]{:S(2)}) %all-to-all-start) | async-done | bytes 5242912 | tf_op jit(solution)/shard_map/all_to_all | solution.py:242
  210.0 6.6 %all-to-all-start.2 = ((bf16[128,8,2560]{2,1,0:T(8,128)(2,1)}), bf16[128,8,2560]{2,1,0:T(8,128)(2,1)}, u32[]{:S(2)}, u32[]{:S(2)}) async-start(bf16[128,8,2560]{2,1,0:T(8,128)(2,1)} %fusion.17), calls=%async_computation.2 | async-start | bytes 10485760 | tf_op jit(solution)/shard_map/all_to_all | solution.py:242
  216.6 7.5 %fusion.12 = f32[1024,768]{1,0:T(8,128)S(1)} fusion(bf16[128,8,2560]{2,1,0:T(8,128)(2,1)} %all-to-all-done, bf16[1,2560,768]{2,1,0:T(8,128)(2,1)} %param.22), kind=kOutput, calls=%fused_computation.16 | convolution fusion | flops 4026531840 | bytes 12320768 | tf_op jit(solution)/shard_map/dot_general | solution.py:245
  224.1 7.2 %multiply_convert_fusion.1 = bf16[1024,768]{1,0:T(8,128)(2,1)S(1)} fusion(f32[1024,768]{1,0:T(8,128)S(1)} %fusion.12, bf16[1,2560,768]{2,1,0:T(8,128)(2,1)S(1)} %copy-done.3, bf16[128,8,2560]{2,1,0:T(8,128)(2,1)} %all-to-all-done), kind=kOutput, calls=%fused_computation.38 | convolution fusion | flops 4031250432 | bytes 13893632 | tf_op jit(solution)/shard_map/dot_general | solution.py:244
  231.3 6.0 %fusion.18 = bf16[128,8,2560]{2,1,0:T(8,128)(2,1)} fusion(bf16[1024,768]{1,0:T(8,128)(2,1)S(1)} %multiply_convert_fusion.1, bf16[1,768,2560]{2,1,0:T(8,128)(2,1)S(1)} %copy-done.5), kind=kOutput, calls=%fused_computation.22 | convolution fusion | flops 4029153280 | bytes 10747904 | tf_op jit(solution)/shard_map/dot_general | solution.py:248
  237.3 41.4 %all-to-all-done.2 = bf16[128,8,2560]{2,1,0:T(8,128)(2,1)} async-done(((bf16[128,8,2560]{2,1,0:T(8,128)(2,1)}), bf16[128,8,2560]{2,1,0:T(8,128)(2,1)}, u32[]{:S(2)}, u32[]{:S(2)}) %all-to-all-start.2) | async-done | bytes 5242912 | tf_op jit(solution)/shard_map/all_to_all | solution.py:242
  278.7 6.6 %all-to-all-start.1 = ((bf16[128,8,2560]{2,1,0:T(8,128)(2,1)}), bf16[128,8,2560]{2,1,0:T(8,128)(2,1)}, u32[]{:S(2)}, u32[]{:S(2)}) async-start(bf16[128,8,2560]{2,1,0:T(8,128)(2,1)} %fusion.18), calls=%async_computation.1 | async-start | bytes 10485760 | tf_op jit(solution)/shard_map/all_to_all | solution.py:247
  285.3 7.5 %fusion.4 = f32[1024,768]{1,0:T(8,128)S(1)} fusion(bf16[128,8,2560]{2,1,0:T(8,128)(2,1)} %all-to-all-done.2, bf16[1,2560,768]{2,1,0:T(8,128)(2,1)} %param.22), kind=kOutput, calls=%fused_computation.8 | convolution fusion | flops 4026531840 | bytes 12320768 | tf_op jit(solution)/shard_map/dot_general | solution.py:245
  292.8 7.2 %multiply_convert_fusion = bf16[1024,768]{1,0:T(8,128)(2,1)S(1)} fusion(f32[1024,768]{1,0:T(8,128)S(1)} %fusion.4, bf16[1,2560,768]{2,1,0:T(8,128)(2,1)S(1)} %copy-done.4, bf16[128,8,2560]{2,1,0:T(8,128)(2,1)} %all-to-all-done.2), kind=kOutput, calls=%fused_computation.37 | convolution fusion | flops 4031250432 | bytes 13893632 | tf_op jit(solution)/shard_map/dot_general | solution.py:244
  300.0 6.0 %fusion.19 = bf16[128,8,2560]{2,1,0:T(8,128)(2,1)} fusion(bf16[1024,768]{1,0:T(8,128)(2,1)S(1)} %multiply_convert_fusion, bf16[1,768,2560]{2,1,0:T(8,128)(2,1)S(1)} %copy-done.6), kind=kOutput, calls=%fused_computation.23 | convolution fusion | flops 4029153280 | bytes 10747904 | tf_op jit(solution)/shard_map/dot_general | solution.py:248
  306.0 41.4 %all-to-all-done.1 = bf16[128,8,2560]{2,1,0:T(8,128)(2,1)} async-done(((bf16[128,8,2560]{2,1,0:T(8,128)(2,1)}), bf16[128,8,2560]{2,1,0:T(8,128)(2,1)}, u32[]{:S(2)}, u32[]{:S(2)}) %all-to-all-start.1) | async-done | bytes 5242912 | tf_op jit(solution)/shard_map/all_to_all | solution.py:247
  347.4 6.5 %all-to-all-start.3 = ((bf16[128,8,2560]{2,1,0:T(8,128)(2,1)}), bf16[128,8,2560]{2,1,0:T(8,128)(2,1)}, u32[]{:S(2)}, u32[]{:S(2)}) async-start(bf16[128,8,2560]{2,1,0:T(8,128)(2,1)} %fusion.19), calls=%async_computation.3 | async-start | bytes 10485760 | tf_op jit(solution)/shard_map/all_to_all | solution.py:247
  354.0 0.4 fusion.69
  354.8 3.4 fusion.26
  358.2 3.4 fusion.29
  361.6 54.5 %all-to-all-done.3 = bf16[128,8,2560]{2,1,0:T(8,128)(2,1)} async-done(((bf16[128,8,2560]{2,1,0:T(8,128)(2,1)}), bf16[128,8,2560]{2,1,0:T(8,128)(2,1)}, u32[]{:S(2)}, u32[]{:S(2)}) %all-to-all-start.3) | async-done | bytes 5242912 | tf_op jit(solution)/shard_map/all_to_all | solution.py:247
  416.1 3.4 fusion.32
  419.6 4.2 fusion.39
  (56 shorter events, 1.9 us)
Async XLA Ops:
  6.5 347.4 %copy-start = (bf16[2560,64]{0,1:T(8,128)(2,1)S(1)}, bf16[2560,64]{0,1:T(8,128)(2,1)}, u32[]{:S(2)}) copy-start(bf16[2560,64]{0,1:T(8,128)(2,1)} %param.19) | copy-start | bytes 983044
  6.5 36.7 %all-gather.4.cloned.1.call-start = ((), (), s32[]{:S(2)}) async-start(), calls=%async_computation.4 | async-start | bytes 4718592 | tf_op jit(solution)/shard_map/all_gather | solution.py:154
  8.5 43.2 %copy-start.7 = (s32[1,4]{1,0:T(1,128)S(1)}, s32[1,4]{1,0:T(1,128)}, u32[]{:S(2)}) copy-start(s32[1,4]{1,0:T(1,128)} %param.15) | copy-start | bytes 52
  8.5 43.3 %copy-start.2 = (s32[128,6]{0,1:T(8,128)S(1)}, s32[128,6]{0,1:T(8,128)}, u32[]{:S(2)}) copy-start(s32[128,6]{0,1:T(8,128)} %param.20) | copy-start | bytes 9220
  8.5 76.8 %all-gather.8.cloned.1.call-start = ((), (), s32[]{:S(2)}) async-start(), calls=%async_computation.6 | async-start | bytes 3538944 | tf_op jit(solution)/shard_map/all_gather | solution.py:158
  43.3 75.3 %all-gather.6.cloned.1.call-start = ((), (), s32[]{:S(2)}) async-start(), calls=%async_computation.5 | async-start | bytes 2228224 | tf_op jit(solution)/shard_map/all_gather | solution.py:159
  108.6 21.2 %copy-start.1 = (bf16[128,2560]{1,0:T(8,128)(2,1)S(1)}, bf16[128,2560]{1,0:T(8,128)(2,1)}, u32[]{:S(2)}) copy-start(bf16[128,2560]{1,0:T(8,128)(2,1)} %param.12) | copy-start | bytes 1966084
  138.1 71.9 %all-to-all-start = ((bf16[128,8,2560]{2,1,0:T(8,128)(2,1)}), bf16[128,8,2560]{2,1,0:T(8,128)(2,1)}, u32[]{:S(2)}, u32[]{:S(2)}) async-start(bf16[128,8,2560]{2,1,0:T(8,128)(2,1)} %fusion.16), calls=%async_computation | async-start | bytes 10485760 | tf_op jit(solution)/shard_map/all_to_all | solution.py:242
  210.0 68.7 %all-to-all-start.2 = ((bf16[128,8,2560]{2,1,0:T(8,128)(2,1)}), bf16[128,8,2560]{2,1,0:T(8,128)(2,1)}, u32[]{:S(2)}, u32[]{:S(2)}) async-start(bf16[128,8,2560]{2,1,0:T(8,128)(2,1)} %fusion.17), calls=%async_computation.2 | async-start | bytes 10485760 | tf_op jit(solution)/shard_map/all_to_all | solution.py:242
  216.6 7.5 %copy-start.3 = (bf16[1,2560,768]{2,1,0:T(8,128)(2,1)S(1)}, bf16[1,2560,768]{2,1,0:T(8,128)(2,1)}, u32[]{:S(2)}) copy-start(bf16[1,2560,768]{2,1,0:T(8,128)(2,1)} %param.21) | copy-start | bytes 11796484
  224.1 7.2 %copy-start.5 = (bf16[1,768,2560]{2,1,0:T(8,128)(2,1)S(1)}, bf16[1,768,2560]{2,1,0:T(8,128)(2,1)}, u32[]{:S(2)}) copy-start(bf16[1,768,2560]{2,1,0:T(8,128)(2,1)} %param.23) | copy-start | bytes 11796484
  278.7 68.7 %all-to-all-start.1 = ((bf16[128,8,2560]{2,1,0:T(8,128)(2,1)}), bf16[128,8,2560]{2,1,0:T(8,128)(2,1)}, u32[]{:S(2)}, u32[]{:S(2)}) async-start(bf16[128,8,2560]{2,1,0:T(8,128)(2,1)} %fusion.18), calls=%async_computation.1 | async-start | bytes 10485760 | tf_op jit(solution)/shard_map/all_to_all | solution.py:247
  285.3 7.5 %copy-start.4 = (bf16[1,2560,768]{2,1,0:T(8,128)(2,1)S(1)}, bf16[1,2560,768]{2,1,0:T(8,128)(2,1)}, u32[]{:S(2)}) copy-start(bf16[1,2560,768]{2,1,0:T(8,128)(2,1)} %param.21) | copy-start | bytes 11796484
  292.8 7.2 %copy-start.6 = (bf16[1,768,2560]{2,1,0:T(8,128)(2,1)S(1)}, bf16[1,768,2560]{2,1,0:T(8,128)(2,1)}, u32[]{:S(2)}) copy-start(bf16[1,768,2560]{2,1,0:T(8,128)(2,1)} %param.23) | copy-start | bytes 11796484
  347.4 68.7 %all-to-all-start.3 = ((bf16[128,8,2560]{2,1,0:T(8,128)(2,1)}), bf16[128,8,2560]{2,1,0:T(8,128)(2,1)}, u32[]{:S(2)}, u32[]{:S(2)}) async-start(bf16[128,8,2560]{2,1,0:T(8,128)(2,1)} %fusion.19), calls=%async_computation.3 | async-start | bytes 10485760 | tf_op jit(solution)/shard_map/all_to_all | solution.py:247
Sparse Core Ops, SparseCore 0:
  9.1 34.1 all-gather.3
  44.9 27.7 all-gather.7
  74.9 43.6 all-gather.5

commit v6 on v5

--- a/solution.py
+++ b/solution.py
@@ -21,6 +21,7 @@
 
 
 KEY_BLOCK = 512
+GROUP_REACH = 1024
 
 
 def attn_kernel(flags_ref, q_ref, w_ref, kv_ref, m_in, l_in, acc_in, *refs, first_call, last_call, groups, reps, hs):
@@ -79,11 +80,11 @@
             acc_out[...] = acc_ref[...]
 
 
-def flash(queries, weights, kv_rows, carry, first_call, last_call, groups, hs):
+def flash(queries, weights, kv_rows, carry, first_call, last_call, groups, hs, key_block=KEY_BLOCK):
     t, width = queries.shape
     reps = width // hs // groups
-    n_blocks = kv_rows.shape[0] // KEY_BLOCK
-    flags = (jnp.max(weights.reshape(t, n_blocks, KEY_BLOCK), axis=(0, 2)) > 0).astype(jnp.int32)
+    n_blocks = kv_rows.shape[0] // key_block
+    flags = (jnp.max(weights.reshape(t, n_blocks, key_block), axis=(0, 2)) > 0).astype(jnp.int32)
     kern = functools.partial(attn_kernel, first_call=first_call, last_call=last_call,
                              groups=groups, reps=reps, hs=hs)
     state = [
@@ -106,8 +107,8 @@
         grid=(n_blocks,),
         in_specs=[
             pl.BlockSpec((t, width), lambda j, f: (0, 0)),
-            pl.BlockSpec((t, KEY_BLOCK), lambda j, f: (0, j)),
-            pl.BlockSpec((KEY_BLOCK, kv_rows.shape[1]), lambda j, f: (j, 0)),
+            pl.BlockSpec((t, key_block), lambda j, f: (0, j)),
+            pl.BlockSpec((key_block, kv_rows.shape[1]), lambda j, f: (j, 0)),
         ] + state_specs,
         out_specs=out_specs,
         scratch_shapes=[
@@ -152,11 +153,21 @@
     first = jnp.sum(jnp.where(pick, starts[None, :], 0), axis=1)
     split = (pool_per_shard + 1) // 2
     pool_first = lax.all_gather(page_pool[:split], "req", axis=0, tiled=True)
-    pool_first, pool_later, suffix_after = lax.optimization_barrier(
-        (pool_first, page_pool[split:], suffix_kv)
-    )
+    pool_first, pool_later = lax.optimization_barrier((pool_first, page_pool[split:]))
     pool_second = lax.all_gather(pool_later, "req", axis=0, tiled=True)
-    segment = lax.all_gather(suffix_after, "exp", axis=0, tiled=True)
+    exp_count = lax.axis_size("exp")
+    reach = min(exp_count - 1, (GROUP_REACH + token_index - 2) // token_index)
+    segment = jnp.concatenate(
+        [
+            lax.ppermute(
+                suffix_kv, "exp", [(s, (s + k) % exp_count) for s in range(exp_count)]
+            )
+            for k in range(reach, 0, -1)
+        ]
+        + [suffix_kv],
+        axis=0,
+    )
+    source_block = (lax.axis_index("exp") - jnp.arange(reach, -1, -1, dtype=jnp.int32)) % exp_count
     counts = jnp.sum(
         (page_table[0][:, :, None] == jnp.arange(pool_all, dtype=jnp.int32)[None, None, :]).astype(
             jnp.float32
@@ -164,7 +175,9 @@
         axis=1,
     )
     query_counts = jnp.dot(pick.astype(jnp.float32), counts, precision=lax.Precision.HIGHEST)
-    keypos = jnp.arange(segment.shape[0], dtype=jnp.int32)
+    keypos = (
+        source_block[:, None] * token_index + jnp.arange(token_index, dtype=jnp.int32)[None, :]
+    ).reshape(-1)
     suffix_weights = (keypos[None, :] <= positions[:, None]) & (keypos[None, :] >= first[:, None])
     shard_counts = query_counts.reshape(token_index, request_count, pool_per_shard)
     carry = None
@@ -194,6 +207,7 @@
         True,
         KEY_VALUE_HEADS,
         HEAD_SIZE,
+        segment.shape[0] // 3,
     )
     projected = jnp.dot(attended, w_out, preferred_element_type=jnp.float32)
     resid = lax.optimization_barrier((hidden.astype(jnp.float32) + projected).astype(jnp.bfloat16))

time: 433 us -> 449 us (1.037); the launches traced: 430 us -> 441 us
  starting transfers between devices: 29.6 us -> 52.1 us
  waiting for transfers between devices: 239 us -> 232 us
  Pallas kernels: 62.6 us -> 57 us
    ppermute x0 -> x8, starting transfers between devices: none -> 16.1 us  [on_device(): lax.ppermute(suffix_kv, 'exp', [(s, (s + k) % exp_count) for s in range(e...]
    all_gather x1 -> x0, waiting for transfers between devices: 9.97 us -> none  [on_device(): segment = lax.all_gather(suffix_after, 'exp', axis=0, tiled=True)]
    all_to_all x2, starting transfers between devices: 16.4 us -> 22.2 us  [on_device(): lax.all_to_all(outgoing, ('req', 'exp'), split_axis=0, concat_axis=0, til...]
    pallas_call x3, Pallas kernels: 62.6 us -> 57 us  [flash(): pl.pallas_call(kern, grid_spec=grid_spec, out_shape=out_shape)]
  transfers between devices with their start and end apart: 7 -> 14, of which waited for: 6 -> 7; matrix products, arithmetic and copies ran while one was open for 16% -> 15% of each run, Pallas kernels for 12% -> 6%
where the time goes in v6:
time: 449 us; the launch traced here: 441 us
  waiting for transfers between devices  232 us (52%)
  matrix products  68.3 us (15%)
  Pallas kernels  57 us (13%)
  starting transfers between devices  52.1 us (12%)
  between operations  14.3 us (3%)
  local copies, waits for them, and re-layouts  10.2 us (2%)
  other arithmetic  6.84 us (2%)
    all_to_all x2, waiting for transfers between devices, on_device(): lax.all_to_all(outgoing, ('req', 'exp'), split_axis=0, concat_axis=0, til...  99.6 us
    all_to_all x2, waiting for transfers between devices, on_device(): lax.all_to_all(jnp.dot(inner, w_down[0], preferred_element_type=jnp.float...  95.6 us
    pallas_call x3, Pallas kernels, flash(): pl.pallas_call(kern, grid_spec=grid_spec, out_shape=out_shape)  57 us
    all_gather x1, waiting for transfers between devices, on_device(): pool_first = lax.all_gather(page_pool[:split], 'req', axis=0, tiled=True)  32.9 us
    all_to_all x2, starting transfers between devices, on_device(): lax.all_to_all(outgoing, ('req', 'exp'), split_axis=0, concat_axis=0, til...  22.2 us
    ppermute x8, starting transfers between devices, on_device(): lax.ppermute(suffix_kv, 'exp', [(s, (s + k) % exp_count) for s in range(e...  16.1 us
    dot_general x2, matrix products, on_device(): up_part = jnp.dot(flat_rows, w_up[0], preferred_element_type=jnp.float32)  14.9 us
    dot_general x2, matrix products, on_device(): jnp.dot(flat_rows, w_gate[0], preferred_element_type=jnp.float32)  14.4 us
  transfers between devices with their start and end apart: 14, of which 7 were waited for; matrix products, arithmetic and copies ran while one was open for 15% of the time, Pallas kernels for 6%

profile of v6, /device:TPU:34, one launch (start us, length us, event | category | flops | bytes accessed | tf_op | source)
XLA Modules:
  0.0 441.0 jit_solution(17178906820094131383)
XLA Ops:
  6.5 1.9 slice.27
  8.5 1.8 slice.28
  10.3 32.9 %all-gather.3.cloned.1.call-done = bf16[32,128,512]{2,1,0:T(8,128)(2,1)} async-done(((bf16[4,128,512]{2,1,0:T(8,128)(2,1)}), bf16[32,128,512]{2,1,0:T(8,128)(2,1)}) %all-gather.3.cloned.1.call-update) | async-done | bytes 4194320 | tf_op jit(solution)/shard_map/all_gather | solution.py:155
  43.3 2.3 collective-permute-start
  45.6 1.3 collective-permute-start.1
  46.9 3.4 collective-permute-start.2
  50.2 1.9 collective-permute-start.3
  52.4 0.8 convert_reduce_fusion
  53.4 0.8 reduce-window.4
  54.7 0.6 broadcast_reduce_fusion.1
  55.5 0.7 broadcast_reduce_fusion
  57.1 0.5 compare_convert_fusion.2.flags_ref
  57.6 0.5 compare_convert_fusion.1.flags_ref
  58.5 0.9 and_convert_fusion.w_ref
  60.3 1.0 copy.43
  61.4 0.6 broadcast_in_dim.104
  62.0 1.5 copy.42
  63.5 1.8 collective-permute-start.5
  65.3 2.8 collective-permute-start.6
  68.2 2.3 collective-permute-start.7
  70.6 2.5 collective-permute-done.6
  73.1 1.5 collective-permute-done.7
  74.7 1.0 broadcast_13_m_in_l_in.2.m_in.l_in
  75.6 0.9 broadcast_in_dim.105.acc_in
  76.5 27.8 %shard_map.118 = (f32[2,640,1]{2,1,0:T(8,128)}, f32[2,640,1]{2,1,0:T(8,128)}, f32[2,640,128]{2,1,0:T(8,128)}) custom-call(s32[8]{0:T(128)} %compare_convert_fusion.flags_ref, bf16[128,1280]{1,0:T(8,128)(2,1)} %q_ref.5, bf16[128,4096]{1,0:T(8,128)(2,1)} %bitcast.122, bf16[4096,512]{1,0:T(8,128)(2,1)} %bitcast.120, ...), custom_call_target="tpu_custom_call" | custom-call | tf_op jit(solution)/shard_map/pallas_call | solution.py:123
  104.4 21.3 %shard_map.119 = (f32[2,640,1]{2,1,0:T(8,128)}, f32[2,640,1]{2,1,0:T(8,128)}, f32[2,640,128]{2,1,0:T(8,128)}) custom-call(s32[6]{0:T(128)} %compare_convert_fusion.1.flags_ref, bf16[128,1280]{1,0:T(8,128)(2,1)} %q_ref.5, bf16[128,3072]{1,0:T(8,128)(2,1)} %bitcast.123, bf16[3072,512]{1,0:T(8,128)(2,1)} %bitcast.124, f32[2,640,1]{2,1,0:T(8,128)} %get-tuple-element.15.m_in, ...), custom_call_target="tpu_custom_call" | custom-call | tf_op jit(solution)/shard_map/pallas_call | solution.py:123
  125.6 7.9 %shard_map.120 = bf16[128,1280]{1,0:T(8,128)(2,1)} custom-call(s32[3]{0:T(128)} %compare_convert_fusion.2.flags_ref, bf16[128,1280]{1,0:T(8,128)(2,1)} %q_ref.5, bf16[128,1152]{1,0:T(8,128)(2,1)} %and_convert_fusion.w_ref, bf16[1152,512]{1,0:T(8,128)(2,1)} %copy-done.1, f32[2,640,1]{2,1,0:T(8,128)} %get-tuple-element.18.m_in, ...), custom_call_target="tpu_custom_call" | custom-call | tf_op jit(solution)/shard_map/pallas_call | solution.py:123
  133.6 4.0 fusion.38
  137.9 3.9 fusion.16
  141.8 15.6 %all-to-all-start = ((bf16[128,8,2560]{2,1,0:T(8,128)(2,1)}), bf16[128,8,2560]{2,1,0:T(8,128)(2,1)}, u32[]{:S(2)}, u32[]{:S(2)}) async-start(bf16[128,8,2560]{2,1,0:T(8,128)(2,1)} %fusion.16), calls=%async_computation | async-start | bytes 10485760 | tf_op jit(solution)/shard_map/all_to_all | solution.py:256
  157.5 3.9 fusion.17
  161.4 58.2 %all-to-all-done = bf16[128,8,2560]{2,1,0:T(8,128)(2,1)} async-done(((bf16[128,8,2560]{2,1,0:T(8,128)(2,1)}), bf16[128,8,2560]{2,1,0:T(8,128)(2,1)}, u32[]{:S(2)}, u32[]{:S(2)}) %all-to-all-start) | async-done | bytes 5242912 | tf_op jit(solution)/shard_map/all_to_all | solution.py:256
  219.6 6.6 %all-to-all-start.2 = ((bf16[128,8,2560]{2,1,0:T(8,128)(2,1)}), bf16[128,8,2560]{2,1,0:T(8,128)(2,1)}, u32[]{:S(2)}, u32[]{:S(2)}) async-start(bf16[128,8,2560]{2,1,0:T(8,128)(2,1)} %fusion.17), calls=%async_computation.2 | async-start | bytes 10485760 | tf_op jit(solution)/shard_map/all_to_all | solution.py:256
  226.2 7.5 %fusion.12 = f32[1024,768]{1,0:T(8,128)S(1)} fusion(bf16[128,8,2560]{2,1,0:T(8,128)(2,1)} %all-to-all-done, bf16[1,2560,768]{2,1,0:T(8,128)(2,1)} %param.22), kind=kOutput, calls=%fused_computation.16 | convolution fusion | flops 4026531840 | bytes 12320768 | tf_op jit(solution)/shard_map/dot_general | solution.py:259
  233.7 7.2 %multiply_convert_fusion.1 = bf16[1024,768]{1,0:T(8,128)(2,1)S(1)} fusion(f32[1024,768]{1,0:T(8,128)S(1)} %fusion.12, bf16[1,2560,768]{2,1,0:T(8,128)(2,1)S(1)} %copy-done.5, bf16[128,8,2560]{2,1,0:T(8,128)(2,1)} %all-to-all-done), kind=kOutput, calls=%fused_computation.38 | convolution fusion | flops 4031250432 | bytes 13893632 | tf_op jit(solution)/shard_map/dot_general | solution.py:258
  240.9 6.0 %fusion.18 = bf16[128,8,2560]{2,1,0:T(8,128)(2,1)} fusion(bf16[1024,768]{1,0:T(8,128)(2,1)S(1)} %multiply_convert_fusion.1, bf16[1,768,2560]{2,1,0:T(8,128)(2,1)S(1)} %copy-done.7), kind=kOutput, calls=%fused_computation.22 | convolution fusion | flops 4029153280 | bytes 10747904 | tf_op jit(solution)/shard_map/dot_general | solution.py:262
  246.9 41.4 %all-to-all-done.2 = bf16[128,8,2560]{2,1,0:T(8,128)(2,1)} async-done(((bf16[128,8,2560]{2,1,0:T(8,128)(2,1)}), bf16[128,8,2560]{2,1,0:T(8,128)(2,1)}, u32[]{:S(2)}, u32[]{:S(2)}) %all-to-all-start.2) | async-done | bytes 5242912 | tf_op jit(solution)/shard_map/all_to_all | solution.py:256
  288.3 7.0 %all-to-all-start.1 = ((bf16[128,8,2560]{2,1,0:T(8,128)(2,1)}), bf16[128,8,2560]{2,1,0:T(8,128)(2,1)}, u32[]{:S(2)}, u32[]{:S(2)}) async-start(bf16[128,8,2560]{2,1,0:T(8,128)(2,1)} %fusion.18), calls=%async_computation.1 | async-start | bytes 10485760 | tf_op jit(solution)/shard_map/all_to_all | solution.py:261
  295.3 7.5 %fusion.4 = f32[1024,768]{1,0:T(8,128)S(1)} fusion(bf16[128,8,2560]{2,1,0:T(8,128)(2,1)} %all-to-all-done.2, bf16[1,2560,768]{2,1,0:T(8,128)(2,1)} %param.22), kind=kOutput, calls=%fused_computation.8 | convolution fusion | flops 4026531840 | bytes 12320768 | tf_op jit(solution)/shard_map/dot_general | solution.py:259
  302.8 7.2 %multiply_convert_fusion = bf16[1024,768]{1,0:T(8,128)(2,1)S(1)} fusion(f32[1024,768]{1,0:T(8,128)S(1)} %fusion.4, bf16[1,2560,768]{2,1,0:T(8,128)(2,1)S(1)} %copy-done.6, bf16[128,8,2560]{2,1,0:T(8,128)(2,1)} %all-to-all-done.2), kind=kOutput, calls=%fused_computation.37 | convolution fusion | flops 4031250432 | bytes 13893632 | tf_op jit(solution)/shard_map/dot_general | solution.py:258
  310.1 6.0 %fusion.19 = bf16[128,8,2560]{2,1,0:T(8,128)(2,1)} fusion(bf16[1024,768]{1,0:T(8,128)(2,1)S(1)} %multiply_convert_fusion, bf16[1,768,2560]{2,1,0:T(8,128)(2,1)S(1)} %copy-done.8), kind=kOutput, calls=%fused_computation.23 | convolution fusion | flops 4029153280 | bytes 10747904 | tf_op jit(solution)/shard_map/dot_general | solution.py:262
  316.1 41.1 %all-to-all-done.1 = bf16[128,8,2560]{2,1,0:T(8,128)(2,1)} async-done(((bf16[128,8,2560]{2,1,0:T(8,128)(2,1)}), bf16[128,8,2560]{2,1,0:T(8,128)(2,1)}, u32[]{:S(2)}, u32[]{:S(2)}) %all-to-all-start.1) | async-done | bytes 5242912 | tf_op jit(solution)/shard_map/all_to_all | solution.py:261
  357.2 6.7 %all-to-all-start.3 = ((bf16[128,8,2560]{2,1,0:T(8,128)(2,1)}), bf16[128,8,2560]{2,1,0:T(8,128)(2,1)}, u32[]{:S(2)}, u32[]{:S(2)}) async-start(bf16[128,8,2560]{2,1,0:T(8,128)(2,1)} %fusion.19), calls=%async_computation.3 | async-start | bytes 10485760 | tf_op jit(solution)/shard_map/all_to_all | solution.py:261
  364.7 3.4 fusion.26
  368.1 3.4 fusion.29
  371.5 54.5 %all-to-all-done.3 = bf16[128,8,2560]{2,1,0:T(8,128)(2,1)} async-done(((bf16[128,8,2560]{2,1,0:T(8,128)(2,1)}), bf16[128,8,2560]{2,1,0:T(8,128)(2,1)}, u32[]{:S(2)}, u32[]{:S(2)}) %all-to-all-start.3) | async-done | bytes 5242912 | tf_op jit(solution)/shard_map/all_to_all | solution.py:261
  426.1 3.4 fusion.32
  429.5 4.2 fusion.39
  (88 shorter events, 4.7 us)
Async XLA Ops:
  6.5 357.4 %copy-start = (bf16[2560,64]{0,1:T(8,128)(2,1)S(1)}, bf16[2560,64]{0,1:T(8,128)(2,1)}, u32[]{:S(2)}) copy-start(bf16[2560,64]{0,1:T(8,128)(2,1)} %param.19) | copy-start | bytes 983044
  6.5 50.1 %copy-start.9 = (s32[1,4]{1,0:T(1,128)S(1)}, s32[1,4]{1,0:T(1,128)}, u32[]{:S(2)}) copy-start(s32[1,4]{1,0:T(1,128)} %param.15) | copy-start | bytes 52
  6.5 50.2 %copy-start.4 = (s32[128,6]{0,1:T(8,128)S(1)}, s32[128,6]{0,1:T(8,128)}, u32[]{:S(2)}) copy-start(s32[128,6]{0,1:T(8,128)} %param.20) | copy-start | bytes 9220
  6.5 36.7 %all-gather.3.cloned.1.call-start = ((), (), s32[]{:S(2)}) async-start(), calls=%async_computation.4 | async-start | bytes 4718592 | tf_op jit(solution)/shard_map/all_gather | solution.py:155
  8.5 95.9 %all-gather.5.cloned.1.call-start = ((), (), s32[]{:S(2)}) async-start(), calls=%async_computation.5 | async-start | bytes 3538944 | tf_op jit(solution)/shard_map/all_gather | solution.py:157
  43.3 20.2 %collective-permute-start = (bf16[128,512]{1,0:T(8,128)(2,1)}, bf16[128,512]{1,0:T(8,128)(2,1)S(1)}, u32[]{:S(2)}, u32[]{:S(2)}) collective-permute-start(bf16[128,512]{1,0:T(8,128)(2,1)} %param.14), channel_id=1, source_target_pairs={{0,8},{1,9},{2,10},{3,11},{4,12},{5,13},{6,14},{7,15},{8,0},{9,1},... | collective-permute-start | bytes 393224 | tf_op jit(solution)/shard_map/ppermute | solution.py:162
  45.6 19.7 %collective-permute-start.1 = (bf16[128,512]{1,0:T(8,128)(2,1)}, bf16[128,512]{1,0:T(8,128)(2,1)S(1)}, u32[]{:S(2)}, u32[]{:S(2)}) collective-permute-start(bf16[128,512]{1,0:T(8,128)(2,1)} %param.14), channel_id=1, source_target_pairs={{0,7},{1,8},{2,9},{3,10},{4,11},{5,12},{6,13},{7,14},{8,15},{9,0},... | collective-permute-start | bytes 393224 | tf_op jit(solution)/shard_map/ppermute | solution.py:162
  46.9 21.3 %collective-permute-start.2 = (bf16[128,512]{1,0:T(8,128)(2,1)}, bf16[128,512]{1,0:T(8,128)(2,1)S(1)}, u32[]{:S(2)}, u32[]{:S(2)}) collective-permute-start(bf16[128,512]{1,0:T(8,128)(2,1)} %param.14), channel_id=1, source_target_pairs={{0,6},{1,7},{2,8},{3,9},{4,10},{5,11},{6,12},{7,13},{8,14},{9,15},... | collective-permute-start | bytes 393224 | tf_op jit(solution)/shard_map/ppermute | solution.py:162
  50.2 20.3 %collective-permute-start.3 = (bf16[128,512]{1,0:T(8,128)(2,1)}, bf16[128,512]{1,0:T(8,128)(2,1)S(1)}, u32[]{:S(2)}, u32[]{:S(2)}) collective-permute-start(bf16[128,512]{1,0:T(8,128)(2,1)} %param.14), channel_id=1, source_target_pairs={{0,5},{1,6},{2,7},{3,8},{4,9},{5,10},{6,11},{7,12},{8,13},{9,14},{... | collective-permute-start | bytes 393224 | tf_op jit(solution)/shard_map/ppermute | solution.py:162
  52.1 18.4 %collective-permute-start.4 = (bf16[128,512]{1,0:T(8,128)(2,1)}, bf16[128,512]{1,0:T(8,128)(2,1)S(1)}, u32[]{:S(2)}, u32[]{:S(2)}) collective-permute-start(bf16[128,512]{1,0:T(8,128)(2,1)} %param.14), channel_id=1, source_target_pairs={{0,4},{1,5},{2,6},{3,7},{4,8},{5,9},{6,10},{7,11},{8,12},{9,13},{1... | collective-permute-start | bytes 393224 | tf_op jit(solution)/shard_map/ppermute | solution.py:162
  55.4 8.1 %copy-start.3 = (bf16[128,512]{1,0:T(8,128)(2,1)S(1)}, bf16[128,512]{1,0:T(8,128)(2,1)}, u32[]{:S(2)}) copy-start(bf16[128,512]{1,0:T(8,128)(2,1)} %param.14) | copy-start | bytes 393220
  63.5 7.1 %collective-permute-start.5 = (bf16[128,512]{1,0:T(8,128)(2,1)S(1)}, bf16[128,512]{1,0:T(8,128)(2,1)S(1)}, u32[]{:S(2)}, u32[]{:S(2)}) collective-permute-start(bf16[128,512]{1,0:T(8,128)(2,1)S(1)} %copy-done.3), channel_id=1, source_target_pairs={{0,3},{1,4},{2,5},{3,6},{4,7},{5,8},{6,9},{7,10},{8,11},{9,12},{10... | collective-permute-start | bytes 393224 | tf_op jit(solution)/shard_map/ppermute | solution.py:162
  65.3 7.8 %collective-permute-start.6 = (bf16[128,512]{1,0:T(8,128)(2,1)S(1)}, bf16[128,512]{1,0:T(8,128)(2,1)S(1)}, u32[]{:S(2)}, u32[]{:S(2)}) collective-permute-start(bf16[128,512]{1,0:T(8,128)(2,1)S(1)} %copy-done.3), channel_id=1, source_target_pairs={{0,2},{1,3},{2,4},{3,5},{4,6},{5,7},{6,8},{7,9},{8,10},{9,11},{10,... | collective-permute-start | bytes 393224 | tf_op jit(solution)/shard_map/ppermute | solution.py:162
  68.2 6.4 %collective-permute-start.7 = (bf16[128,512]{1,0:T(8,128)(2,1)S(1)}, bf16[128,512]{1,0:T(8,128)(2,1)S(1)}, u32[]{:S(2)}, u32[]{:S(2)}) collective-permute-start(bf16[128,512]{1,0:T(8,128)(2,1)S(1)} %copy-done.3), channel_id=1, source_target_pairs={{0,1},{1,2},{2,3},{3,4},{4,5},{5,6},{6,7},{7,8},{8,9},{9,10},{10,1... | collective-permute-start | bytes 393224 | tf_op jit(solution)/shard_map/ppermute | solution.py:162
  74.6 29.7 %copy-start.1 = (bf16[1152,512]{1,0:T(8,128)(2,1)}, bf16[1152,512]{1,0:T(8,128)(2,1)S(1)}, u32[]{:S(2)}) copy-start(bf16[1152,512]{1,0:T(8,128)(2,1)S(1)} %constant_dynamic-update-slice_fusion.kv_ref) | copy-start | bytes 3538948
  125.6 7.9 %copy-start.2 = (bf16[128,2560]{1,0:T(8,128)(2,1)S(1)}, bf16[128,2560]{1,0:T(8,128)(2,1)}, u32[]{:S(2)}) copy-start(bf16[128,2560]{1,0:T(8,128)(2,1)} %param.12) | copy-start | bytes 1966084
  141.8 77.8 %all-to-all-start = ((bf16[128,8,2560]{2,1,0:T(8,128)(2,1)}), bf16[128,8,2560]{2,1,0:T(8,128)(2,1)}, u32[]{:S(2)}, u32[]{:S(2)}) async-start(bf16[128,8,2560]{2,1,0:T(8,128)(2,1)} %fusion.16), calls=%async_computation | async-start | bytes 10485760 | tf_op jit(solution)/shard_map/all_to_all | solution.py:256
  219.6 68.7 %all-to-all-start.2 = ((bf16[128,8,2560]{2,1,0:T(8,128)(2,1)}), bf16[128,8,2560]{2,1,0:T(8,128)(2,1)}, u32[]{:S(2)}, u32[]{:S(2)}) async-start(bf16[128,8,2560]{2,1,0:T(8,128)(2,1)} %fusion.17), calls=%async_computation.2 | async-start | bytes 10485760 | tf_op jit(solution)/shard_map/all_to_all | solution.py:256
  226.2 7.5 %copy-start.5 = (bf16[1,2560,768]{2,1,0:T(8,128)(2,1)S(1)}, bf16[1,2560,768]{2,1,0:T(8,128)(2,1)}, u32[]{:S(2)}) copy-start(bf16[1,2560,768]{2,1,0:T(8,128)(2,1)} %param.21) | copy-start | bytes 11796484
  233.7 7.2 %copy-start.7 = (bf16[1,768,2560]{2,1,0:T(8,128)(2,1)S(1)}, bf16[1,768,2560]{2,1,0:T(8,128)(2,1)}, u32[]{:S(2)}) copy-start(bf16[1,768,2560]{2,1,0:T(8,128)(2,1)} %param.23) | copy-start | bytes 11796484
  288.3 68.9 %all-to-all-start.1 = ((bf16[128,8,2560]{2,1,0:T(8,128)(2,1)}), bf16[128,8,2560]{2,1,0:T(8,128)(2,1)}, u32[]{:S(2)}, u32[]{:S(2)}) async-start(bf16[128,8,2560]{2,1,0:T(8,128)(2,1)} %fusion.18), calls=%async_computation.1 | async-start | bytes 10485760 | tf_op jit(solution)/shard_map/all_to_all | solution.py:261
  295.3 7.5 %copy-start.6 = (bf16[1,2560,768]{2,1,0:T(8,128)(2,1)S(1)}, bf16[1,2560,768]{2,1,0:T(8,128)(2,1)}, u32[]{:S(2)}) copy-start(bf16[1,2560,768]{2,1,0:T(8,128)(2,1)} %param.21) | copy-start | bytes 11796484
  302.8 7.2 %copy-start.8 = (bf16[1,768,2560]{2,1,0:T(8,128)(2,1)S(1)}, bf16[1,768,2560]{2,1,0:T(8,128)(2,1)}, u32[]{:S(2)}) copy-start(bf16[1,768,2560]{2,1,0:T(8,128)(2,1)} %param.23) | copy-start | bytes 11796484
  357.2 68.8 %all-to-all-start.3 = ((bf16[128,8,2560]{2,1,0:T(8,128)(2,1)}), bf16[128,8,2560]{2,1,0:T(8,128)(2,1)}, u32[]{:S(2)}, u32[]{:S(2)}) async-start(bf16[128,8,2560]{2,1,0:T(8,128)(2,1)} %fusion.19), calls=%async_computation.3 | async-start | bytes 10485760 | tf_op jit(solution)/shard_map/all_to_all | solution.py:261
Sparse Core Ops, SparseCore 0:
  9.1 34.1 all-gather.2
  44.9 27.6 all-gather.4

commit v7 on v4

--- a/solution.py
+++ b/solution.py
@@ -21,6 +21,7 @@
 
 
 KEY_BLOCK = 512
+LOG2_E = 1.4426950408889634
 
 
 def attn_kernel(flags_ref, q_ref, w_ref, kv_ref, m_in, l_in, acc_in, *refs, first_call, last_call, groups, reps, hs):
@@ -48,18 +49,17 @@
 
     @pl.when(flags_ref[j] > 0)
     def _():
-        w = w_ref[...].astype(jnp.float32)
-        live = (w > 0)[None]
+        bias = w_ref[...][None]
         for g in range(groups):
             k = kv_ref[:, g * hs:(g + 1) * hs]
             v = kv_ref[:, (groups + g) * hs:(groups + g + 1) * hs]
             s = lax.dot_general(qs[g], k, (((1,), (1,)), ((), ())),
-                                preferred_element_type=jnp.float32) * (1.0 / math.sqrt(hs))
-            s = jnp.where(live, s.reshape(reps, t, key_block), NEGATIVE_MASK)
+                                preferred_element_type=jnp.float32) * (LOG2_E / math.sqrt(hs))
+            s = s.reshape(reps, t, key_block) + bias
             m_old = m_ref[g].reshape(reps, t, 1)
             m_new = jnp.maximum(m_old, jnp.max(s, axis=-1, keepdims=True))
-            p = jnp.exp(s - m_new) * w[None]
-            alpha = jnp.exp(m_old - m_new)
+            p = jnp.exp2(s - m_new)
+            alpha = jnp.exp2(m_old - m_new)
             l_ref[g] = (alpha * l_ref[g].reshape(reps, t, 1) + jnp.sum(p, axis=-1, keepdims=True)).reshape(reps * t, 1)
             pv = jnp.dot(p.reshape(reps * t, key_block).astype(jnp.bfloat16), v, preferred_element_type=jnp.float32)
             acc_ref[g] = alpha.reshape(reps * t, 1) * acc_ref[g] + pv
@@ -83,7 +83,9 @@
     t, width = queries.shape
     reps = width // hs // groups
     n_blocks = kv_rows.shape[0] // KEY_BLOCK
-    flags = (jnp.max(weights.reshape(t, n_blocks, KEY_BLOCK), axis=(0, 2)) > 0).astype(jnp.int32)
+    flags = (
+        jnp.max(weights.reshape(t, n_blocks, KEY_BLOCK), axis=(0, 2)) > 0.5 * NEGATIVE_MASK
+    ).astype(jnp.int32)
     kern = functools.partial(attn_kernel, first_call=first_call, last_call=last_call,
                              groups=groups, reps=reps, hs=hs)
     state = [
@@ -164,11 +166,14 @@
     query_counts = jnp.dot(pick.astype(jnp.float32), counts, precision=lax.Precision.HIGHEST)
     keypos = jnp.arange(segment.shape[0], dtype=jnp.int32)
     suffix_weights = (keypos[None, :] <= positions[:, None]) & (keypos[None, :] >= first[:, None])
-    pool_weights = jnp.repeat(query_counts, PAGE_TOKENS, axis=1).astype(jnp.bfloat16)
+    pool_bias = jnp.where(
+        query_counts > 0, jnp.log2(jnp.maximum(query_counts, 1.0)), NEGATIVE_MASK
+    )
+    pool_weights = jnp.repeat(pool_bias, PAGE_TOKENS, axis=1)
     carry = flash(queries, pool_weights, pool_rows, None, True, False, KEY_VALUE_HEADS, HEAD_SIZE)
     attended = flash(
         queries,
-        suffix_weights.astype(jnp.bfloat16),
+        jnp.where(suffix_weights, 0.0, NEGATIVE_MASK).astype(jnp.float32),
         segment,
         carry,
         False,

time: 431 us -> 435 us (level)
  Pallas kernels: 56.4 us -> 63 us
    pallas_call x2, Pallas kernels: 56.4 us -> 63 us  [flash(): pl.pallas_call(kern, grid_spec=grid_spec, out_shape=out_shape)]
  transfers between devices with their start and end apart: 6 -> 6, of which waited for: 5 -> 5; matrix products, arithmetic and copies ran while one was open for 15% -> 15% of each run, Pallas kernels for 11% -> 12%
where the time goes in v7:
time: 435 us; the launch traced here: 434 us
  waiting for transfers between devices  245 us (56%)
  matrix products  68.3 us (16%)
  Pallas kernels  63 us (14%)
  starting transfers between devices  30.7 us (7%)
  between operations  13.7 us (3%)
  other arithmetic  6.7 us (2%)
  local copies, waits for them, and re-layouts  5.76 us (1%)
    all_to_all x2, waiting for transfers between devices, on_device(): lax.all_to_all(outgoing, ('req', 'exp'), split_axis=0, concat_axis=0, til...  99.7 us
    all_to_all x2, waiting for transfers between devices, on_device(): lax.all_to_all(jnp.dot(inner, w_down[0], preferred_element_type=jnp.float...  95.8 us
    pallas_call x2, Pallas kernels, flash(): pl.pallas_call(kern, grid_spec=grid_spec, out_shape=out_shape)  63 us
    all_gather x1, waiting for transfers between devices, on_device(): lax.all_gather(page_pool, 'req', axis=0, tiled=True)  49.1 us
    all_to_all x2, starting transfers between devices, on_device(): lax.all_to_all(outgoing, ('req', 'exp'), split_axis=0, concat_axis=0, til...  17.6 us
    dot_general x2, matrix products, on_device(): up_part = jnp.dot(flat_rows, w_up[0], preferred_element_type=jnp.float32)  14.9 us
    dot_general x2, matrix products, on_device(): jnp.dot(flat_rows, w_gate[0], preferred_element_type=jnp.float32)  14.4 us
    all_to_all x2, starting transfers between devices, on_device(): lax.all_to_all(jnp.dot(inner, w_down[0], preferred_element_type=jnp.float...  13.1 us
  transfers between devices with their start and end apart: 6, of which 5 were waited for; matrix products, arithmetic and copies ran while one was open for 15% of the time, Pallas kernels for 12%

profile of v7, /device:TPU:34, one launch (start us, length us, event | category | flops | bytes accessed | tf_op | source)
XLA Modules:
  0.0 433.5 jit_solution(5299499535424673281)
XLA Ops:
  6.5 0.7 all-gather.3.cloned.1.call-update
  7.3 49.1 %all-gather.3.cloned.1.call-done = bf16[56,128,512]{2,1,0:T(8,128)(2,1)} async-done(((bf16[7,128,512]{2,1,0:T(8,128)(2,1)}), bf16[56,128,512]{2,1,0:T(8,128)(2,1)}) %all-gather.3.cloned.1.call-update) | async-done | bytes 7340048 | tf_op jit(solution)/shard_map/all_gather | solution.py:155
  56.4 0.8 reduce-window.4
  57.3 0.1 convert_reduce_fusion.1
  57.4 0.8 convert_reduce_fusion
  58.1 0.2 multiply_select_fusion
  58.4 0.1 copy.24
  58.5 1.0 broadcast_in_dim.121
  59.5 2.5 copy.27
  62.1 1.2 broadcast_reduce_fusion
  63.2 0.1 reduce_max.36
  63.3 0.1 reduce_max.37
  63.5 0.1 select_reduce_fusion.3
  63.6 0.3 select_reduce_fusion
  63.9 0.6 compare_convert_fusion.flags_ref
  64.6 0.5 compare_convert_fusion.1.flags_ref
  65.1 0.1 convolution_convert_fusion.4
  65.2 0.1 fusion.56
  65.4 1.4 fusion.53.w_ref
  66.8 0.9 broadcast_6_m_in_l_in.2.m_in.l_in
  67.7 0.9 broadcast_in_dim.122.acc_in
  68.6 51.3 %shard_map.118 = (f32[2,640,1]{2,1,0:T(8,128)}, f32[2,640,1]{2,1,0:T(8,128)}, f32[2,640,128]{2,1,0:T(8,128)}) custom-call(s32[14]{0:T(128)} %compare_convert_fusion.flags_ref, bf16[128,1280]{1,0:T(8,128)(2,1)} %q_ref.3, f32[128,7168]{1,0:T(8,128)} %bitcast.101, bf16[7168,512]{1,0:T(8,128)(2,1)} %bitcast.102, f32[2,640,1]{2,1,0:T(8,128)} %broadcast_6_m_in_l_in.2.m_in.l_in, ...), custom_call_target="tpu_custom_call" | custom-call | tf_op jit(solution)/shard_map/pallas_call | solution.py:124
  119.9 11.6 %shard_map.119 = bf16[128,1280]{1,0:T(8,128)(2,1)} custom-call(s32[4]{0:T(128)} %compare_convert_fusion.1.flags_ref, bf16[128,1280]{1,0:T(8,128)(2,1)} %q_ref.3, f32[128,2048]{1,0:T(8,128)} %fusion.53.w_ref, bf16[2048,512]{1,0:T(8,128)(2,1)} %all-gather.5.cloned.1.call-done.kv_ref, f32[2,640,1]{2,1,0:T(8,128)} %get-tuple-element.12.m_in, ...), custom_call_target="tpu_custom_call" | custom-call | tf_op jit(solution)/shard_map/pallas_call | solution.py:124
  131.5 4.0 fusion.38
  135.6 0.2 fusion.50
  135.8 0.1 broadcast_in_dim.129
  135.9 3.9 fusion.16
  139.8 11.0 %all-to-all-start = ((bf16[128,8,2560]{2,1,0:T(8,128)(2,1)}), bf16[128,8,2560]{2,1,0:T(8,128)(2,1)}, u32[]{:S(2)}, u32[]{:S(2)}) async-start(bf16[128,8,2560]{2,1,0:T(8,128)(2,1)} %fusion.16), calls=%async_computation | async-start | bytes 10485760 | tf_op jit(solution)/shard_map/all_to_all | solution.py:228
  150.8 3.9 fusion.17
  154.7 58.2 %all-to-all-done = bf16[128,8,2560]{2,1,0:T(8,128)(2,1)} async-done(((bf16[128,8,2560]{2,1,0:T(8,128)(2,1)}), bf16[128,8,2560]{2,1,0:T(8,128)(2,1)}, u32[]{:S(2)}, u32[]{:S(2)}) %all-to-all-start) | async-done | bytes 5242912 | tf_op jit(solution)/shard_map/all_to_all | solution.py:228
  212.9 6.6 %all-to-all-start.2 = ((bf16[128,8,2560]{2,1,0:T(8,128)(2,1)}), bf16[128,8,2560]{2,1,0:T(8,128)(2,1)}, u32[]{:S(2)}, u32[]{:S(2)}) async-start(bf16[128,8,2560]{2,1,0:T(8,128)(2,1)} %fusion.17), calls=%async_computation.2 | async-start | bytes 10485760 | tf_op jit(solution)/shard_map/all_to_all | solution.py:228
  219.5 7.5 %fusion.12 = f32[1024,768]{1,0:T(8,128)S(1)} fusion(bf16[128,8,2560]{2,1,0:T(8,128)(2,1)} %all-to-all-done, bf16[1,2560,768]{2,1,0:T(8,128)(2,1)} %param.22), kind=kOutput, calls=%fused_computation.16 | convolution fusion | flops 4026531840 | bytes 12320768 | tf_op jit(solution)/shard_map/dot_general | solution.py:231
  227.0 7.2 %multiply_convert_fusion.1 = bf16[1024,768]{1,0:T(8,128)(2,1)S(1)} fusion(f32[1024,768]{1,0:T(8,128)S(1)} %fusion.12, bf16[1,2560,768]{2,1,0:T(8,128)(2,1)S(1)} %copy-done.3, bf16[128,8,2560]{2,1,0:T(8,128)(2,1)} %all-to-all-done), kind=kOutput, calls=%fused_computation.39 | convolution fusion | flops 4031250432 | bytes 13893632 | tf_op jit(solution)/shard_map/dot_general | solution.py:230
  234.2 6.0 %fusion.18 = bf16[128,8,2560]{2,1,0:T(8,128)(2,1)} fusion(bf16[1024,768]{1,0:T(8,128)(2,1)S(1)} %multiply_convert_fusion.1, bf16[1,768,2560]{2,1,0:T(8,128)(2,1)S(1)} %copy-done.5), kind=kOutput, calls=%fused_computation.22 | convolution fusion | flops 4029153280 | bytes 10747904 | tf_op jit(solution)/shard_map/dot_general | solution.py:234
  240.2 41.4 %all-to-all-done.2 = bf16[128,8,2560]{2,1,0:T(8,128)(2,1)} async-done(((bf16[128,8,2560]{2,1,0:T(8,128)(2,1)}), bf16[128,8,2560]{2,1,0:T(8,128)(2,1)}, u32[]{:S(2)}, u32[]{:S(2)}) %all-to-all-start.2) | async-done | bytes 5242912 | tf_op jit(solution)/shard_map/all_to_all | solution.py:228
  281.6 6.6 %all-to-all-start.1 = ((bf16[128,8,2560]{2,1,0:T(8,128)(2,1)}), bf16[128,8,2560]{2,1,0:T(8,128)(2,1)}, u32[]{:S(2)}, u32[]{:S(2)}) async-start(bf16[128,8,2560]{2,1,0:T(8,128)(2,1)} %fusion.18), calls=%async_computation.1 | async-start | bytes 10485760 | tf_op jit(solution)/shard_map/all_to_all | solution.py:233
  288.2 7.5 %fusion.4 = f32[1024,768]{1,0:T(8,128)S(1)} fusion(bf16[128,8,2560]{2,1,0:T(8,128)(2,1)} %all-to-all-done.2, bf16[1,2560,768]{2,1,0:T(8,128)(2,1)} %param.22), kind=kOutput, calls=%fused_computation.8 | convolution fusion | flops 4026531840 | bytes 12320768 | tf_op jit(solution)/shard_map/dot_general | solution.py:231
  295.7 7.2 %multiply_convert_fusion = bf16[1024,768]{1,0:T(8,128)(2,1)S(1)} fusion(f32[1024,768]{1,0:T(8,128)S(1)} %fusion.4, bf16[1,2560,768]{2,1,0:T(8,128)(2,1)S(1)} %copy-done.4, bf16[128,8,2560]{2,1,0:T(8,128)(2,1)} %all-to-all-done.2), kind=kOutput, calls=%fused_computation.38 | convolution fusion | flops 4031250432 | bytes 13893632 | tf_op jit(solution)/shard_map/dot_general | solution.py:230
  302.9 6.0 %fusion.19 = bf16[128,8,2560]{2,1,0:T(8,128)(2,1)} fusion(bf16[1024,768]{1,0:T(8,128)(2,1)S(1)} %multiply_convert_fusion, bf16[1,768,2560]{2,1,0:T(8,128)(2,1)S(1)} %copy-done.6), kind=kOutput, calls=%fused_computation.23 | convolution fusion | flops 4029153280 | bytes 10747904 | tf_op jit(solution)/shard_map/dot_general | solution.py:234
  309.0 41.4 %all-to-all-done.1 = bf16[128,8,2560]{2,1,0:T(8,128)(2,1)} async-done(((bf16[128,8,2560]{2,1,0:T(8,128)(2,1)}), bf16[128,8,2560]{2,1,0:T(8,128)(2,1)}, u32[]{:S(2)}, u32[]{:S(2)}) %all-to-all-start.1) | async-done | bytes 5242912 | tf_op jit(solution)/shard_map/all_to_all | solution.py:233
  350.3 6.5 %all-to-all-start.3 = ((bf16[128,8,2560]{2,1,0:T(8,128)(2,1)}), bf16[128,8,2560]{2,1,0:T(8,128)(2,1)}, u32[]{:S(2)}, u32[]{:S(2)}) async-start(bf16[128,8,2560]{2,1,0:T(8,128)(2,1)} %fusion.19), calls=%async_computation.3 | async-start | bytes 10485760 | tf_op jit(solution)/shard_map/all_to_all | solution.py:233
  356.9 0.4 fusion.65
  357.4 0.1 fusion.55
  357.7 3.4 fusion.26
  361.1 3.4 fusion.29
  364.5 54.5 %all-to-all-done.3 = bf16[128,8,2560]{2,1,0:T(8,128)(2,1)} async-done(((bf16[128,8,2560]{2,1,0:T(8,128)(2,1)}), bf16[128,8,2560]{2,1,0:T(8,128)(2,1)}, u32[]{:S(2)}, u32[]{:S(2)}) %all-to-all-start.3) | async-done | bytes 5242912 | tf_op jit(solution)/shard_map/all_to_all | solution.py:233
  419.1 3.4 fusion.32
  422.5 4.2 fusion.39
  (36 shorter events, 0.5 us)
Async XLA Ops:
  6.5 350.3 %copy-start = (bf16[2560,64]{0,1:T(8,128)(2,1)S(1)}, bf16[2560,64]{0,1:T(8,128)(2,1)}, u32[]{:S(2)}) copy-start(bf16[2560,64]{0,1:T(8,128)(2,1)} %param.19) | copy-start | bytes 983044
  6.5 49.9 %all-gather.3.cloned.1.call-start = ((), (), s32[]{:S(2)}) async-start(), calls=%async_computation.4 | async-start | bytes 8257536 | tf_op jit(solution)/shard_map/all_gather | solution.py:155
  7.3 112.7 %all-gather.5.cloned.1.call-start = ((), (), s32[]{:S(2)}) async-start(), calls=%async_computation.5 | async-start | bytes 2228224 | tf_op jit(solution)/shard_map/all_gather | solution.py:159
  59.5 4.0 copy-start.7
  59.5 4.1 copy-start.2
  119.9 11.6 %copy-start.1 = (bf16[128,2560]{1,0:T(8,128)(2,1)S(1)}, bf16[128,2560]{1,0:T(8,128)(2,1)}, u32[]{:S(2)}) copy-start(bf16[128,2560]{1,0:T(8,128)(2,1)} %param.12) | copy-start | bytes 1966084
  139.8 73.1 %all-to-all-start = ((bf16[128,8,2560]{2,1,0:T(8,128)(2,1)}), bf16[128,8,2560]{2,1,0:T(8,128)(2,1)}, u32[]{:S(2)}, u32[]{:S(2)}) async-start(bf16[128,8,2560]{2,1,0:T(8,128)(2,1)} %fusion.16), calls=%async_computation | async-start | bytes 10485760 | tf_op jit(solution)/shard_map/all_to_all | solution.py:228
  212.9 68.7 %all-to-all-start.2 = ((bf16[128,8,2560]{2,1,0:T(8,128)(2,1)}), bf16[128,8,2560]{2,1,0:T(8,128)(2,1)}, u32[]{:S(2)}, u32[]{:S(2)}) async-start(bf16[128,8,2560]{2,1,0:T(8,128)(2,1)} %fusion.17), calls=%async_computation.2 | async-start | bytes 10485760 | tf_op jit(solution)/shard_map/all_to_all | solution.py:228
  219.5 7.5 %copy-start.3 = (bf16[1,2560,768]{2,1,0:T(8,128)(2,1)S(1)}, bf16[1,2560,768]{2,1,0:T(8,128)(2,1)}, u32[]{:S(2)}) copy-start(bf16[1,2560,768]{2,1,0:T(8,128)(2,1)} %param.21) | copy-start | bytes 11796484
  227.0 7.2 %copy-start.5 = (bf16[1,768,2560]{2,1,0:T(8,128)(2,1)S(1)}, bf16[1,768,2560]{2,1,0:T(8,128)(2,1)}, u32[]{:S(2)}) copy-start(bf16[1,768,2560]{2,1,0:T(8,128)(2,1)} %param.23) | copy-start | bytes 11796484
  281.6 68.7 %all-to-all-start.1 = ((bf16[128,8,2560]{2,1,0:T(8,128)(2,1)}), bf16[128,8,2560]{2,1,0:T(8,128)(2,1)}, u32[]{:S(2)}, u32[]{:S(2)}) async-start(bf16[128,8,2560]{2,1,0:T(8,128)(2,1)} %fusion.18), calls=%async_computation.1 | async-start | bytes 10485760 | tf_op jit(solution)/shard_map/all_to_all | solution.py:233
  288.2 7.5 %copy-start.4 = (bf16[1,2560,768]{2,1,0:T(8,128)(2,1)S(1)}, bf16[1,2560,768]{2,1,0:T(8,128)(2,1)}, u32[]{:S(2)}) copy-start(bf16[1,2560,768]{2,1,0:T(8,128)(2,1)} %param.21) | copy-start | bytes 11796484
  295.7 7.2 %copy-start.6 = (bf16[1,768,2560]{2,1,0:T(8,128)(2,1)S(1)}, bf16[1,768,2560]{2,1,0:T(8,128)(2,1)}, u32[]{:S(2)}) copy-start(bf16[1,768,2560]{2,1,0:T(8,128)(2,1)} %param.23) | copy-start | bytes 11796484
  350.3 68.7 %all-to-all-start.3 = ((bf16[128,8,2560]{2,1,0:T(8,128)(2,1)}), bf16[128,8,2560]{2,1,0:T(8,128)(2,1)}, u32[]{:S(2)}, u32[]{:S(2)}) async-start(bf16[128,8,2560]{2,1,0:T(8,128)(2,1)} %fusion.19), calls=%async_computation.3 | async-start | bytes 10485760 | tf_op jit(solution)/shard_map/all_to_all | solution.py:233
Sparse Core Ops, SparseCore 0:
  9.0 47.3 all-gather.2
  58.5 43.7 all-gather.4

commit v8 on v7

--- a/solution.py
+++ b/solution.py
@@ -22,13 +22,14 @@
 
 KEY_BLOCK = 512
 LOG2_E = 1.4426950408889634
+SOFTMAX_ROWS = 32
 
 
 def attn_kernel(flags_ref, q_ref, w_ref, kv_ref, m_in, l_in, acc_in, *refs, first_call, last_call, groups, reps, hs):
     if last_call:
-        o_ref, qs, m_ref, l_ref, acc_ref = refs
+        o_ref, qs, m_ref, l_ref, acc_ref, s_scr, p_scr, a_scr = refs
     else:
-        m_out, l_out, acc_out, qs, m_ref, l_ref, acc_ref = refs
+        m_out, l_out, acc_out, qs, m_ref, l_ref, acc_ref, s_scr, p_scr, a_scr = refs
     j = pl.program_id(0)
     t = q_ref.shape[0]
     key_block = kv_ref.shape[0]
@@ -49,21 +50,31 @@
 
     @pl.when(flags_ref[j] > 0)
     def _():
-        bias = w_ref[...][None]
+        chunk = SOFTMAX_ROWS
         for g in range(groups):
             k = kv_ref[:, g * hs:(g + 1) * hs]
             v = kv_ref[:, (groups + g) * hs:(groups + g + 1) * hs]
-            s = lax.dot_general(qs[g], k, (((1,), (1,)), ((), ())),
-                                preferred_element_type=jnp.float32) * (LOG2_E / math.sqrt(hs))
-            s = s.reshape(reps, t, key_block) + bias
-            m_old = m_ref[g].reshape(reps, t, 1)
-            m_new = jnp.maximum(m_old, jnp.max(s, axis=-1, keepdims=True))
-            p = jnp.exp2(s - m_new)
-            alpha = jnp.exp2(m_old - m_new)
-            l_ref[g] = (alpha * l_ref[g].reshape(reps, t, 1) + jnp.sum(p, axis=-1, keepdims=True)).reshape(reps * t, 1)
-            pv = jnp.dot(p.reshape(reps * t, key_block).astype(jnp.bfloat16), v, preferred_element_type=jnp.float32)
-            acc_ref[g] = alpha.reshape(reps * t, 1) * acc_ref[g] + pv
-            m_ref[g] = m_new.reshape(reps * t, 1)
+            s_scr[...] = lax.dot_general(qs[g], k, (((1,), (1,)), ((), ())),
+                                         preferred_element_type=jnp.float32)
+
+            def body(i, c):
+                r = pl.multiple_of(i * chunk, chunk)
+                b = pl.multiple_of((i * chunk) % t, chunk)
+                s = s_scr[pl.ds(r, chunk), :] * (LOG2_E / math.sqrt(hs)) + w_ref[pl.ds(b, chunk), :]
+                m_old = m_ref[g, pl.ds(r, chunk), :]
+                m_new = jnp.maximum(m_old, jnp.max(s, axis=-1, keepdims=True))
+                p = jnp.exp2(s - m_new)
+                alpha = jnp.exp2(m_old - m_new)
+                l_ref[g, pl.ds(r, chunk), :] = alpha * l_ref[g, pl.ds(r, chunk), :] + jnp.sum(
+                    p, axis=-1, keepdims=True)
+                m_ref[g, pl.ds(r, chunk), :] = m_new
+                a_scr[pl.ds(r, chunk), :] = alpha
+                p_scr[pl.ds(r, chunk), :] = p.astype(jnp.bfloat16)
+                return c
+
+            lax.fori_loop(0, reps * t // chunk, body, 0, unroll=2)
+            pv = jnp.dot(p_scr[...], v, preferred_element_type=jnp.float32)
+            acc_ref[g] = a_scr[...] * acc_ref[g] + pv
 
     @pl.when(j == pl.num_programs(0) - 1)
     def _():
@@ -117,6 +128,9 @@
             pltpu.VMEM((groups, reps * t, 1), jnp.float32),
             pltpu.VMEM((groups, reps * t, 1), jnp.float32),
             pltpu.VMEM((groups, reps * t, hs), jnp.float32),
+            pltpu.VMEM((reps * t, KEY_BLOCK), jnp.float32),
+            pltpu.VMEM((reps * t, KEY_BLOCK), jnp.bfloat16),
+            pltpu.VMEM((reps * t, 1), jnp.float32),
         ],
     )
     if carry is None:

time: 435 us -> 494 us (1.14)
  Pallas kernels: 63 us -> 118 us
    pallas_call x2, Pallas kernels: 63 us -> 118 us  [flash(): pl.pallas_call(kern, grid_spec=grid_spec, out_shape=out_shape)]
  transfers between devices with their start and end apart: 6 -> 6, of which waited for: 5 -> 5; matrix products, arithmetic and copies ran while one was open for 15% -> 13% of each run, Pallas kernels for 12% -> 20%
where the time goes in v8:
time: 494 us; the launch traced here: 492 us
  waiting for transfers between devices  245 us (50%)
  Pallas kernels  118 us (24%)
  matrix products  68.3 us (14%)
  starting transfers between devices  33.7 us (7%)
  between operations  13.7 us (3%)
  other arithmetic  6.7 us (1%)
  local copies, waits for them, and re-layouts  5.76 us (1%)
    pallas_call x2, Pallas kernels, flash(): pl.pallas_call(kern, grid_spec=grid_spec, out_shape=out_shape)  118 us
    all_to_all x2, waiting for transfers between devices, on_device(): lax.all_to_all(outgoing, ('req', 'exp'), split_axis=0, concat_axis=0, til...  99.6 us
    all_to_all x2, waiting for transfers between devices, on_device(): lax.all_to_all(jnp.dot(inner, w_down[0], preferred_element_type=jnp.float...  95.8 us
    all_gather x1, waiting for transfers between devices, on_device(): lax.all_gather(page_pool, 'req', axis=0, tiled=True)  49.1 us
    all_to_all x2, starting transfers between devices, on_device(): lax.all_to_all(outgoing, ('req', 'exp'), split_axis=0, concat_axis=0, til...  20.6 us
    dot_general x2, matrix products, on_device(): up_part = jnp.dot(flat_rows, w_up[0], preferred_element_type=jnp.float32)  14.9 us
    dot_general x2, matrix products, on_device(): jnp.dot(flat_rows, w_gate[0], preferred_element_type=jnp.float32)  14.4 us
    all_to_all x2, starting transfers between devices, on_device(): lax.all_to_all(jnp.dot(inner, w_down[0], preferred_element_type=jnp.float...  13.1 us
  transfers between devices with their start and end apart: 6, of which 5 were waited for; matrix products, arithmetic and copies ran while one was open for 13% of the time, Pallas kernels for 20%

profile of v8, /device:TPU:34, one launch (start us, length us, event | category | flops | bytes accessed | tf_op | source)
XLA Modules:
  0.0 491.9 jit_solution(16110338941806967045)
XLA Ops:
  6.5 0.7 all-gather.3.cloned.1.call-update
  7.3 49.1 %all-gather.3.cloned.1.call-done = bf16[56,128,512]{2,1,0:T(8,128)(2,1)} async-done(((bf16[7,128,512]{2,1,0:T(8,128)(2,1)}), bf16[56,128,512]{2,1,0:T(8,128)(2,1)}) %all-gather.3.cloned.1.call-update) | async-done | bytes 7340048 | tf_op jit(solution)/shard_map/all_gather | solution.py:169
  56.4 0.8 reduce-window.4
  57.3 0.1 convert_reduce_fusion.1
  57.4 0.8 convert_reduce_fusion
  58.1 0.2 multiply_select_fusion
  58.4 0.1 copy.24
  58.5 1.0 broadcast_in_dim.121
  59.5 2.5 copy.27
  62.1 1.2 broadcast_reduce_fusion
  63.2 0.1 reduce_max.36
  63.3 0.1 reduce_max.37
  63.5 0.1 select_reduce_fusion.3
  63.6 0.3 select_reduce_fusion
  63.9 0.6 compare_convert_fusion.flags_ref
  64.6 0.5 compare_convert_fusion.1.flags_ref
  65.1 0.1 convolution_convert_fusion.4
  65.2 0.1 fusion.56
  65.4 1.4 fusion.53.w_ref
  66.8 0.9 broadcast_6_m_in_l_in.2.m_in.l_in
  67.7 0.9 broadcast_in_dim.122.acc_in
  68.6 99.8 %shard_map.118 = (f32[2,640,1]{2,1,0:T(8,128)}, f32[2,640,1]{2,1,0:T(8,128)}, f32[2,640,128]{2,1,0:T(8,128)}) custom-call(s32[14]{0:T(128)} %compare_convert_fusion.flags_ref, bf16[128,1280]{1,0:T(8,128)(2,1)} %q_ref.3, f32[128,7168]{1,0:T(8,128)} %bitcast.101, bf16[7168,512]{1,0:T(8,128)(2,1)} %bitcast.102, f32[2,640,1]{2,1,0:T(8,128)} %broadcast_6_m_in_l_in.2.m_in.l_in, ...), custom_call_target="tpu_custom_call" | custom-call | tf_op jit(solution)/shard_map/pallas_call | solution.py:138
  168.4 18.5 %shard_map.119 = bf16[128,1280]{1,0:T(8,128)(2,1)} custom-call(s32[4]{0:T(128)} %compare_convert_fusion.1.flags_ref, bf16[128,1280]{1,0:T(8,128)(2,1)} %q_ref.3, f32[128,2048]{1,0:T(8,128)} %fusion.53.w_ref, bf16[2048,512]{1,0:T(8,128)(2,1)} %all-gather.5.cloned.1.call-done.kv_ref, f32[2,640,1]{2,1,0:T(8,128)} %get-tuple-element.12.m_in, ...), custom_call_target="tpu_custom_call" | custom-call | tf_op jit(solution)/shard_map/pallas_call | solution.py:138
  186.9 4.0 fusion.38
  190.9 0.2 fusion.50
  191.2 0.1 broadcast_in_dim.129
  191.2 3.9 fusion.16
  195.2 14.0 %all-to-all-start = ((bf16[128,8,2560]{2,1,0:T(8,128)(2,1)}), bf16[128,8,2560]{2,1,0:T(8,128)(2,1)}, u32[]{:S(2)}, u32[]{:S(2)}) async-start(bf16[128,8,2560]{2,1,0:T(8,128)(2,1)} %fusion.16), calls=%async_computation | async-start | bytes 10485760 | tf_op jit(solution)/shard_map/all_to_all | solution.py:242
  209.2 3.9 fusion.17
  213.1 58.2 %all-to-all-done = bf16[128,8,2560]{2,1,0:T(8,128)(2,1)} async-done(((bf16[128,8,2560]{2,1,0:T(8,128)(2,1)}), bf16[128,8,2560]{2,1,0:T(8,128)(2,1)}, u32[]{:S(2)}, u32[]{:S(2)}) %all-to-all-start) | async-done | bytes 5242912 | tf_op jit(solution)/shard_map/all_to_all | solution.py:242
  271.3 6.6 %all-to-all-start.2 = ((bf16[128,8,2560]{2,1,0:T(8,128)(2,1)}), bf16[128,8,2560]{2,1,0:T(8,128)(2,1)}, u32[]{:S(2)}, u32[]{:S(2)}) async-start(bf16[128,8,2560]{2,1,0:T(8,128)(2,1)} %fusion.17), calls=%async_computation.2 | async-start | bytes 10485760 | tf_op jit(solution)/shard_map/all_to_all | solution.py:242
  277.9 7.5 %fusion.12 = f32[1024,768]{1,0:T(8,128)S(1)} fusion(bf16[128,8,2560]{2,1,0:T(8,128)(2,1)} %all-to-all-done, bf16[1,2560,768]{2,1,0:T(8,128)(2,1)} %param.22), kind=kOutput, calls=%fused_computation.16 | convolution fusion | flops 4026531840 | bytes 12320768 | tf_op jit(solution)/shard_map/dot_general | solution.py:245
  285.4 7.2 %multiply_convert_fusion.1 = bf16[1024,768]{1,0:T(8,128)(2,1)S(1)} fusion(f32[1024,768]{1,0:T(8,128)S(1)} %fusion.12, bf16[1,2560,768]{2,1,0:T(8,128)(2,1)S(1)} %copy-done.3, bf16[128,8,2560]{2,1,0:T(8,128)(2,1)} %all-to-all-done), kind=kOutput, calls=%fused_computation.39 | convolution fusion | flops 4031250432 | bytes 13893632 | tf_op jit(solution)/shard_map/dot_general | solution.py:244
  292.7 6.0 %fusion.18 = bf16[128,8,2560]{2,1,0:T(8,128)(2,1)} fusion(bf16[1024,768]{1,0:T(8,128)(2,1)S(1)} %multiply_convert_fusion.1, bf16[1,768,2560]{2,1,0:T(8,128)(2,1)S(1)} %copy-done.5), kind=kOutput, calls=%fused_computation.22 | convolution fusion | flops 4029153280 | bytes 10747904 | tf_op jit(solution)/shard_map/dot_general | solution.py:248
  298.6 41.4 %all-to-all-done.2 = bf16[128,8,2560]{2,1,0:T(8,128)(2,1)} async-done(((bf16[128,8,2560]{2,1,0:T(8,128)(2,1)}), bf16[128,8,2560]{2,1,0:T(8,128)(2,1)}, u32[]{:S(2)}, u32[]{:S(2)}) %all-to-all-start.2) | async-done | bytes 5242912 | tf_op jit(solution)/shard_map/all_to_all | solution.py:242
  340.1 6.5 %all-to-all-start.1 = ((bf16[128,8,2560]{2,1,0:T(8,128)(2,1)}), bf16[128,8,2560]{2,1,0:T(8,128)(2,1)}, u32[]{:S(2)}, u32[]{:S(2)}) async-start(bf16[128,8,2560]{2,1,0:T(8,128)(2,1)} %fusion.18), calls=%async_computation.1 | async-start | bytes 10485760 | tf_op jit(solution)/shard_map/all_to_all | solution.py:247
  346.6 7.5 %fusion.4 = f32[1024,768]{1,0:T(8,128)S(1)} fusion(bf16[128,8,2560]{2,1,0:T(8,128)(2,1)} %all-to-all-done.2, bf16[1,2560,768]{2,1,0:T(8,128)(2,1)} %param.22), kind=kOutput, calls=%fused_computation.8 | convolution fusion | flops 4026531840 | bytes 12320768 | tf_op jit(solution)/shard_map/dot_general | solution.py:245
  354.1 7.2 %multiply_convert_fusion = bf16[1024,768]{1,0:T(8,128)(2,1)S(1)} fusion(f32[1024,768]{1,0:T(8,128)S(1)} %fusion.4, bf16[1,2560,768]{2,1,0:T(8,128)(2,1)S(1)} %copy-done.4, bf16[128,8,2560]{2,1,0:T(8,128)(2,1)} %all-to-all-done.2), kind=kOutput, calls=%fused_computation.38 | convolution fusion | flops 4031250432 | bytes 13893632 | tf_op jit(solution)/shard_map/dot_general | solution.py:244
  361.3 6.0 %fusion.19 = bf16[128,8,2560]{2,1,0:T(8,128)(2,1)} fusion(bf16[1024,768]{1,0:T(8,128)(2,1)S(1)} %multiply_convert_fusion, bf16[1,768,2560]{2,1,0:T(8,128)(2,1)S(1)} %copy-done.6), kind=kOutput, calls=%fused_computation.23 | convolution fusion | flops 4029153280 | bytes 10747904 | tf_op jit(solution)/shard_map/dot_general | solution.py:248
  367.4 41.4 %all-to-all-done.1 = bf16[128,8,2560]{2,1,0:T(8,128)(2,1)} async-done(((bf16[128,8,2560]{2,1,0:T(8,128)(2,1)}), bf16[128,8,2560]{2,1,0:T(8,128)(2,1)}, u32[]{:S(2)}, u32[]{:S(2)}) %all-to-all-start.1) | async-done | bytes 5242912 | tf_op jit(solution)/shard_map/all_to_all | solution.py:247
  408.7 6.5 %all-to-all-start.3 = ((bf16[128,8,2560]{2,1,0:T(8,128)(2,1)}), bf16[128,8,2560]{2,1,0:T(8,128)(2,1)}, u32[]{:S(2)}, u32[]{:S(2)}) async-start(bf16[128,8,2560]{2,1,0:T(8,128)(2,1)} %fusion.19), calls=%async_computation.3 | async-start | bytes 10485760 | tf_op jit(solution)/shard_map/all_to_all | solution.py:247
  415.3 0.4 fusion.65
  415.8 0.1 fusion.55
  416.1 3.4 fusion.26
  419.5 3.4 fusion.29
  422.9 54.5 %all-to-all-done.3 = bf16[128,8,2560]{2,1,0:T(8,128)(2,1)} async-done(((bf16[128,8,2560]{2,1,0:T(8,128)(2,1)}), bf16[128,8,2560]{2,1,0:T(8,128)(2,1)}, u32[]{:S(2)}, u32[]{:S(2)}) %all-to-all-start.3) | async-done | bytes 5242912 | tf_op jit(solution)/shard_map/all_to_all | solution.py:247
  477.4 3.4 fusion.32
  480.9 4.2 fusion.39
  (36 shorter events, 0.5 us)
Async XLA Ops:
  6.5 408.7 %copy-start = (bf16[2560,64]{0,1:T(8,128)(2,1)S(1)}, bf16[2560,64]{0,1:T(8,128)(2,1)}, u32[]{:S(2)}) copy-start(bf16[2560,64]{0,1:T(8,128)(2,1)} %param.19) | copy-start | bytes 983044
  6.5 49.9 %all-gather.3.cloned.1.call-start = ((), (), s32[]{:S(2)}) async-start(), calls=%async_computation.4 | async-start | bytes 8257536 | tf_op jit(solution)/shard_map/all_gather | solution.py:169
  7.3 161.1 %all-gather.5.cloned.1.call-start = ((), (), s32[]{:S(2)}) async-start(), calls=%async_computation.5 | async-start | bytes 2228224 | tf_op jit(solution)/shard_map/all_gather | solution.py:173
  59.5 4.0 copy-start.7
  59.5 4.1 copy-start.2
  168.4 18.5 %copy-start.1 = (bf16[128,2560]{1,0:T(8,128)(2,1)S(1)}, bf16[128,2560]{1,0:T(8,128)(2,1)}, u32[]{:S(2)}) copy-start(bf16[128,2560]{1,0:T(8,128)(2,1)} %param.12) | copy-start | bytes 1966084
  195.2 76.2 %all-to-all-start = ((bf16[128,8,2560]{2,1,0:T(8,128)(2,1)}), bf16[128,8,2560]{2,1,0:T(8,128)(2,1)}, u32[]{:S(2)}, u32[]{:S(2)}) async-start(bf16[128,8,2560]{2,1,0:T(8,128)(2,1)} %fusion.16), calls=%async_computation | async-start | bytes 10485760 | tf_op jit(solution)/shard_map/all_to_all | solution.py:242
  271.3 68.7 %all-to-all-start.2 = ((bf16[128,8,2560]{2,1,0:T(8,128)(2,1)}), bf16[128,8,2560]{2,1,0:T(8,128)(2,1)}, u32[]{:S(2)}, u32[]{:S(2)}) async-start(bf16[128,8,2560]{2,1,0:T(8,128)(2,1)} %fusion.17), calls=%async_computation.2 | async-start | bytes 10485760 | tf_op jit(solution)/shard_map/all_to_all | solution.py:242
  277.9 7.5 %copy-start.3 = (bf16[1,2560,768]{2,1,0:T(8,128)(2,1)S(1)}, bf16[1,2560,768]{2,1,0:T(8,128)(2,1)}, u32[]{:S(2)}) copy-start(bf16[1,2560,768]{2,1,0:T(8,128)(2,1)} %param.21) | copy-start | bytes 11796484
  285.4 7.2 %copy-start.5 = (bf16[1,768,2560]{2,1,0:T(8,128)(2,1)S(1)}, bf16[1,768,2560]{2,1,0:T(8,128)(2,1)}, u32[]{:S(2)}) copy-start(bf16[1,768,2560]{2,1,0:T(8,128)(2,1)} %param.23) | copy-start | bytes 11796484
  340.1 68.7 %all-to-all-start.1 = ((bf16[128,8,2560]{2,1,0:T(8,128)(2,1)}), bf16[128,8,2560]{2,1,0:T(8,128)(2,1)}, u32[]{:S(2)}, u32[]{:S(2)}) async-start(bf16[128,8,2560]{2,1,0:T(8,128)(2,1)} %fusion.18), calls=%async_computation.1 | async-start | bytes 10485760 | tf_op jit(solution)/shard_map/all_to_all | solution.py:247
  346.6 7.5 %copy-start.4 = (bf16[1,2560,768]{2,1,0:T(8,128)(2,1)S(1)}, bf16[1,2560,768]{2,1,0:T(8,128)(2,1)}, u32[]{:S(2)}) copy-start(bf16[1,2560,768]{2,1,0:T(8,128)(2,1)} %param.21) | copy-start | bytes 11796484
  354.1 7.2 %copy-start.6 = (bf16[1,768,2560]{2,1,0:T(8,128)(2,1)S(1)}, bf16[1,768,2560]{2,1,0:T(8,128)(2,1)}, u32[]{:S(2)}) copy-start(bf16[1,768,2560]{2,1,0:T(8,128)(2,1)} %param.23) | copy-start | bytes 11796484
  408.7 68.7 %all-to-all-start.3 = ((bf16[128,8,2560]{2,1,0:T(8,128)(2,1)}), bf16[128,8,2560]{2,1,0:T(8,128)(2,1)}, u32[]{:S(2)}, u32[]{:S(2)}) async-start(bf16[128,8,2560]{2,1,0:T(8,128)(2,1)} %fusion.19), calls=%async_computation.3 | async-start | bytes 10485760 | tf_op jit(solution)/shard_map/all_to_all | solution.py:247
Sparse Core Ops, SparseCore 0:
  9.0 47.3 all-gather.2
  58.5 43.6 all-gather.4

commit v9 on v7

--- a/solution.py
+++ b/solution.py
@@ -24,14 +24,18 @@
 LOG2_E = 1.4426950408889634
 
 
-def attn_kernel(flags_ref, q_ref, w_ref, kv_ref, m_in, l_in, acc_in, *refs, first_call, last_call, groups, reps, hs):
+def attn_kernel(flags_ref, order_ref, q_ref, *refs, parts, first_call, last_call, groups, reps, hs):
+    w_refs = refs[:parts]
+    kv_refs = refs[parts:2 * parts]
+    m_in, l_in, acc_in = refs[2 * parts:2 * parts + 3]
+    refs = refs[2 * parts + 3:]
     if last_call:
         o_ref, qs, m_ref, l_ref, acc_ref = refs
     else:
         m_out, l_out, acc_out, qs, m_ref, l_ref, acc_ref = refs
     j = pl.program_id(0)
     t = q_ref.shape[0]
-    key_block = kv_ref.shape[0]
+    key_block = sum(kv.shape[0] for kv in kv_refs)
 
     @pl.when(j == 0)
     def _():
@@ -47,12 +51,15 @@
             l_ref[...] = l_in[...]
             acc_ref[...] = acc_in[...]
 
+    def joined(pieces, axis):
+        return pieces[0] if len(pieces) == 1 else jnp.concatenate(pieces, axis=axis)
+
     @pl.when(flags_ref[j] > 0)
     def _():
-        bias = w_ref[...][None]
+        bias = joined([w[...] for w in w_refs], 1)[None]
         for g in range(groups):
-            k = kv_ref[:, g * hs:(g + 1) * hs]
-            v = kv_ref[:, (groups + g) * hs:(groups + g + 1) * hs]
+            k = joined([kv[:, g * hs:(g + 1) * hs] for kv in kv_refs], 0)
+            v = joined([kv[:, (groups + g) * hs:(groups + g + 1) * hs] for kv in kv_refs], 0)
             s = lax.dot_general(qs[g], k, (((1,), (1,)), ((), ())),
                                 preferred_element_type=jnp.float32) * (LOG2_E / math.sqrt(hs))
             s = s.reshape(reps, t, key_block) + bias
@@ -79,38 +86,51 @@
             acc_out[...] = acc_ref[...]
 
 
-def flash(queries, weights, kv_rows, carry, first_call, last_call, groups, hs):
+def flash(queries, bias, kv_rows, carry, first_call, last_call, groups, hs, order=None, parts=1):
     t, width = queries.shape
     reps = width // hs // groups
-    n_blocks = kv_rows.shape[0] // KEY_BLOCK
-    flags = (
-        jnp.max(weights.reshape(t, n_blocks, KEY_BLOCK), axis=(0, 2)) > 0.5 * NEGATIVE_MASK
-    ).astype(jnp.int32)
-    kern = functools.partial(attn_kernel, first_call=first_call, last_call=last_call,
-                             groups=groups, reps=reps, hs=hs)
+    if order is None:
+        block = KEY_BLOCK
+        n_blocks = kv_rows.shape[0] // block
+        flags = (
+            jnp.max(bias.reshape(t, n_blocks, block), axis=(0, 2)) > 0.5 * NEGATIVE_MASK
+        ).astype(jnp.int32)
+        order = jnp.zeros((1,), jnp.int32)
+        w_specs = [pl.BlockSpec((t, block), lambda j, f, o: (0, j))]
+        kv_specs = [pl.BlockSpec((block, kv_rows.shape[1]), lambda j, f, o: (j, 0))]
+    else:
+        order, live_count = order
+        block = kv_rows.shape[0] // order.shape[0]
+        n_blocks = order.shape[0] // parts
+        flags = (jnp.arange(n_blocks, dtype=jnp.int32) * parts < live_count).astype(jnp.int32)
+        w_specs = [
+            pl.BlockSpec((t, block), lambda j, f, o, i=i: (0, o[parts * j + i])) for i in range(parts)
+        ]
+        kv_specs = [
+            pl.BlockSpec((block, kv_rows.shape[1]), lambda j, f, o, i=i: (o[parts * j + i], 0))
+            for i in range(parts)
+        ]
+    kern = functools.partial(attn_kernel, parts=len(w_specs), first_call=first_call,
+                             last_call=last_call, groups=groups, reps=reps, hs=hs)
     state = [
         jax.ShapeDtypeStruct((groups, reps * t, 1), jnp.float32),
         jax.ShapeDtypeStruct((groups, reps * t, 1), jnp.float32),
         jax.ShapeDtypeStruct((groups, reps * t, hs), jnp.float32),
     ]
     state_specs = [
-        pl.BlockSpec((groups, reps * t, 1), lambda j, f: (0, 0, 0)),
-        pl.BlockSpec((groups, reps * t, 1), lambda j, f: (0, 0, 0)),
-        pl.BlockSpec((groups, reps * t, hs), lambda j, f: (0, 0, 0)),
+        pl.BlockSpec((groups, reps * t, 1), lambda j, f, o: (0, 0, 0)),
+        pl.BlockSpec((groups, reps * t, 1), lambda j, f, o: (0, 0, 0)),
+        pl.BlockSpec((groups, reps * t, hs), lambda j, f, o: (0, 0, 0)),
     ]
     if last_call:
         out_shape = jax.ShapeDtypeStruct((t, width), jnp.bfloat16)
-        out_specs = pl.BlockSpec((t, width), lambda j, f: (0, 0))
+        out_specs = pl.BlockSpec((t, width), lambda j, f, o: (0, 0))
     else:
         out_shape, out_specs = state, state_specs
     grid_spec = pltpu.PrefetchScalarGridSpec(
-        num_scalar_prefetch=1,
+        num_scalar_prefetch=2,
         grid=(n_blocks,),
-        in_specs=[
-            pl.BlockSpec((t, width), lambda j, f: (0, 0)),
-            pl.BlockSpec((t, KEY_BLOCK), lambda j, f: (0, j)),
-            pl.BlockSpec((KEY_BLOCK, kv_rows.shape[1]), lambda j, f: (j, 0)),
-        ] + state_specs,
+        in_specs=[pl.BlockSpec((t, width), lambda j, f, o: (0, 0))] + w_specs + kv_specs + state_specs,
         out_specs=out_specs,
         scratch_shapes=[
             pltpu.VMEM((groups, reps * t, hs), jnp.bfloat16),
@@ -121,8 +141,8 @@
     )
     if carry is None:
         carry = tuple(jnp.zeros(s.shape, s.dtype) for s in state)
-    return pl.pallas_call(kern, grid_spec=grid_spec, out_shape=out_shape)(
-        flags, queries, weights, kv_rows, *carry)
+    operands = [queries] + [bias] * len(w_specs) + [kv_rows] * len(kv_specs) + list(carry)
+    return pl.pallas_call(kern, grid_spec=grid_spec, out_shape=out_shape)(flags, order, *operands)
 
 
 def on_device(
@@ -170,7 +190,28 @@
         query_counts > 0, jnp.log2(jnp.maximum(query_counts, 1.0)), NEGATIVE_MASK
     )
     pool_weights = jnp.repeat(pool_bias, PAGE_TOKENS, axis=1)
-    carry = flash(queries, pool_weights, pool_rows, None, True, False, KEY_VALUE_HEADS, HEAD_SIZE)
+    live = jnp.max(query_counts, axis=0) > 0
+    live_int = live.astype(jnp.int32)
+    live_count = jnp.sum(live_int)
+    destination = jnp.where(
+        live, jnp.cumsum(live_int) - 1, live_count + jnp.cumsum(1 - live_int) - 1
+    )
+    slots = jnp.arange(pool_all, dtype=jnp.int32)
+    order = jnp.sum(
+        jnp.where(destination[None, :] == slots[:, None], slots[None, :], 0), axis=1
+    ).astype(jnp.int32)
+    carry = flash(
+        queries,
+        pool_weights,
+        pool_rows,
+        None,
+        True,
+        False,
+        KEY_VALUE_HEADS,
+        HEAD_SIZE,
+        (order, live_count),
+        KEY_BLOCK // PAGE_TOKENS,
+    )
     attended = flash(
         queries,
         jnp.where(suffix_weights, 0.0, NEGATIVE_MASK).astype(jnp.float32),

time: 435 us -> 428 us (0.984)
  Pallas kernels: 63 us -> 53.1 us
    pallas_call x2, Pallas kernels: 63 us -> 53.1 us  [flash(): pl.pallas_call(kern, grid_spec=grid_spec, out_shape=out_shape)]
  transfers between devices with their start and end apart: 6 -> 6, of which waited for: 5 -> 5; matrix products, arithmetic and copies ran while one was open for 15% -> 16% of each run, Pallas kernels for 12% -> 10%
where the time goes in v9:
time: 428 us; the launch traced here: 424 us
  waiting for transfers between devices  245 us (57%)
  matrix products  68.4 us (16%)
  Pallas kernels  53.1 us (12%)
  starting transfers between devices  29.3 us (7%)
  between operations  13.7 us (3%)
  other arithmetic  8.25 us (2%)
  local copies, waits for them, and re-layouts  5.87 us (1%)
    all_to_all x2, waiting for transfers between devices, on_device(): lax.all_to_all(outgoing, ('req', 'exp'), split_axis=0, concat_axis=0, til...  99.6 us
    all_to_all x2, waiting for transfers between devices, on_device(): lax.all_to_all(jnp.dot(inner, w_down[0], preferred_element_type=jnp.float...  95.8 us
    pallas_call x2, Pallas kernels, flash(): pl.pallas_call(kern, grid_spec=grid_spec, out_shape=out_shape)  53.1 us
    all_gather x1, waiting for transfers between devices, on_device(): lax.all_gather(page_pool, 'req', axis=0, tiled=True)  49.1 us
    all_to_all x2, starting transfers between devices, on_device(): lax.all_to_all(outgoing, ('req', 'exp'), split_axis=0, concat_axis=0, til...  16.2 us
    dot_general x2, matrix products, on_device(): up_part = jnp.dot(flat_rows, w_up[0], preferred_element_type=jnp.float32)  14.9 us
    dot_general x2, matrix products, on_device(): jnp.dot(flat_rows, w_gate[0], preferred_element_type=jnp.float32)  14.4 us
    all_to_all x2, starting transfers between devices, on_device(): lax.all_to_all(jnp.dot(inner, w_down[0], preferred_element_type=jnp.float...  13.1 us
  transfers between devices with their start and end apart: 6, of which 5 were waited for; matrix products, arithmetic and copies ran while one was open for 16% of the time, Pallas kernels for 10%

profile of v9, /device:TPU:34, one launch (start us, length us, event | category | flops | bytes accessed | tf_op | source)
XLA Modules:
  0.0 424.0 jit_solution(2151110868970119458)
XLA Ops:
  6.5 0.7 all-gather.3.cloned.1.call-update
  7.3 49.1 %all-gather.3.cloned.1.call-done = bf16[56,128,512]{2,1,0:T(8,128)(2,1)} async-done(((bf16[7,128,512]{2,1,0:T(8,128)(2,1)}), bf16[56,128,512]{2,1,0:T(8,128)(2,1)}) %all-gather.3.cloned.1.call-update) | async-done | bytes 7340048 | tf_op jit(solution)/shard_map/all_gather | solution.py:175
  56.4 0.8 reduce-window.21
  57.3 0.1 convert_reduce_fusion.1
  57.4 0.8 convert_reduce_fusion
  58.1 0.3 multiply_select_fusion
  58.5 0.1 copy.30
  58.7 0.1 copy.31
  58.8 0.1 copy.32
  58.9 1.0 broadcast_in_dim.138
  60.0 2.5 copy.35
  62.5 0.6 fusion.64
  63.1 1.2 compare_convert_fusion.flags_ref
  64.4 0.8 add_reduce_fusion
  65.2 0.7 select_reduce_fusion.3.order_ref
  65.9 0.3 select_reduce_fusion
  66.3 0.5 compare_convert_fusion.1.flags_ref
  66.8 0.2 convolution_convert_fusion.4
  67.0 0.1 fusion.56
  67.1 1.4 fusion.53.refs_0_
  68.5 0.9 broadcast_7_refs_8__refs_9_.2.refs_8_.refs_9_
  69.4 0.9 broadcast_in_dim.139.refs_10_
  70.3 41.4 %shard_map.118 = (f32[2,640,1]{2,1,0:T(8,128)}, f32[2,640,1]{2,1,0:T(8,128)}, f32[2,640,128]{2,1,0:T(8,128)}) custom-call(s32[14]{0:T(128)} %compare_convert_fusion.flags_ref, s32[56]{0:T(128)} %select_reduce_fusion.3.order_ref, bf16[128,1280]{1,0:T(8,128)(2,1)} %q_ref.3, f32[128,7168]{1,0:T(8,128)} %bitcast.108, f32[128,7168]{1,0:T(8,128)} %bitcast.109, ...), custom_call_target="tpu_custom_call" | custom-call | tf_op jit(solution)/shard_map/pallas_call | solution.py:145
  111.8 11.6 %shard_map.119 = bf16[128,1280]{1,0:T(8,128)(2,1)} custom-call(s32[4]{0:T(128)} %compare_convert_fusion.1.flags_ref, s32[1]{0:T(128)} %constant.14.clone.1.order_ref, bf16[128,1280]{1,0:T(8,128)(2,1)} %q_ref.3, f32[128,2048]{1,0:T(8,128)} %fusion.53.refs_0_, bf16[2048,512]{1,0:T(8,128)(2,1)} %all-gather.5.cloned.1.call-done.refs_1_, ...), custom_call_target="tpu_custom_call" | custom-call | tf_op jit(solution)/shard_map/pallas_call | solution.py:145
  123.4 4.0 fusion.38
  127.4 0.2 fusion.50
  127.7 3.9 fusion.16
  131.7 9.6 %all-to-all-start = ((bf16[128,8,2560]{2,1,0:T(8,128)(2,1)}), bf16[128,8,2560]{2,1,0:T(8,128)(2,1)}, u32[]{:S(2)}, u32[]{:S(2)}) async-start(bf16[128,8,2560]{2,1,0:T(8,128)(2,1)} %fusion.16), calls=%async_computation | async-start | bytes 10485760 | tf_op jit(solution)/shard_map/all_to_all | solution.py:269
  141.3 3.9 fusion.17
  145.2 58.2 %all-to-all-done = bf16[128,8,2560]{2,1,0:T(8,128)(2,1)} async-done(((bf16[128,8,2560]{2,1,0:T(8,128)(2,1)}), bf16[128,8,2560]{2,1,0:T(8,128)(2,1)}, u32[]{:S(2)}, u32[]{:S(2)}) %all-to-all-start) | async-done | bytes 5242912 | tf_op jit(solution)/shard_map/all_to_all | solution.py:269
  203.4 6.5 %all-to-all-start.2 = ((bf16[128,8,2560]{2,1,0:T(8,128)(2,1)}), bf16[128,8,2560]{2,1,0:T(8,128)(2,1)}, u32[]{:S(2)}, u32[]{:S(2)}) async-start(bf16[128,8,2560]{2,1,0:T(8,128)(2,1)} %fusion.17), calls=%async_computation.2 | async-start | bytes 10485760 | tf_op jit(solution)/shard_map/all_to_all | solution.py:269
  210.0 7.5 %fusion.12 = f32[1024,768]{1,0:T(8,128)S(1)} fusion(bf16[128,8,2560]{2,1,0:T(8,128)(2,1)} %all-to-all-done, bf16[1,2560,768]{2,1,0:T(8,128)(2,1)} %param.22), kind=kOutput, calls=%fused_computation.16 | convolution fusion | flops 4026531840 | bytes 12320768 | tf_op jit(solution)/shard_map/dot_general | solution.py:272
  217.5 7.2 %multiply_convert_fusion.1 = bf16[1024,768]{1,0:T(8,128)(2,1)S(1)} fusion(f32[1024,768]{1,0:T(8,128)S(1)} %fusion.12, bf16[1,2560,768]{2,1,0:T(8,128)(2,1)S(1)} %copy-done.3, bf16[128,8,2560]{2,1,0:T(8,128)(2,1)} %all-to-all-done), kind=kOutput, calls=%fused_computation.39 | convolution fusion | flops 4031250432 | bytes 13893632 | tf_op jit(solution)/shard_map/dot_general | solution.py:271
  224.7 6.0 %fusion.18 = bf16[128,8,2560]{2,1,0:T(8,128)(2,1)} fusion(bf16[1024,768]{1,0:T(8,128)(2,1)S(1)} %multiply_convert_fusion.1, bf16[1,768,2560]{2,1,0:T(8,128)(2,1)S(1)} %copy-done.5), kind=kOutput, calls=%fused_computation.22 | convolution fusion | flops 4029153280 | bytes 10747904 | tf_op jit(solution)/shard_map/dot_general | solution.py:275
  230.7 41.4 %all-to-all-done.2 = bf16[128,8,2560]{2,1,0:T(8,128)(2,1)} async-done(((bf16[128,8,2560]{2,1,0:T(8,128)(2,1)}), bf16[128,8,2560]{2,1,0:T(8,128)(2,1)}, u32[]{:S(2)}, u32[]{:S(2)}) %all-to-all-start.2) | async-done | bytes 5242912 | tf_op jit(solution)/shard_map/all_to_all | solution.py:269
  272.1 6.6 %all-to-all-start.1 = ((bf16[128,8,2560]{2,1,0:T(8,128)(2,1)}), bf16[128,8,2560]{2,1,0:T(8,128)(2,1)}, u32[]{:S(2)}, u32[]{:S(2)}) async-start(bf16[128,8,2560]{2,1,0:T(8,128)(2,1)} %fusion.18), calls=%async_computation.1 | async-start | bytes 10485760 | tf_op jit(solution)/shard_map/all_to_all | solution.py:274
  278.7 7.5 %fusion.4 = f32[1024,768]{1,0:T(8,128)S(1)} fusion(bf16[128,8,2560]{2,1,0:T(8,128)(2,1)} %all-to-all-done.2, bf16[1,2560,768]{2,1,0:T(8,128)(2,1)} %param.22), kind=kOutput, calls=%fused_computation.8 | convolution fusion | flops 4026531840 | bytes 12320768 | tf_op jit(solution)/shard_map/dot_general | solution.py:272
  286.2 7.2 %multiply_convert_fusion = bf16[1024,768]{1,0:T(8,128)(2,1)S(1)} fusion(f32[1024,768]{1,0:T(8,128)S(1)} %fusion.4, bf16[1,2560,768]{2,1,0:T(8,128)(2,1)S(1)} %copy-done.4, bf16[128,8,2560]{2,1,0:T(8,128)(2,1)} %all-to-all-done.2), kind=kOutput, calls=%fused_computation.38 | convolution fusion | flops 4031250432 | bytes 13893632 | tf_op jit(solution)/shard_map/dot_general | solution.py:271
  293.4 6.0 %fusion.19 = bf16[128,8,2560]{2,1,0:T(8,128)(2,1)} fusion(bf16[1024,768]{1,0:T(8,128)(2,1)S(1)} %multiply_convert_fusion, bf16[1,768,2560]{2,1,0:T(8,128)(2,1)S(1)} %copy-done.6), kind=kOutput, calls=%fused_computation.23 | convolution fusion | flops 4029153280 | bytes 10747904 | tf_op jit(solution)/shard_map/dot_general | solution.py:275
  299.5 41.4 %all-to-all-done.1 = bf16[128,8,2560]{2,1,0:T(8,128)(2,1)} async-done(((bf16[128,8,2560]{2,1,0:T(8,128)(2,1)}), bf16[128,8,2560]{2,1,0:T(8,128)(2,1)}, u32[]{:S(2)}, u32[]{:S(2)}) %all-to-all-start.1) | async-done | bytes 5242912 | tf_op jit(solution)/shard_map/all_to_all | solution.py:274
  340.8 6.5 %all-to-all-start.3 = ((bf16[128,8,2560]{2,1,0:T(8,128)(2,1)}), bf16[128,8,2560]{2,1,0:T(8,128)(2,1)}, u32[]{:S(2)}, u32[]{:S(2)}) async-start(bf16[128,8,2560]{2,1,0:T(8,128)(2,1)} %fusion.19), calls=%async_computation.3 | async-start | bytes 10485760 | tf_op jit(solution)/shard_map/all_to_all | solution.py:274
  347.4 0.4 fusion.68
  347.9 0.1 fusion.55
  348.2 3.4 fusion.26
  351.6 3.4 fusion.29
  355.0 54.5 %all-to-all-done.3 = bf16[128,8,2560]{2,1,0:T(8,128)(2,1)} async-done(((bf16[128,8,2560]{2,1,0:T(8,128)(2,1)}), bf16[128,8,2560]{2,1,0:T(8,128)(2,1)}, u32[]{:S(2)}, u32[]{:S(2)}) %all-to-all-start.3) | async-done | bytes 5242912 | tf_op jit(solution)/shard_map/all_to_all | solution.py:274
  409.5 3.4 fusion.32
  412.9 4.2 fusion.39
  (43 shorter events, 0.9 us)
Async XLA Ops:
  6.5 340.8 %copy-start = (bf16[2560,64]{0,1:T(8,128)(2,1)S(1)}, bf16[2560,64]{0,1:T(8,128)(2,1)}, u32[]{:S(2)}) copy-start(bf16[2560,64]{0,1:T(8,128)(2,1)} %param.19) | copy-start | bytes 983044
  6.5 49.9 %all-gather.3.cloned.1.call-start = ((), (), s32[]{:S(2)}) async-start(), calls=%async_computation.4 | async-start | bytes 8257536 | tf_op jit(solution)/shard_map/all_gather | solution.py:175
  7.3 104.5 %all-gather.5.cloned.1.call-start = ((), (), s32[]{:S(2)}) async-start(), calls=%async_computation.5 | async-start | bytes 2228224 | tf_op jit(solution)/shard_map/all_gather | solution.py:179
  60.0 5.9 %copy-start.7 = (s32[1,4]{1,0:T(1,128)S(1)}, s32[1,4]{1,0:T(1,128)}, u32[]{:S(2)}) copy-start(s32[1,4]{1,0:T(1,128)} %param.15) | copy-start | bytes 52
  60.0 6.0 %copy-start.2 = (s32[128,6]{0,1:T(8,128)S(1)}, s32[128,6]{0,1:T(8,128)}, u32[]{:S(2)}) copy-start(s32[128,6]{0,1:T(8,128)} %param.20) | copy-start | bytes 9220
  111.7 11.7 %copy-start.1 = (bf16[128,2560]{1,0:T(8,128)(2,1)S(1)}, bf16[128,2560]{1,0:T(8,128)(2,1)}, u32[]{:S(2)}) copy-start(bf16[128,2560]{1,0:T(8,128)(2,1)} %param.12) | copy-start | bytes 1966084
  131.7 71.8 %all-to-all-start = ((bf16[128,8,2560]{2,1,0:T(8,128)(2,1)}), bf16[128,8,2560]{2,1,0:T(8,128)(2,1)}, u32[]{:S(2)}, u32[]{:S(2)}) async-start(bf16[128,8,2560]{2,1,0:T(8,128)(2,1)} %fusion.16), calls=%async_computation | async-start | bytes 10485760 | tf_op jit(solution)/shard_map/all_to_all | solution.py:269
  203.4 68.7 %all-to-all-start.2 = ((bf16[128,8,2560]{2,1,0:T(8,128)(2,1)}), bf16[128,8,2560]{2,1,0:T(8,128)(2,1)}, u32[]{:S(2)}, u32[]{:S(2)}) async-start(bf16[128,8,2560]{2,1,0:T(8,128)(2,1)} %fusion.17), calls=%async_computation.2 | async-start | bytes 10485760 | tf_op jit(solution)/shard_map/all_to_all | solution.py:269
  210.0 7.5 %copy-start.3 = (bf16[1,2560,768]{2,1,0:T(8,128)(2,1)S(1)}, bf16[1,2560,768]{2,1,0:T(8,128)(2,1)}, u32[]{:S(2)}) copy-start(bf16[1,2560,768]{2,1,0:T(8,128)(2,1)} %param.21) | copy-start | bytes 11796484
  217.5 7.2 %copy-start.5 = (bf16[1,768,2560]{2,1,0:T(8,128)(2,1)S(1)}, bf16[1,768,2560]{2,1,0:T(8,128)(2,1)}, u32[]{:S(2)}) copy-start(bf16[1,768,2560]{2,1,0:T(8,128)(2,1)} %param.23) | copy-start | bytes 11796484
  272.1 68.7 %all-to-all-start.1 = ((bf16[128,8,2560]{2,1,0:T(8,128)(2,1)}), bf16[128,8,2560]{2,1,0:T(8,128)(2,1)}, u32[]{:S(2)}, u32[]{:S(2)}) async-start(bf16[128,8,2560]{2,1,0:T(8,128)(2,1)} %fusion.18), calls=%async_computation.1 | async-start | bytes 10485760 | tf_op jit(solution)/shard_map/all_to_all | solution.py:274
  278.7 7.5 %copy-start.4 = (bf16[1,2560,768]{2,1,0:T(8,128)(2,1)S(1)}, bf16[1,2560,768]{2,1,0:T(8,128)(2,1)}, u32[]{:S(2)}) copy-start(bf16[1,2560,768]{2,1,0:T(8,128)(2,1)} %param.21) | copy-start | bytes 11796484
  286.2 7.2 %copy-start.6 = (bf16[1,768,2560]{2,1,0:T(8,128)(2,1)S(1)}, bf16[1,768,2560]{2,1,0:T(8,128)(2,1)}, u32[]{:S(2)}) copy-start(bf16[1,768,2560]{2,1,0:T(8,128)(2,1)} %param.23) | copy-start | bytes 11796484
  340.8 68.7 %all-to-all-start.3 = ((bf16[128,8,2560]{2,1,0:T(8,128)(2,1)}), bf16[128,8,2560]{2,1,0:T(8,128)(2,1)}, u32[]{:S(2)}, u32[]{:S(2)}) async-start(bf16[128,8,2560]{2,1,0:T(8,128)(2,1)} %fusion.19), calls=%async_computation.3 | async-start | bytes 10485760 | tf_op jit(solution)/shard_map/all_to_all | solution.py:274
Sparse Core Ops, SparseCore 0:
  9.0 47.3 all-gather.2
  58.5 43.8 all-gather.4

commit v10 on v9

--- a/solution.py
+++ b/solution.py
@@ -27,8 +27,10 @@
 def attn_kernel(flags_ref, order_ref, q_ref, *refs, parts, first_call, last_call, groups, reps, hs):
     w_refs = refs[:parts]
     kv_refs = refs[parts:2 * parts]
-    m_in, l_in, acc_in = refs[2 * parts:2 * parts + 3]
-    refs = refs[2 * parts + 3:]
+    carried = 0 if first_call else 3
+    if not first_call:
+        m_in, l_in, acc_in = refs[2 * parts:2 * parts + 3]
+    refs = refs[2 * parts + carried:]
     if last_call:
         o_ref, qs, m_ref, l_ref, acc_ref = refs
     else:
@@ -130,7 +132,10 @@
     grid_spec = pltpu.PrefetchScalarGridSpec(
         num_scalar_prefetch=2,
         grid=(n_blocks,),
-        in_specs=[pl.BlockSpec((t, width), lambda j, f, o: (0, 0))] + w_specs + kv_specs + state_specs,
+        in_specs=[pl.BlockSpec((t, width), lambda j, f, o: (0, 0))]
+        + w_specs
+        + kv_specs
+        + ([] if first_call else state_specs),
         out_specs=out_specs,
         scratch_shapes=[
             pltpu.VMEM((groups, reps * t, hs), jnp.bfloat16),
@@ -139,9 +144,9 @@
             pltpu.VMEM((groups, reps * t, hs), jnp.float32),
         ],
     )
-    if carry is None:
-        carry = tuple(jnp.zeros(s.shape, s.dtype) for s in state)
-    operands = [queries] + [bias] * len(w_specs) + [kv_rows] * len(kv_specs) + list(carry)
+    operands = [queries] + [bias] * len(w_specs) + [kv_rows] * len(kv_specs)
+    if not first_call:
+        operands += list(carry)
     return pl.pallas_call(kern, grid_spec=grid_spec, out_shape=out_shape)(flags, order, *operands)
 
 
@@ -186,10 +191,16 @@
     query_counts = jnp.dot(pick.astype(jnp.float32), counts, precision=lax.Precision.HIGHEST)
     keypos = jnp.arange(segment.shape[0], dtype=jnp.int32)
     suffix_weights = (keypos[None, :] <= positions[:, None]) & (keypos[None, :] >= first[:, None])
-    pool_bias = jnp.where(
-        query_counts > 0, jnp.log2(jnp.maximum(query_counts, 1.0)), NEGATIVE_MASK
-    )
-    pool_weights = jnp.repeat(pool_bias, PAGE_TOKENS, axis=1)
+    spread = (
+        jnp.arange(pool_all, dtype=jnp.int32)[:, None]
+        == jnp.arange(pool_all * PAGE_TOKENS, dtype=jnp.int32)[None, :] // PAGE_TOKENS
+    ).astype(jnp.bfloat16)
+    key_counts = jnp.dot(
+        query_counts.astype(jnp.bfloat16), spread, preferred_element_type=jnp.float32
+    )
+    pool_weights = jnp.where(
+        key_counts > 0, jnp.log2(jnp.maximum(key_counts, 1.0)), NEGATIVE_MASK
+    )
     live = jnp.max(query_counts, axis=0) > 0
     live_int = live.astype(jnp.int32)
     live_count = jnp.sum(live_int)

time: 428 us -> 426 us (level)
  starting transfers between devices: 29.3 us -> 43.4 us
  Pallas kernels: 53.1 us -> 39.9 us
  local copies, waits for them, and re-layouts: 5.87 us -> 0.44 us
    all_to_all x2, starting transfers between devices: 16.2 us -> 30.3 us  [on_device(): lax.all_to_all(outgoing, ('req', 'exp'), split_axis=0, concat_axis=0, til...]
    pallas_call x2, Pallas kernels: 53.1 us -> 39.9 us  [flash(): pl.pallas_call(kern, grid_spec=grid_spec, out_shape=out_shape)]
  transfers between devices with their start and end apart: 6 -> 6, of which waited for: 5 -> 6; matrix products, arithmetic and copies ran while one was open for 16% -> 15% of each run, Pallas kernels for 10% -> 7%
where the time goes in v10:
time: 426 us; the launch traced here: 425 us
  waiting for transfers between devices  247 us (58%)
  matrix products  71.7 us (17%)
  starting transfers between devices  43.4 us (10%)
  Pallas kernels  39.9 us (9%)
  between operations  13.7 us (3%)
  other arithmetic  9.59 us (2%)
    all_to_all x2, waiting for transfers between devices, on_device(): lax.all_to_all(outgoing, ('req', 'exp'), split_axis=0, concat_axis=0, til...  99.6 us
    all_to_all x2, waiting for transfers between devices, on_device(): lax.all_to_all(jnp.dot(inner, w_down[0], preferred_element_type=jnp.float...  95.9 us
    all_gather x1, waiting for transfers between devices, on_device(): lax.all_gather(page_pool, 'req', axis=0, tiled=True)  47.5 us
    pallas_call x2, Pallas kernels, flash(): pl.pallas_call(kern, grid_spec=grid_spec, out_shape=out_shape)  39.9 us
    all_to_all x2, starting transfers between devices, on_device(): lax.all_to_all(outgoing, ('req', 'exp'), split_axis=0, concat_axis=0, til...  30.3 us
    dot_general x2, matrix products, on_device(): up_part = jnp.dot(flat_rows, w_up[0], preferred_element_type=jnp.float32)  14.9 us
    dot_general x2, matrix products, on_device(): jnp.dot(flat_rows, w_gate[0], preferred_element_type=jnp.float32)  14.4 us
    all_to_all x2, starting transfers between devices, on_device(): lax.all_to_all(jnp.dot(inner, w_down[0], preferred_element_type=jnp.float...  13.1 us
  transfers between devices with their start and end apart: 6, of which 6 were waited for; matrix products, arithmetic and copies ran while one was open for 15% of the time, Pallas kernels for 7%

profile of v10, /device:TPU:34, one launch (start us, length us, event | category | flops | bytes accessed | tf_op | source)
XLA Modules:
  0.0 425.3 jit_solution(9151589550981139236)
XLA Ops:
  6.5 0.7 all-gather.3.cloned.1.call-update
  7.3 0.8 reduce-window.21
  8.1 0.8 convert_reduce_fusion
  8.9 47.5 %all-gather.3.cloned.1.call-done = bf16[56,128,512]{2,1,0:T(8,128)(2,1)} async-done(((bf16[7,128,512]{2,1,0:T(8,128)(2,1)}), bf16[56,128,512]{2,1,0:T(8,128)(2,1)}) %all-gather.3.cloned.1.call-update) | async-done | bytes 7340048 | tf_op jit(solution)/shard_map/all_gather | solution.py:180
  56.5 0.3 fusion.75
  56.8 0.1 copy.28
  56.9 0.1 reduce-window.23
  57.0 0.1 copy.27
  57.2 0.6 fusion.69
  57.9 1.2 compare_convert_fusion.flags_ref
  59.0 0.8 add_reduce_fusion
  59.8 0.7 select_reduce_fusion.3.order_ref
  60.5 0.7 fusion.67
  61.2 0.1 select_reduce_fusion.4
  61.3 0.7 fusion.58
  62.0 0.3 select_reduce_fusion
  62.3 0.5 compare_convert_fusion.1.flags_ref
  62.9 0.1 convolution_convert_fusion.4
  63.0 0.1 fusion.57
  63.1 3.3 multiply_select_fusion.refs_0_.refs_1_.refs_2_.refs_3_
  66.4 1.4 fusion.53.refs_0_
  67.8 31.8 %shard_map.118 = (f32[2,640,1]{2,1,0:T(8,128)}, f32[2,640,1]{2,1,0:T(8,128)}, f32[2,640,128]{2,1,0:T(8,128)}) custom-call(s32[14]{0:T(128)} %compare_convert_fusion.flags_ref, s32[56]{0:T(128)} %select_reduce_fusion.3.order_ref, bf16[128,1280]{1,0:T(8,128)(2,1)} %q_ref.3, f32[128,7168]{1,0:T(8,128)} %multiply_select_fusion.refs_0_.refs_1_.refs_2_.refs_3_, ...), custom_call_target="tpu_custom_call" | custom-call | tf_op jit(solution)/shard_map/pallas_call | solution.py:150
  99.6 2.8 all-gather.5.cloned.1.call-done.refs_1_
  102.4 8.2 %shard_map.119 = bf16[128,1280]{1,0:T(8,128)(2,1)} custom-call(s32[4]{0:T(128)} %compare_convert_fusion.1.flags_ref, s32[1]{0:T(128)} %constant.56.clone.1.order_ref, bf16[128,1280]{1,0:T(8,128)(2,1)} %q_ref.3, f32[128,2048]{1,0:T(8,128)} %fusion.53.refs_0_, bf16[2048,512]{1,0:T(8,128)(2,1)} %all-gather.5.cloned.1.call-done.refs_1_, ...), custom_call_target="tpu_custom_call" | custom-call | tf_op jit(solution)/shard_map/pallas_call | solution.py:150
  110.6 4.0 fusion.38
  114.6 0.2 fusion.50
  114.9 3.9 fusion.16
  118.8 23.7 %all-to-all-start = ((bf16[128,8,2560]{2,1,0:T(8,128)(2,1)}), bf16[128,8,2560]{2,1,0:T(8,128)(2,1)}, u32[]{:S(2)}, u32[]{:S(2)}) async-start(bf16[128,8,2560]{2,1,0:T(8,128)(2,1)} %fusion.16), calls=%async_computation | async-start | bytes 10485760 | tf_op jit(solution)/shard_map/all_to_all | solution.py:280
  142.6 3.9 fusion.17
  146.5 58.2 %all-to-all-done = bf16[128,8,2560]{2,1,0:T(8,128)(2,1)} async-done(((bf16[128,8,2560]{2,1,0:T(8,128)(2,1)}), bf16[128,8,2560]{2,1,0:T(8,128)(2,1)}, u32[]{:S(2)}, u32[]{:S(2)}) %all-to-all-start) | async-done | bytes 5242912 | tf_op jit(solution)/shard_map/all_to_all | solution.py:280
  204.7 6.5 %all-to-all-start.2 = ((bf16[128,8,2560]{2,1,0:T(8,128)(2,1)}), bf16[128,8,2560]{2,1,0:T(8,128)(2,1)}, u32[]{:S(2)}, u32[]{:S(2)}) async-start(bf16[128,8,2560]{2,1,0:T(8,128)(2,1)} %fusion.17), calls=%async_computation.2 | async-start | bytes 10485760 | tf_op jit(solution)/shard_map/all_to_all | solution.py:280
  211.2 7.5 %fusion.12 = f32[1024,768]{1,0:T(8,128)S(1)} fusion(bf16[128,8,2560]{2,1,0:T(8,128)(2,1)} %all-to-all-done, bf16[1,2560,768]{2,1,0:T(8,128)(2,1)} %param.22), kind=kOutput, calls=%fused_computation.16 | convolution fusion | flops 4026531840 | bytes 12320768 | tf_op jit(solution)/shard_map/dot_general | solution.py:283
  218.7 7.2 %multiply_convert_fusion.1 = bf16[1024,768]{1,0:T(8,128)(2,1)S(1)} fusion(f32[1024,768]{1,0:T(8,128)S(1)} %fusion.12, bf16[1,2560,768]{2,1,0:T(8,128)(2,1)S(1)} %copy-done.3, bf16[128,8,2560]{2,1,0:T(8,128)(2,1)} %all-to-all-done), kind=kOutput, calls=%fused_computation.39 | convolution fusion | flops 4031250432 | bytes 13893632 | tf_op jit(solution)/shard_map/dot_general | solution.py:282
  225.9 6.0 %fusion.18 = bf16[128,8,2560]{2,1,0:T(8,128)(2,1)} fusion(bf16[1024,768]{1,0:T(8,128)(2,1)S(1)} %multiply_convert_fusion.1, bf16[1,768,2560]{2,1,0:T(8,128)(2,1)S(1)} %copy-done.5), kind=kOutput, calls=%fused_computation.22 | convolution fusion | flops 4029153280 | bytes 10747904 | tf_op jit(solution)/shard_map/dot_general | solution.py:286
  231.9 41.4 %all-to-all-done.2 = bf16[128,8,2560]{2,1,0:T(8,128)(2,1)} async-done(((bf16[128,8,2560]{2,1,0:T(8,128)(2,1)}), bf16[128,8,2560]{2,1,0:T(8,128)(2,1)}, u32[]{:S(2)}, u32[]{:S(2)}) %all-to-all-start.2) | async-done | bytes 5242912 | tf_op jit(solution)/shard_map/all_to_all | solution.py:280
  273.4 6.6 %all-to-all-start.1 = ((bf16[128,8,2560]{2,1,0:T(8,128)(2,1)}), bf16[128,8,2560]{2,1,0:T(8,128)(2,1)}, u32[]{:S(2)}, u32[]{:S(2)}) async-start(bf16[128,8,2560]{2,1,0:T(8,128)(2,1)} %fusion.18), calls=%async_computation.1 | async-start | bytes 10485760 | tf_op jit(solution)/shard_map/all_to_all | solution.py:285
  280.0 7.5 %fusion.4 = f32[1024,768]{1,0:T(8,128)S(1)} fusion(bf16[128,8,2560]{2,1,0:T(8,128)(2,1)} %all-to-all-done.2, bf16[1,2560,768]{2,1,0:T(8,128)(2,1)} %param.22), kind=kOutput, calls=%fused_computation.8 | convolution fusion | flops 4026531840 | bytes 12320768 | tf_op jit(solution)/shard_map/dot_general | solution.py:283
  287.5 7.2 %multiply_convert_fusion = bf16[1024,768]{1,0:T(8,128)(2,1)S(1)} fusion(f32[1024,768]{1,0:T(8,128)S(1)} %fusion.4, bf16[1,2560,768]{2,1,0:T(8,128)(2,1)S(1)} %copy-done.4, bf16[128,8,2560]{2,1,0:T(8,128)(2,1)} %all-to-all-done.2), kind=kOutput, calls=%fused_computation.38 | convolution fusion | flops 4031250432 | bytes 13893632 | tf_op jit(solution)/shard_map/dot_general | solution.py:282
  294.7 6.0 %fusion.19 = bf16[128,8,2560]{2,1,0:T(8,128)(2,1)} fusion(bf16[1024,768]{1,0:T(8,128)(2,1)S(1)} %multiply_convert_fusion, bf16[1,768,2560]{2,1,0:T(8,128)(2,1)S(1)} %copy-done.6), kind=kOutput, calls=%fused_computation.23 | convolution fusion | flops 4029153280 | bytes 10747904 | tf_op jit(solution)/shard_map/dot_general | solution.py:286
  300.7 41.4 %all-to-all-done.1 = bf16[128,8,2560]{2,1,0:T(8,128)(2,1)} async-done(((bf16[128,8,2560]{2,1,0:T(8,128)(2,1)}), bf16[128,8,2560]{2,1,0:T(8,128)(2,1)}, u32[]{:S(2)}, u32[]{:S(2)}) %all-to-all-start.1) | async-done | bytes 5242912 | tf_op jit(solution)/shard_map/all_to_all | solution.py:285
  342.1 6.5 %all-to-all-start.3 = ((bf16[128,8,2560]{2,1,0:T(8,128)(2,1)}), bf16[128,8,2560]{2,1,0:T(8,128)(2,1)}, u32[]{:S(2)}, u32[]{:S(2)}) async-start(bf16[128,8,2560]{2,1,0:T(8,128)(2,1)} %fusion.19), calls=%async_computation.3 | async-start | bytes 10485760 | tf_op jit(solution)/shard_map/all_to_all | solution.py:285
  348.6 0.4 fusion.73
  349.2 0.1 fusion.56
  349.4 3.4 fusion.26
  352.9 3.4 fusion.29
  356.2 54.5 %all-to-all-done.3 = bf16[128,8,2560]{2,1,0:T(8,128)(2,1)} async-done(((bf16[128,8,2560]{2,1,0:T(8,128)(2,1)}), bf16[128,8,2560]{2,1,0:T(8,128)(2,1)}, u32[]{:S(2)}, u32[]{:S(2)}) %all-to-all-start.3) | async-done | bytes 5242912 | tf_op jit(solution)/shard_map/all_to_all | solution.py:285
  410.8 3.4 fusion.32
  414.2 4.2 fusion.39
  (38 shorter events, 0.7 us)
Async XLA Ops:
  6.5 342.1 %copy-start = (bf16[2560,64]{0,1:T(8,128)(2,1)S(1)}, bf16[2560,64]{0,1:T(8,128)(2,1)}, u32[]{:S(2)}) copy-start(bf16[2560,64]{0,1:T(8,128)(2,1)} %param.19) | copy-start | bytes 983044
  6.5 49.9 %all-gather.3.cloned.1.call-start = ((), (), s32[]{:S(2)}) async-start(), calls=%async_computation.4 | async-start | bytes 8257536 | tf_op jit(solution)/shard_map/all_gather | solution.py:180
  7.3 95.2 %all-gather.5.cloned.1.call-start = ((), (), s32[]{:S(2)}) async-start(), calls=%async_computation.5 | async-start | bytes 2228224 | tf_op jit(solution)/shard_map/all_gather | solution.py:184
  99.6 11.0 %copy-start.1 = (bf16[128,2560]{1,0:T(8,128)(2,1)S(1)}, bf16[128,2560]{1,0:T(8,128)(2,1)}, u32[]{:S(2)}) copy-start(bf16[128,2560]{1,0:T(8,128)(2,1)} %param.12) | copy-start | bytes 1966084
  118.8 85.9 %all-to-all-start = ((bf16[128,8,2560]{2,1,0:T(8,128)(2,1)}), bf16[128,8,2560]{2,1,0:T(8,128)(2,1)}, u32[]{:S(2)}, u32[]{:S(2)}) async-start(bf16[128,8,2560]{2,1,0:T(8,128)(2,1)} %fusion.16), calls=%async_computation | async-start | bytes 10485760 | tf_op jit(solution)/shard_map/all_to_all | solution.py:280
  204.7 68.7 %all-to-all-start.2 = ((bf16[128,8,2560]{2,1,0:T(8,128)(2,1)}), bf16[128,8,2560]{2,1,0:T(8,128)(2,1)}, u32[]{:S(2)}, u32[]{:S(2)}) async-start(bf16[128,8,2560]{2,1,0:T(8,128)(2,1)} %fusion.17), calls=%async_computation.2 | async-start | bytes 10485760 | tf_op jit(solution)/shard_map/all_to_all | solution.py:280
  211.2 7.5 %copy-start.3 = (bf16[1,2560,768]{2,1,0:T(8,128)(2,1)S(1)}, bf16[1,2560,768]{2,1,0:T(8,128)(2,1)}, u32[]{:S(2)}) copy-start(bf16[1,2560,768]{2,1,0:T(8,128)(2,1)} %param.21) | copy-start | bytes 11796484
  218.7 7.2 %copy-start.5 = (bf16[1,768,2560]{2,1,0:T(8,128)(2,1)S(1)}, bf16[1,768,2560]{2,1,0:T(8,128)(2,1)}, u32[]{:S(2)}) copy-start(bf16[1,768,2560]{2,1,0:T(8,128)(2,1)} %param.23) | copy-start | bytes 11796484
  273.4 68.7 %all-to-all-start.1 = ((bf16[128,8,2560]{2,1,0:T(8,128)(2,1)}), bf16[128,8,2560]{2,1,0:T(8,128)(2,1)}, u32[]{:S(2)}, u32[]{:S(2)}) async-start(bf16[128,8,2560]{2,1,0:T(8,128)(2,1)} %fusion.18), calls=%async_computation.1 | async-start | bytes 10485760 | tf_op jit(solution)/shard_map/all_to_all | solution.py:285
  279.9 7.5 %copy-start.4 = (bf16[1,2560,768]{2,1,0:T(8,128)(2,1)S(1)}, bf16[1,2560,768]{2,1,0:T(8,128)(2,1)}, u32[]{:S(2)}) copy-start(bf16[1,2560,768]{2,1,0:T(8,128)(2,1)} %param.21) | copy-start | bytes 11796484
  287.4 7.2 %copy-start.6 = (bf16[1,768,2560]{2,1,0:T(8,128)(2,1)S(1)}, bf16[1,768,2560]{2,1,0:T(8,128)(2,1)}, u32[]{:S(2)}) copy-start(bf16[1,768,2560]{2,1,0:T(8,128)(2,1)} %param.23) | copy-start | bytes 11796484
  300.7 48.3 %copy-start.2 = (s32[128,6]{0,1:T(8,128)S(1)}, s32[128,6]{0,1:T(8,128)}, u32[]{:S(2)}) copy-start(s32[128,6]{0,1:T(8,128)} %param.20) | copy-start | bytes 9220
  342.1 68.7 %all-to-all-start.3 = ((bf16[128,8,2560]{2,1,0:T(8,128)(2,1)}), bf16[128,8,2560]{2,1,0:T(8,128)(2,1)}, u32[]{:S(2)}, u32[]{:S(2)}) async-start(bf16[128,8,2560]{2,1,0:T(8,128)(2,1)} %fusion.19), calls=%async_computation.3 | async-start | bytes 10485760 | tf_op jit(solution)/shard_map/all_to_all | solution.py:285
Sparse Core Ops, SparseCore 0:
  9.0 47.3 all-gather.2
  58.5 43.8 all-gather.4

commit v11 on v10

--- a/solution.py
+++ b/solution.py
@@ -177,10 +177,12 @@
     req_of = jnp.sum((positions[:, None] >= ends[None, :]).astype(jnp.int32), axis=1)
     pick = req_of[:, None] == jnp.arange(lens.shape[0], dtype=jnp.int32)[None, :]
     first = jnp.sum(jnp.where(pick, starts[None, :], 0), axis=1)
-    pool_rows = lax.all_gather(page_pool, "req", axis=0, tiled=True).reshape(
-        pool_all * PAGE_TOKENS, 2 * row_width
-    )
-    pool_rows, suffix_after = lax.optimization_barrier((pool_rows, suffix_kv))
+    split = (pool_per_shard + 1) // 2
+    pool_first = lax.all_gather(page_pool[:split], "req", axis=0, tiled=True)
+    pool_first, pool_later, suffix_after = lax.optimization_barrier(
+        (pool_first, page_pool[split:], suffix_kv)
+    )
+    pool_second = lax.all_gather(pool_later, "req", axis=0, tiled=True)
     segment = lax.all_gather(suffix_after, "exp", axis=0, tiled=True)
     counts = jnp.sum(
         (page_table[0][:, :, None] == jnp.arange(pool_all, dtype=jnp.int32)[None, None, :]).astype(
@@ -191,38 +193,46 @@
     query_counts = jnp.dot(pick.astype(jnp.float32), counts, precision=lax.Precision.HIGHEST)
     keypos = jnp.arange(segment.shape[0], dtype=jnp.int32)
     suffix_weights = (keypos[None, :] <= positions[:, None]) & (keypos[None, :] >= first[:, None])
-    spread = (
-        jnp.arange(pool_all, dtype=jnp.int32)[:, None]
-        == jnp.arange(pool_all * PAGE_TOKENS, dtype=jnp.int32)[None, :] // PAGE_TOKENS
-    ).astype(jnp.bfloat16)
-    key_counts = jnp.dot(
-        query_counts.astype(jnp.bfloat16), spread, preferred_element_type=jnp.float32
-    )
-    pool_weights = jnp.where(
-        key_counts > 0, jnp.log2(jnp.maximum(key_counts, 1.0)), NEGATIVE_MASK
-    )
-    live = jnp.max(query_counts, axis=0) > 0
-    live_int = live.astype(jnp.int32)
-    live_count = jnp.sum(live_int)
-    destination = jnp.where(
-        live, jnp.cumsum(live_int) - 1, live_count + jnp.cumsum(1 - live_int) - 1
-    )
-    slots = jnp.arange(pool_all, dtype=jnp.int32)
-    order = jnp.sum(
-        jnp.where(destination[None, :] == slots[:, None], slots[None, :], 0), axis=1
-    ).astype(jnp.int32)
-    carry = flash(
-        queries,
-        pool_weights,
-        pool_rows,
-        None,
-        True,
-        False,
-        KEY_VALUE_HEADS,
-        HEAD_SIZE,
-        (order, live_count),
-        KEY_BLOCK // PAGE_TOKENS,
-    )
+    shard_counts = query_counts.reshape(token_index, request_count, pool_per_shard)
+    carry = None
+    for part_counts, rows in (
+        (shard_counts[:, :, :split], pool_first),
+        (shard_counts[:, :, split:], pool_second),
+    ):
+        part_counts = part_counts.reshape(token_index, -1)
+        pages = part_counts.shape[1]
+        spread = (
+            jnp.arange(pages, dtype=jnp.int32)[:, None]
+            == jnp.arange(pages * PAGE_TOKENS, dtype=jnp.int32)[None, :] // PAGE_TOKENS
+        ).astype(jnp.bfloat16)
+        key_counts = jnp.dot(
+            part_counts.astype(jnp.bfloat16), spread, preferred_element_type=jnp.float32
+        )
+        part_bias = jnp.where(
+            key_counts > 0, jnp.log2(jnp.maximum(key_counts, 1.0)), NEGATIVE_MASK
+        )
+        live = jnp.max(part_counts, axis=0) > 0
+        live_int = live.astype(jnp.int32)
+        live_count = jnp.sum(live_int)
+        destination = jnp.where(
+            live, jnp.cumsum(live_int) - 1, live_count + jnp.cumsum(1 - live_int) - 1
+        )
+        slots = jnp.arange(pages, dtype=jnp.int32)
+        order = jnp.sum(
+            jnp.where(destination[None, :] == slots[:, None], slots[None, :], 0), axis=1
+        ).astype(jnp.int32)
+        carry = flash(
+            queries,
+            part_bias,
+            rows.reshape(-1, 2 * row_width),
+            carry,
+            carry is None,
+            False,
+            KEY_VALUE_HEADS,
+            HEAD_SIZE,
+            (order, live_count),
+            KEY_BLOCK // PAGE_TOKENS,
+        )
     attended = flash(
         queries,
         jnp.where(suffix_weights, 0.0, NEGATIVE_MASK).astype(jnp.float32),

time: 426 us -> 433 us (1.016)
  starting transfers between devices: 43.4 us -> 33.6 us
  waiting for transfers between devices: 247 us -> 253 us
  local copies, waits for them, and re-layouts: 0.44 us -> 5.22 us
    all_gather x1, waiting for transfers between devices: 2.79 us -> 24.9 us  [on_device(): segment = lax.all_gather(suffix_after, 'exp', axis=0, tiled=True)]
    all_gather x1 -> x2, waiting for transfers between devices: 47.5 us -> 32.9 us  [the longest x1 32.9 us: on_device(): pool_first = lax.all_gather(page_pool[:split], 'req', axis=0, tiled=True)]
    all_to_all x2, starting transfers between devices: 30.3 us -> 20.4 us  [on_device(): lax.all_to_all(outgoing, ('req', 'exp'), split_axis=0, concat_axis=0, til...]
    pallas_call x2 -> x3, Pallas kernels: 39.9 us -> 41.8 us  [flash(): pl.pallas_call(kern, grid_spec=grid_spec, out_shape=out_shape)]
  transfers between devices with their start and end apart: 6 -> 7, of which waited for: 6 -> 6; matrix products, arithmetic and copies ran while one was open for 15% -> 16% of each run, Pallas kernels for 7% -> 8%
where the time goes in v11:
time: 433 us; the launch traced here: 431 us
  waiting for transfers between devices  253 us (58%)
  matrix products  72.2 us (17%)
  Pallas kernels  41.8 us (10%)
  starting transfers between devices  33.6 us (8%)
  between operations  13.4 us (3%)
  other arithmetic  11.6 us (3%)
  local copies, waits for them, and re-layouts  5.22 us (1%)
    all_to_all x2, waiting for transfers between devices, on_device(): lax.all_to_all(outgoing, ('req', 'exp'), split_axis=0, concat_axis=0, til...  99.6 us
    all_to_all x2, waiting for transfers between devices, on_device(): lax.all_to_all(jnp.dot(inner, w_down[0], preferred_element_type=jnp.float...  95.8 us
    pallas_call x3, Pallas kernels, flash(): pl.pallas_call(kern, grid_spec=grid_spec, out_shape=out_shape)  41.8 us
    all_gather x1, waiting for transfers between devices, on_device(): pool_first = lax.all_gather(page_pool[:split], 'req', axis=0, tiled=True)  32.9 us
    all_gather x1, waiting for transfers between devices, on_device(): segment = lax.all_gather(suffix_after, 'exp', axis=0, tiled=True)  24.9 us
    all_to_all x2, starting transfers between devices, on_device(): lax.all_to_all(outgoing, ('req', 'exp'), split_axis=0, concat_axis=0, til...  20.4 us
    dot_general x2, matrix products, on_device(): up_part = jnp.dot(flat_rows, w_up[0], preferred_element_type=jnp.float32)  14.9 us
    dot_general x2, matrix products, on_device(): jnp.dot(flat_rows, w_gate[0], preferred_element_type=jnp.float32)  14.4 us
  transfers between devices with their start and end apart: 7, of which 6 were waited for; matrix products, arithmetic and copies ran while one was open for 16% of the time, Pallas kernels for 8%

profile of v11, /device:TPU:34, one launch (start us, length us, event | category | flops | bytes accessed | tf_op | source)
XLA Modules:
  0.0 431.2 jit_solution(18115607197641669252)
XLA Ops:
  6.5 1.9 slice.26
  8.5 1.8 slice.27
  10.3 32.9 %all-gather.4.cloned.1.call-done = bf16[32,128,512]{2,1,0:T(8,128)(2,1)} async-done(((bf16[4,128,512]{2,1,0:T(8,128)(2,1)}), bf16[32,128,512]{2,1,0:T(8,128)(2,1)}) %all-gather.4.cloned.1.call-update) | async-done | bytes 4194320 | tf_op jit(solution)/shard_map/all_gather | solution.py:181
  43.3 0.8 convert_reduce_fusion
  44.3 0.8 reduce-window.37
  45.2 0.2 fusion.69
  47.0 0.6 convert_reduce_fusion.3
  47.6 0.8 add_reduce_fusion.2
  48.4 0.7 convert_reduce_fusion.2
  49.0 0.7 add_reduce_fusion
  49.8 1.2 compare_convert_fusion.1.flags_ref
  51.0 1.1 compare_convert_fusion.flags_ref
  52.1 0.7 select_reduce_fusion.4.order_ref
  52.8 0.6 select_reduce_fusion.3.order_ref
  53.5 0.3 select_reduce_fusion
  53.9 0.6 compare_convert_fusion.2.flags_ref
  54.4 0.1 convolution_convert_fusion.4
  54.6 0.1 fusion.56
  54.7 1.8 multiply_select_fusion.1.refs_0_.refs_1_.refs_2_.refs_3_
  56.5 2.1 multiply_select_fusion.refs_0_.refs_1_.refs_2_.refs_3_
  58.6 1.4 fusion.53.refs_0_
  60.0 20.0 %shard_map.118 = (f32[2,640,1]{2,1,0:T(8,128)}, f32[2,640,1]{2,1,0:T(8,128)}, f32[2,640,128]{2,1,0:T(8,128)}) custom-call(s32[8]{0:T(128)} %compare_convert_fusion.flags_ref, s32[32]{0:T(128)} %select_reduce_fusion.3.order_ref, bf16[128,1280]{1,0:T(8,128)(2,1)} %q_ref.5, f32[128,4096]{1,0:T(8,128)} %multiply_select_fusion.refs_0_.refs_1_.refs_2_.refs_3_, ...), custom_call_target="tpu_custom_call" | custom-call | tf_op jit(solution)/shard_map/pallas_call | solution.py:150
  80.0 13.6 %shard_map.119 = (f32[2,640,1]{2,1,0:T(8,128)}, f32[2,640,1]{2,1,0:T(8,128)}, f32[2,640,128]{2,1,0:T(8,128)}) custom-call(s32[6]{0:T(128)} %compare_convert_fusion.1.flags_ref, s32[24]{0:T(128)} %select_reduce_fusion.4.order_ref, bf16[128,1280]{1,0:T(8,128)(2,1)} %q_ref.5, f32[128,3072]{1,0:T(8,128)} %multiply_select_fusion.1.refs_0_.refs_1_.refs_2_.refs_3_, ...), custom_call_target="tpu_custom_call" | custom-call | tf_op jit(solution)/shard_map/pallas_call | solution.py:150
  93.6 24.9 %all-gather.6.cloned.1.call-done.refs_1_ = bf16[2048,512]{1,0:T(8,128)(2,1)} async-done(((bf16[128,512]{1,0:T(8,128)(2,1)}), bf16[2048,512]{1,0:T(8,128)(2,1)}) %all-gather.6.cloned.1.call-update) | async-done | bytes 2097168 | tf_op jit(solution)/shard_map/all_gather | solution.py:186
  118.5 8.2 %shard_map.120 = bf16[128,1280]{1,0:T(8,128)(2,1)} custom-call(s32[4]{0:T(128)} %compare_convert_fusion.2.flags_ref, s32[1]{0:T(128)} %constant.79.clone.1.order_ref, bf16[128,1280]{1,0:T(8,128)(2,1)} %q_ref.5, f32[128,2048]{1,0:T(8,128)} %fusion.53.refs_0_, bf16[2048,512]{1,0:T(8,128)(2,1)} %all-gather.6.cloned.1.call-done.refs_1_, ...), custom_call_target="tpu_custom_call" | custom-call | tf_op jit(solution)/shard_map/pallas_call | solution.py:150
  126.7 4.0 fusion.38
  130.7 0.2 fusion.50
  131.0 3.9 fusion.16
  134.9 13.9 %all-to-all-start = ((bf16[128,8,2560]{2,1,0:T(8,128)(2,1)}), bf16[128,8,2560]{2,1,0:T(8,128)(2,1)}, u32[]{:S(2)}, u32[]{:S(2)}) async-start(bf16[128,8,2560]{2,1,0:T(8,128)(2,1)} %fusion.16), calls=%async_computation | async-start | bytes 10485760 | tf_op jit(solution)/shard_map/all_to_all | solution.py:290
  148.8 3.9 fusion.17
  152.7 58.2 %all-to-all-done = bf16[128,8,2560]{2,1,0:T(8,128)(2,1)} async-done(((bf16[128,8,2560]{2,1,0:T(8,128)(2,1)}), bf16[128,8,2560]{2,1,0:T(8,128)(2,1)}, u32[]{:S(2)}, u32[]{:S(2)}) %all-to-all-start) | async-done | bytes 5242912 | tf_op jit(solution)/shard_map/all_to_all | solution.py:290
  211.0 6.5 %all-to-all-start.2 = ((bf16[128,8,2560]{2,1,0:T(8,128)(2,1)}), bf16[128,8,2560]{2,1,0:T(8,128)(2,1)}, u32[]{:S(2)}, u32[]{:S(2)}) async-start(bf16[128,8,2560]{2,1,0:T(8,128)(2,1)} %fusion.17), calls=%async_computation.2 | async-start | bytes 10485760 | tf_op jit(solution)/shard_map/all_to_all | solution.py:290
  217.5 7.5 %fusion.12 = f32[1024,768]{1,0:T(8,128)S(1)} fusion(bf16[128,8,2560]{2,1,0:T(8,128)(2,1)} %all-to-all-done, bf16[1,2560,768]{2,1,0:T(8,128)(2,1)} %param.22), kind=kOutput, calls=%fused_computation.16 | convolution fusion | flops 4026531840 | bytes 12320768 | tf_op jit(solution)/shard_map/dot_general | solution.py:293
  225.0 7.2 %multiply_convert_fusion.1 = bf16[1024,768]{1,0:T(8,128)(2,1)S(1)} fusion(f32[1024,768]{1,0:T(8,128)S(1)} %fusion.12, bf16[1,2560,768]{2,1,0:T(8,128)(2,1)S(1)} %copy-done.3, bf16[128,8,2560]{2,1,0:T(8,128)(2,1)} %all-to-all-done), kind=kOutput, calls=%fused_computation.38 | convolution fusion | flops 4031250432 | bytes 13893632 | tf_op jit(solution)/shard_map/dot_general | solution.py:292
  232.2 6.0 %fusion.18 = bf16[128,8,2560]{2,1,0:T(8,128)(2,1)} fusion(bf16[1024,768]{1,0:T(8,128)(2,1)S(1)} %multiply_convert_fusion.1, bf16[1,768,2560]{2,1,0:T(8,128)(2,1)S(1)} %copy-done.5), kind=kOutput, calls=%fused_computation.22 | convolution fusion | flops 4029153280 | bytes 10747904 | tf_op jit(solution)/shard_map/dot_general | solution.py:296
  238.2 41.4 %all-to-all-done.2 = bf16[128,8,2560]{2,1,0:T(8,128)(2,1)} async-done(((bf16[128,8,2560]{2,1,0:T(8,128)(2,1)}), bf16[128,8,2560]{2,1,0:T(8,128)(2,1)}, u32[]{:S(2)}, u32[]{:S(2)}) %all-to-all-start.2) | async-done | bytes 5242912 | tf_op jit(solution)/shard_map/all_to_all | solution.py:290
  279.6 6.6 %all-to-all-start.1 = ((bf16[128,8,2560]{2,1,0:T(8,128)(2,1)}), bf16[128,8,2560]{2,1,0:T(8,128)(2,1)}, u32[]{:S(2)}, u32[]{:S(2)}) async-start(bf16[128,8,2560]{2,1,0:T(8,128)(2,1)} %fusion.18), calls=%async_computation.1 | async-start | bytes 10485760 | tf_op jit(solution)/shard_map/all_to_all | solution.py:295
  286.2 7.5 %fusion.4 = f32[1024,768]{1,0:T(8,128)S(1)} fusion(bf16[128,8,2560]{2,1,0:T(8,128)(2,1)} %all-to-all-done.2, bf16[1,2560,768]{2,1,0:T(8,128)(2,1)} %param.22), kind=kOutput, calls=%fused_computation.8 | convolution fusion | flops 4026531840 | bytes 12320768 | tf_op jit(solution)/shard_map/dot_general | solution.py:293
  293.7 7.2 %multiply_convert_fusion = bf16[1024,768]{1,0:T(8,128)(2,1)S(1)} fusion(f32[1024,768]{1,0:T(8,128)S(1)} %fusion.4, bf16[1,2560,768]{2,1,0:T(8,128)(2,1)S(1)} %copy-done.4, bf16[128,8,2560]{2,1,0:T(8,128)(2,1)} %all-to-all-done.2), kind=kOutput, calls=%fused_computation.37 | convolution fusion | flops 4031250432 | bytes 13893632 | tf_op jit(solution)/shard_map/dot_general | solution.py:292
  300.9 6.0 %fusion.19 = bf16[128,8,2560]{2,1,0:T(8,128)(2,1)} fusion(bf16[1024,768]{1,0:T(8,128)(2,1)S(1)} %multiply_convert_fusion, bf16[1,768,2560]{2,1,0:T(8,128)(2,1)S(1)} %copy-done.6), kind=kOutput, calls=%fused_computation.23 | convolution fusion | flops 4029153280 | bytes 10747904 | tf_op jit(solution)/shard_map/dot_general | solution.py:296
  307.0 41.4 %all-to-all-done.1 = bf16[128,8,2560]{2,1,0:T(8,128)(2,1)} async-done(((bf16[128,8,2560]{2,1,0:T(8,128)(2,1)}), bf16[128,8,2560]{2,1,0:T(8,128)(2,1)}, u32[]{:S(2)}, u32[]{:S(2)}) %all-to-all-start.1) | async-done | bytes 5242912 | tf_op jit(solution)/shard_map/all_to_all | solution.py:295
  348.3 6.5 %all-to-all-start.3 = ((bf16[128,8,2560]{2,1,0:T(8,128)(2,1)}), bf16[128,8,2560]{2,1,0:T(8,128)(2,1)}, u32[]{:S(2)}, u32[]{:S(2)}) async-start(bf16[128,8,2560]{2,1,0:T(8,128)(2,1)} %fusion.19), calls=%async_computation.3 | async-start | bytes 10485760 | tf_op jit(solution)/shard_map/all_to_all | solution.py:295
  354.9 0.4 fusion.76
  355.7 3.4 fusion.26
  359.1 3.4 fusion.29
  362.5 54.5 %all-to-all-done.3 = bf16[128,8,2560]{2,1,0:T(8,128)(2,1)} async-done(((bf16[128,8,2560]{2,1,0:T(8,128)(2,1)}), bf16[128,8,2560]{2,1,0:T(8,128)(2,1)}, u32[]{:S(2)}, u32[]{:S(2)}) %all-to-all-start.3) | async-done | bytes 5242912 | tf_op jit(solution)/shard_map/all_to_all | solution.py:295
  417.0 3.4 fusion.32
  420.5 4.2 fusion.39
  (76 shorter events, 2.6 us)
Async XLA Ops:
  6.5 348.3 %copy-start = (bf16[2560,64]{0,1:T(8,128)(2,1)S(1)}, bf16[2560,64]{0,1:T(8,128)(2,1)}, u32[]{:S(2)}) copy-start(bf16[2560,64]{0,1:T(8,128)(2,1)} %param.19) | copy-start | bytes 983044
  6.5 46.9 %copy-start.7 = (s32[1,4]{1,0:T(1,128)S(1)}, s32[1,4]{1,0:T(1,128)}, u32[]{:S(2)}) copy-start(s32[1,4]{1,0:T(1,128)} %param.15) | copy-start | bytes 52
  6.5 47.0 %copy-start.2 = (s32[128,6]{0,1:T(8,128)S(1)}, s32[128,6]{0,1:T(8,128)}, u32[]{:S(2)}) copy-start(s32[128,6]{0,1:T(8,128)} %param.20) | copy-start | bytes 9220
  6.5 36.7 %all-gather.4.cloned.1.call-start = ((), (), s32[]{:S(2)}) async-start(), calls=%async_computation.4 | async-start | bytes 4718592 | tf_op jit(solution)/shard_map/all_gather | solution.py:181
  8.5 71.5 %all-gather.8.cloned.1.call-start = ((), (), s32[]{:S(2)}) async-start(), calls=%async_computation.6 | async-start | bytes 3538944 | tf_op jit(solution)/shard_map/all_gather | solution.py:185
  43.3 75.2 %all-gather.6.cloned.1.call-start = ((), (), s32[]{:S(2)}) async-start(), calls=%async_computation.5 | async-start | bytes 2228224 | tf_op jit(solution)/shard_map/all_gather | solution.py:186
  93.6 33.1 %copy-start.1 = (bf16[128,2560]{1,0:T(8,128)(2,1)S(1)}, bf16[128,2560]{1,0:T(8,128)(2,1)}, u32[]{:S(2)}) copy-start(bf16[128,2560]{1,0:T(8,128)(2,1)} %param.12) | copy-start | bytes 1966084
  134.9 76.0 %all-to-all-start = ((bf16[128,8,2560]{2,1,0:T(8,128)(2,1)}), bf16[128,8,2560]{2,1,0:T(8,128)(2,1)}, u32[]{:S(2)}, u32[]{:S(2)}) async-start(bf16[128,8,2560]{2,1,0:T(8,128)(2,1)} %fusion.16), calls=%async_computation | async-start | bytes 10485760 | tf_op jit(solution)/shard_map/all_to_all | solution.py:290
  211.0 68.7 %all-to-all-start.2 = ((bf16[128,8,2560]{2,1,0:T(8,128)(2,1)}), bf16[128,8,2560]{2,1,0:T(8,128)(2,1)}, u32[]{:S(2)}, u32[]{:S(2)}) async-start(bf16[128,8,2560]{2,1,0:T(8,128)(2,1)} %fusion.17), calls=%async_computation.2 | async-start | bytes 10485760 | tf_op jit(solution)/shard_map/all_to_all | solution.py:290
  217.5 7.5 %copy-start.3 = (bf16[1,2560,768]{2,1,0:T(8,128)(2,1)S(1)}, bf16[1,2560,768]{2,1,0:T(8,128)(2,1)}, u32[]{:S(2)}) copy-start(bf16[1,2560,768]{2,1,0:T(8,128)(2,1)} %param.21) | copy-start | bytes 11796484
  225.0 7.2 %copy-start.5 = (bf16[1,768,2560]{2,1,0:T(8,128)(2,1)S(1)}, bf16[1,768,2560]{2,1,0:T(8,128)(2,1)}, u32[]{:S(2)}) copy-start(bf16[1,768,2560]{2,1,0:T(8,128)(2,1)} %param.23) | copy-start | bytes 11796484
  279.6 68.7 %all-to-all-start.1 = ((bf16[128,8,2560]{2,1,0:T(8,128)(2,1)}), bf16[128,8,2560]{2,1,0:T(8,128)(2,1)}, u32[]{:S(2)}, u32[]{:S(2)}) async-start(bf16[128,8,2560]{2,1,0:T(8,128)(2,1)} %fusion.18), calls=%async_computation.1 | async-start | bytes 10485760 | tf_op jit(solution)/shard_map/all_to_all | solution.py:295
  286.2 7.5 %copy-start.4 = (bf16[1,2560,768]{2,1,0:T(8,128)(2,1)S(1)}, bf16[1,2560,768]{2,1,0:T(8,128)(2,1)}, u32[]{:S(2)}) copy-start(bf16[1,2560,768]{2,1,0:T(8,128)(2,1)} %param.21) | copy-start | bytes 11796484
  293.7 7.2 %copy-start.6 = (bf16[1,768,2560]{2,1,0:T(8,128)(2,1)S(1)}, bf16[1,768,2560]{2,1,0:T(8,128)(2,1)}, u32[]{:S(2)}) copy-start(bf16[1,768,2560]{2,1,0:T(8,128)(2,1)} %param.23) | copy-start | bytes 11796484
  348.3 68.7 %all-to-all-start.3 = ((bf16[128,8,2560]{2,1,0:T(8,128)(2,1)}), bf16[128,8,2560]{2,1,0:T(8,128)(2,1)}, u32[]{:S(2)}, u32[]{:S(2)}) async-start(bf16[128,8,2560]{2,1,0:T(8,128)(2,1)} %fusion.19), calls=%async_computation.3 | async-start | bytes 10485760 | tf_op jit(solution)/shard_map/all_to_all | solution.py:295
Sparse Core Ops, SparseCore 0:
  9.1 34.1 all-gather.3
  44.9 27.6 all-gather.7
  74.8 43.6 all-gather.5

commit v12 on v10

--- a/solution.py
+++ b/solution.py
@@ -180,8 +180,6 @@
     pool_rows = lax.all_gather(page_pool, "req", axis=0, tiled=True).reshape(
         pool_all * PAGE_TOKENS, 2 * row_width
     )
-    pool_rows, suffix_after = lax.optimization_barrier((pool_rows, suffix_kv))
-    segment = lax.all_gather(suffix_after, "exp", axis=0, tiled=True)
     counts = jnp.sum(
         (page_table[0][:, :, None] == jnp.arange(pool_all, dtype=jnp.int32)[None, None, :]).astype(
             jnp.float32
@@ -189,7 +187,7 @@
         axis=1,
     )
     query_counts = jnp.dot(pick.astype(jnp.float32), counts, precision=lax.Precision.HIGHEST)
-    keypos = jnp.arange(segment.shape[0], dtype=jnp.int32)
+    keypos = jnp.arange(lax.axis_size("exp") * token_index, dtype=jnp.int32)
     suffix_weights = (keypos[None, :] <= positions[:, None]) & (keypos[None, :] >= first[:, None])
     spread = (
         jnp.arange(pool_all, dtype=jnp.int32)[:, None]
@@ -211,6 +209,10 @@
     order = jnp.sum(
         jnp.where(destination[None, :] == slots[:, None], slots[None, :], 0), axis=1
     ).astype(jnp.int32)
+    suffix_after, pool_weights, order, live_count = lax.optimization_barrier(
+        (suffix_kv, pool_weights, order, live_count)
+    )
+    segment = lax.all_gather(suffix_after, "exp", axis=0, tiled=True)
     carry = flash(
         queries,
         pool_weights,

time: 426 us -> 418 us (0.981)
  starting transfers between devices: 43.4 us -> 30 us
    all_gather x1, waiting for transfers between devices: 2.79 us -> 16.8 us  [on_device(): segment = lax.all_gather(suffix_after, 'exp', axis=0, tiled=True)]
    all_to_all x2, starting transfers between devices: 30.3 us -> 16.9 us  [on_device(): lax.all_to_all(outgoing, ('req', 'exp'), split_axis=0, concat_axis=0, til...]
    all_gather x1, waiting for transfers between devices: 47.5 us -> 37.4 us  [on_device(): lax.all_gather(page_pool, 'req', axis=0, tiled=True)]
  transfers between devices with their start and end apart: 6 -> 6, of which waited for: 6 -> 6; matrix products, arithmetic and copies ran while one was open for 15% -> 16% of each run, Pallas kernels for 7% -> 7%
where the time goes in v12:
time: 418 us; the launch traced here: 415 us
  waiting for transfers between devices  250 us (60%)
  matrix products  71.7 us (17%)
  Pallas kernels  40.6 us (10%)
  starting transfers between devices  30 us (7%)
  between operations  13.7 us (3%)
  other arithmetic  8.26 us (2%)
    all_to_all x2, waiting for transfers between devices, on_device(): lax.all_to_all(outgoing, ('req', 'exp'), split_axis=0, concat_axis=0, til...  99.6 us
    all_to_all x2, waiting for transfers between devices, on_device(): lax.all_to_all(jnp.dot(inner, w_down[0], preferred_element_type=jnp.float...  95.8 us
    pallas_call x2, Pallas kernels, flash(): pl.pallas_call(kern, grid_spec=grid_spec, out_shape=out_shape)  40.6 us
    all_gather x1, waiting for transfers between devices, on_device(): lax.all_gather(page_pool, 'req', axis=0, tiled=True)  37.4 us
    all_to_all x2, starting transfers between devices, on_device(): lax.all_to_all(outgoing, ('req', 'exp'), split_axis=0, concat_axis=0, til...  16.9 us
    all_gather x1, waiting for transfers between devices, on_device(): segment = lax.all_gather(suffix_after, 'exp', axis=0, tiled=True)  16.8 us
    dot_general x2, matrix products, on_device(): up_part = jnp.dot(flat_rows, w_up[0], preferred_element_type=jnp.float32)  14.9 us
    dot_general x2, matrix products, on_device(): jnp.dot(flat_rows, w_gate[0], preferred_element_type=jnp.float32)  14.4 us
  transfers between devices with their start and end apart: 6, of which 6 were waited for; matrix products, arithmetic and copies ran while one was open for 16% of the time, Pallas kernels for 7%

profile of v12, /device:TPU:34, one launch (start us, length us, event | category | flops | bytes accessed | tf_op | source)
XLA Modules:
  0.0 415.1 jit_solution(11313378407488831900)
XLA Ops:
  6.5 0.7 all-gather.5.cloned.1.call-update
  7.3 0.8 reduce-window.21
  8.1 0.1 convert_reduce_fusion.1
  8.2 0.8 convert_reduce_fusion
  9.0 0.3 fusion.75
  9.3 0.1 copy.28
  9.4 0.1 reduce-window.23
  9.5 0.1 copy.27
  9.6 0.1 reduce-window.22
  9.7 0.6 fusion.68
  10.4 0.8 add_reduce_fusion
  11.1 0.6 select_reduce_fusion.3.order_ref
  11.8 3.3 multiply_select_fusion.refs_0_.refs_1_.refs_2_.refs_3_
  15.1 1.2 compare_convert_fusion.flags_ref
  16.3 0.1 select_reduce_fusion.4
  16.4 0.3 select_reduce_fusion
  16.8 0.5 compare_convert_fusion.1.flags_ref
  17.3 0.1 convolution_convert_fusion.4
  17.5 0.1 fusion.57
  17.6 1.4 fusion.53.refs_0_
  19.0 37.4 %all-gather.5.cloned.1.call-done = bf16[56,128,512]{2,1,0:T(8,128)(2,1)} async-done(((bf16[7,128,512]{2,1,0:T(8,128)(2,1)}), bf16[56,128,512]{2,1,0:T(8,128)(2,1)}) %all-gather.5.cloned.1.call-update) | async-done | bytes 7340048 | tf_op jit(solution)/shard_map/all_gather | solution.py:180
  56.4 29.1 %shard_map.118 = (f32[2,640,1]{2,1,0:T(8,128)}, f32[2,640,1]{2,1,0:T(8,128)}, f32[2,640,128]{2,1,0:T(8,128)}) custom-call(s32[14]{0:T(128)} %compare_convert_fusion.flags_ref, s32[56]{0:T(128)} %select_reduce_fusion.3.order_ref, bf16[128,1280]{1,0:T(8,128)(2,1)} %q_ref.3, f32[128,7168]{1,0:T(8,128)} %multiply_select_fusion.refs_0_.refs_1_.refs_2_.refs_3_, ...), custom_call_target="tpu_custom_call" | custom-call | tf_op jit(solution)/shard_map/pallas_call | solution.py:150
  85.5 16.8 %all-gather.3.cloned.1.call-done.refs_1_ = bf16[2048,512]{1,0:T(8,128)(2,1)} async-done(((bf16[128,512]{1,0:T(8,128)(2,1)}), bf16[2048,512]{1,0:T(8,128)(2,1)}) %all-gather.3.cloned.1.call-update) | async-done | bytes 2097168 | tf_op jit(solution)/shard_map/all_gather | solution.py:215
  102.4 11.5 %shard_map.119 = bf16[128,1280]{1,0:T(8,128)(2,1)} custom-call(s32[4]{0:T(128)} %compare_convert_fusion.1.flags_ref, s32[1]{0:T(128)} %constant.56.clone.1.order_ref, bf16[128,1280]{1,0:T(8,128)(2,1)} %q_ref.3, f32[128,2048]{1,0:T(8,128)} %fusion.53.refs_0_, bf16[2048,512]{1,0:T(8,128)(2,1)} %all-gather.3.cloned.1.call-done.refs_1_, ...), custom_call_target="tpu_custom_call" | custom-call | tf_op jit(solution)/shard_map/pallas_call | solution.py:150
  113.8 4.0 fusion.38
  117.8 0.2 fusion.50
  118.1 3.9 fusion.16
  122.1 10.3 %all-to-all-start = ((bf16[128,8,2560]{2,1,0:T(8,128)(2,1)}), bf16[128,8,2560]{2,1,0:T(8,128)(2,1)}, u32[]{:S(2)}, u32[]{:S(2)}) async-start(bf16[128,8,2560]{2,1,0:T(8,128)(2,1)} %fusion.16), calls=%async_computation | async-start | bytes 10485760 | tf_op jit(solution)/shard_map/all_to_all | solution.py:282
  132.4 3.9 fusion.17
  136.3 58.2 %all-to-all-done = bf16[128,8,2560]{2,1,0:T(8,128)(2,1)} async-done(((bf16[128,8,2560]{2,1,0:T(8,128)(2,1)}), bf16[128,8,2560]{2,1,0:T(8,128)(2,1)}, u32[]{:S(2)}, u32[]{:S(2)}) %all-to-all-start) | async-done | bytes 5242912 | tf_op jit(solution)/shard_map/all_to_all | solution.py:282
  194.5 6.5 %all-to-all-start.2 = ((bf16[128,8,2560]{2,1,0:T(8,128)(2,1)}), bf16[128,8,2560]{2,1,0:T(8,128)(2,1)}, u32[]{:S(2)}, u32[]{:S(2)}) async-start(bf16[128,8,2560]{2,1,0:T(8,128)(2,1)} %fusion.17), calls=%async_computation.2 | async-start | bytes 10485760 | tf_op jit(solution)/shard_map/all_to_all | solution.py:282
  201.1 7.5 %fusion.12 = f32[1024,768]{1,0:T(8,128)S(1)} fusion(bf16[128,8,2560]{2,1,0:T(8,128)(2,1)} %all-to-all-done, bf16[1,2560,768]{2,1,0:T(8,128)(2,1)} %param.22), kind=kOutput, calls=%fused_computation.16 | convolution fusion | flops 4026531840 | bytes 12320768 | tf_op jit(solution)/shard_map/dot_general | solution.py:285
  208.6 7.2 %multiply_convert_fusion.1 = bf16[1024,768]{1,0:T(8,128)(2,1)S(1)} fusion(f32[1024,768]{1,0:T(8,128)S(1)} %fusion.12, bf16[1,2560,768]{2,1,0:T(8,128)(2,1)S(1)} %copy-done.3, bf16[128,8,2560]{2,1,0:T(8,128)(2,1)} %all-to-all-done), kind=kOutput, calls=%fused_computation.39 | convolution fusion | flops 4031250432 | bytes 13893632 | tf_op jit(solution)/shard_map/dot_general | solution.py:284
  215.8 6.0 %fusion.18 = bf16[128,8,2560]{2,1,0:T(8,128)(2,1)} fusion(bf16[1024,768]{1,0:T(8,128)(2,1)S(1)} %multiply_convert_fusion.1, bf16[1,768,2560]{2,1,0:T(8,128)(2,1)S(1)} %copy-done.5), kind=kOutput, calls=%fused_computation.22 | convolution fusion | flops 4029153280 | bytes 10747904 | tf_op jit(solution)/shard_map/dot_general | solution.py:288
  221.8 41.4 %all-to-all-done.2 = bf16[128,8,2560]{2,1,0:T(8,128)(2,1)} async-done(((bf16[128,8,2560]{2,1,0:T(8,128)(2,1)}), bf16[128,8,2560]{2,1,0:T(8,128)(2,1)}, u32[]{:S(2)}, u32[]{:S(2)}) %all-to-all-start.2) | async-done | bytes 5242912 | tf_op jit(solution)/shard_map/all_to_all | solution.py:282
  263.2 6.6 %all-to-all-start.1 = ((bf16[128,8,2560]{2,1,0:T(8,128)(2,1)}), bf16[128,8,2560]{2,1,0:T(8,128)(2,1)}, u32[]{:S(2)}, u32[]{:S(2)}) async-start(bf16[128,8,2560]{2,1,0:T(8,128)(2,1)} %fusion.18), calls=%async_computation.1 | async-start | bytes 10485760 | tf_op jit(solution)/shard_map/all_to_all | solution.py:287
  269.8 7.5 %fusion.4 = f32[1024,768]{1,0:T(8,128)S(1)} fusion(bf16[128,8,2560]{2,1,0:T(8,128)(2,1)} %all-to-all-done.2, bf16[1,2560,768]{2,1,0:T(8,128)(2,1)} %param.22), kind=kOutput, calls=%fused_computation.8 | convolution fusion | flops 4026531840 | bytes 12320768 | tf_op jit(solution)/shard_map/dot_general | solution.py:285
  277.3 7.2 %multiply_convert_fusion = bf16[1024,768]{1,0:T(8,128)(2,1)S(1)} fusion(f32[1024,768]{1,0:T(8,128)S(1)} %fusion.4, bf16[1,2560,768]{2,1,0:T(8,128)(2,1)S(1)} %copy-done.4, bf16[128,8,2560]{2,1,0:T(8,128)(2,1)} %all-to-all-done.2), kind=kOutput, calls=%fused_computation.38 | convolution fusion | flops 4031250432 | bytes 13893632 | tf_op jit(solution)/shard_map/dot_general | solution.py:284
  284.5 6.0 %fusion.19 = bf16[128,8,2560]{2,1,0:T(8,128)(2,1)} fusion(bf16[1024,768]{1,0:T(8,128)(2,1)S(1)} %multiply_convert_fusion, bf16[1,768,2560]{2,1,0:T(8,128)(2,1)S(1)} %copy-done.6), kind=kOutput, calls=%fused_computation.23 | convolution fusion | flops 4029153280 | bytes 10747904 | tf_op jit(solution)/shard_map/dot_general | solution.py:288
  290.6 41.4 %all-to-all-done.1 = bf16[128,8,2560]{2,1,0:T(8,128)(2,1)} async-done(((bf16[128,8,2560]{2,1,0:T(8,128)(2,1)}), bf16[128,8,2560]{2,1,0:T(8,128)(2,1)}, u32[]{:S(2)}, u32[]{:S(2)}) %all-to-all-start.1) | async-done | bytes 5242912 | tf_op jit(solution)/shard_map/all_to_all | solution.py:287
  331.9 6.5 %all-to-all-start.3 = ((bf16[128,8,2560]{2,1,0:T(8,128)(2,1)}), bf16[128,8,2560]{2,1,0:T(8,128)(2,1)}, u32[]{:S(2)}, u32[]{:S(2)}) async-start(bf16[128,8,2560]{2,1,0:T(8,128)(2,1)} %fusion.19), calls=%async_computation.3 | async-start | bytes 10485760 | tf_op jit(solution)/shard_map/all_to_all | solution.py:287
  338.5 0.4 fusion.73
  339.0 0.1 fusion.56
  339.3 3.4 fusion.26
  342.7 3.4 fusion.29
  346.1 54.5 %all-to-all-done.3 = bf16[128,8,2560]{2,1,0:T(8,128)(2,1)} async-done(((bf16[128,8,2560]{2,1,0:T(8,128)(2,1)}), bf16[128,8,2560]{2,1,0:T(8,128)(2,1)}, u32[]{:S(2)}, u32[]{:S(2)}) %all-to-all-start.3) | async-done | bytes 5242912 | tf_op jit(solution)/shard_map/all_to_all | solution.py:287
  400.6 3.4 fusion.32
  404.0 4.2 %fusion.39 = bf16[128,2560]{1,0:T(8,128)(2,1)} fusion(f32[128,2560]{1,0:T(8,128)S(1)} %fusion.32, bf16[128,1024]{0,1:T(8,128)(2,1)S(1)} %bitcast.108, bf16[128,8,2560]{2,1,0:T(8,128)(2,1)} %all-to-all-done.3), kind=kOutput, calls=%fused_computation.37 | convolution fusion | flops 671744000 | bytes 7471104 | tf_op jit(solution)/shard_map/dot_general | solution.py:302
  (40 shorter events, 0.6 us)
Async XLA Ops:
  6.5 331.9 %copy-start = (bf16[2560,64]{0,1:T(8,128)(2,1)S(1)}, bf16[2560,64]{0,1:T(8,128)(2,1)}, u32[]{:S(2)}) copy-start(bf16[2560,64]{0,1:T(8,128)(2,1)} %param.19) | copy-start | bytes 983044
  6.5 9.8 %copy-start.7 = (s32[1,4]{1,0:T(1,128)S(1)}, s32[1,4]{1,0:T(1,128)}, u32[]{:S(2)}) copy-start(s32[1,4]{1,0:T(1,128)} %param.15) | copy-start | bytes 52
  6.5 9.9 %copy-start.2 = (s32[128,6]{0,1:T(8,128)S(1)}, s32[128,6]{0,1:T(8,128)}, u32[]{:S(2)}) copy-start(s32[128,6]{0,1:T(8,128)} %param.20) | copy-start | bytes 9220
  6.5 49.9 %all-gather.5.cloned.1.call-start = ((), (), s32[]{:S(2)}) async-start(), calls=%async_computation.5 | async-start | bytes 8257536 | tf_op jit(solution)/shard_map/all_gather | solution.py:180
  7.3 95.1 %all-gather.3.cloned.1.call-start = ((), (), s32[]{:S(2)}) async-start(), calls=%async_computation.4 | async-start | bytes 2228224 | tf_op jit(solution)/shard_map/all_gather | solution.py:215
  85.5 28.3 %copy-start.1 = (bf16[128,2560]{1,0:T(8,128)(2,1)S(1)}, bf16[128,2560]{1,0:T(8,128)(2,1)}, u32[]{:S(2)}) copy-start(bf16[128,2560]{1,0:T(8,128)(2,1)} %param.12) | copy-start | bytes 1966084
  122.1 72.5 %all-to-all-start = ((bf16[128,8,2560]{2,1,0:T(8,128)(2,1)}), bf16[128,8,2560]{2,1,0:T(8,128)(2,1)}, u32[]{:S(2)}, u32[]{:S(2)}) async-start(bf16[128,8,2560]{2,1,0:T(8,128)(2,1)} %fusion.16), calls=%async_computation | async-start | bytes 10485760 | tf_op jit(solution)/shard_map/all_to_all | solution.py:282
  194.5 68.7 %all-to-all-start.2 = ((bf16[128,8,2560]{2,1,0:T(8,128)(2,1)}), bf16[128,8,2560]{2,1,0:T(8,128)(2,1)}, u32[]{:S(2)}, u32[]{:S(2)}) async-start(bf16[128,8,2560]{2,1,0:T(8,128)(2,1)} %fusion.17), calls=%async_computation.2 | async-start | bytes 10485760 | tf_op jit(solution)/shard_map/all_to_all | solution.py:282
  201.1 7.5 %copy-start.3 = (bf16[1,2560,768]{2,1,0:T(8,128)(2,1)S(1)}, bf16[1,2560,768]{2,1,0:T(8,128)(2,1)}, u32[]{:S(2)}) copy-start(bf16[1,2560,768]{2,1,0:T(8,128)(2,1)} %param.21) | copy-start | bytes 11796484
  208.6 7.2 %copy-start.5 = (bf16[1,768,2560]{2,1,0:T(8,128)(2,1)S(1)}, bf16[1,768,2560]{2,1,0:T(8,128)(2,1)}, u32[]{:S(2)}) copy-start(bf16[1,768,2560]{2,1,0:T(8,128)(2,1)} %param.23) | copy-start | bytes 11796484
  263.2 68.7 %all-to-all-start.1 = ((bf16[128,8,2560]{2,1,0:T(8,128)(2,1)}), bf16[128,8,2560]{2,1,0:T(8,128)(2,1)}, u32[]{:S(2)}, u32[]{:S(2)}) async-start(bf16[128,8,2560]{2,1,0:T(8,128)(2,1)} %fusion.18), calls=%async_computation.1 | async-start | bytes 10485760 | tf_op jit(solution)/shard_map/all_to_all | solution.py:287
  269.8 7.5 %copy-start.4 = (bf16[1,2560,768]{2,1,0:T(8,128)(2,1)S(1)}, bf16[1,2560,768]{2,1,0:T(8,128)(2,1)}, u32[]{:S(2)}) copy-start(bf16[1,2560,768]{2,1,0:T(8,128)(2,1)} %param.21) | copy-start | bytes 11796484
  277.3 7.2 %copy-start.6 = (bf16[1,768,2560]{2,1,0:T(8,128)(2,1)S(1)}, bf16[1,768,2560]{2,1,0:T(8,128)(2,1)}, u32[]{:S(2)}) copy-start(bf16[1,768,2560]{2,1,0:T(8,128)(2,1)} %param.23) | copy-start | bytes 11796484
  331.9 68.7 %all-to-all-start.3 = ((bf16[128,8,2560]{2,1,0:T(8,128)(2,1)}), bf16[128,8,2560]{2,1,0:T(8,128)(2,1)}, u32[]{:S(2)}, u32[]{:S(2)}) async-start(bf16[128,8,2560]{2,1,0:T(8,128)(2,1)} %fusion.19), calls=%async_computation.3 | async-start | bytes 10485760 | tf_op jit(solution)/shard_map/all_to_all | solution.py:287
Sparse Core Ops, SparseCore 0:
  9.1 47.3 all-gather.4
  58.5 43.7 all-gather.2

commit v13 on v12

--- a/solution.py
+++ b/solution.py
@@ -296,11 +296,10 @@
         chunk_weight = weight[:, :, :, c * part:(c + 1) * part].reshape(token_index, -1)
         high = chunk_weight.astype(jnp.bfloat16)
         low = (chunk_weight - high.astype(jnp.float32)).astype(jnp.bfloat16)
-        moe = (
-            moe
-            + jnp.dot(high, returned, preferred_element_type=jnp.float32)
-            + jnp.dot(low, returned, preferred_element_type=jnp.float32)
+        both = jnp.dot(
+            jnp.concatenate([high, low], axis=0), returned, preferred_element_type=jnp.float32
         )
+        moe = moe + both[:token_index] + both[token_index:]
     return moe.astype(jnp.bfloat16)
 
 

time: 418 us -> 416 us (level)
  matrix products: 71.7 us -> 67 us
    dot_general x4 -> x2, matrix products: 14.3 us -> 9.7 us  [on_device(): jnp.dot(jnp.concatenate([high, low], axis=0), returned, preferred_element...]
  transfers between devices with their start and end apart: 6 -> 6, of which waited for: 6 -> 6; matrix products, arithmetic and copies ran while one was open for 16% -> 15% of each run, Pallas kernels for 7% -> 8%
where the time goes in v13:
time: 416 us; the launch traced here: 414 us
  waiting for transfers between devices  249 us (60%)
  matrix products  67 us (16%)
  Pallas kernels  43.2 us (10%)
  starting transfers between devices  31.2 us (8%)
  between operations  13.7 us (3%)
  other arithmetic  9.58 us (2%)
    all_to_all x2, waiting for transfers between devices, on_device(): lax.all_to_all(outgoing, ('req', 'exp'), split_axis=0, concat_axis=0, til...  99.6 us
    all_to_all x2, waiting for transfers between devices, on_device(): lax.all_to_all(jnp.dot(inner, w_down[0], preferred_element_type=jnp.float...  97.1 us
    pallas_call x2, Pallas kernels, flash(): pl.pallas_call(kern, grid_spec=grid_spec, out_shape=out_shape)  43.2 us
    all_gather x1, waiting for transfers between devices, on_device(): lax.all_gather(page_pool, 'req', axis=0, tiled=True)  37.4 us
    all_to_all x2, starting transfers between devices, on_device(): lax.all_to_all(outgoing, ('req', 'exp'), split_axis=0, concat_axis=0, til...  18 us
    dot_general x2, matrix products, on_device(): up_part = jnp.dot(flat_rows, w_up[0], preferred_element_type=jnp.float32)  14.9 us
    dot_general x2, matrix products, on_device(): jnp.dot(flat_rows, w_gate[0], preferred_element_type=jnp.float32)  14.4 us
    all_gather x1, waiting for transfers between devices, on_device(): segment = lax.all_gather(suffix_after, 'exp', axis=0, tiled=True)  14.2 us
  transfers between devices with their start and end apart: 6, of which 6 were waited for; matrix products, arithmetic and copies ran while one was open for 15% of the time, Pallas kernels for 8%

profile of v13, /device:TPU:34, one launch (start us, length us, event | category | flops | bytes accessed | tf_op | source)
XLA Modules:
  0.0 414.2 jit_solution(5378815715238084268)
XLA Ops:
  6.5 0.7 all-gather.5.cloned.1.call-update
  7.3 0.8 reduce-window.21
  8.1 0.1 convert_reduce_fusion.1
  8.2 0.8 convert_reduce_fusion
  9.0 0.3 fusion.71
  9.3 0.1 copy.27
  9.4 0.1 reduce-window.22
  9.5 0.1 copy.28
  9.6 0.1 reduce-window.23
  9.7 0.6 fusion.61
  10.4 0.8 add_reduce_fusion
  11.1 0.6 select_reduce_fusion.3.order_ref
  11.8 3.3 multiply_select_fusion.refs_0_.refs_1_.refs_2_.refs_3_
  15.1 1.2 compare_convert_fusion.flags_ref
  16.3 0.1 select_reduce_fusion.4
  16.4 0.3 select_reduce_fusion
  16.8 0.5 compare_convert_fusion.1.flags_ref
  17.3 0.1 convolution_convert_fusion.4
  17.5 0.1 fusion.50
  17.6 1.4 fusion.38.refs_0_
  19.0 37.4 %all-gather.5.cloned.1.call-done = bf16[56,128,512]{2,1,0:T(8,128)(2,1)} async-done(((bf16[7,128,512]{2,1,0:T(8,128)(2,1)}), bf16[56,128,512]{2,1,0:T(8,128)(2,1)}) %all-gather.5.cloned.1.call-update) | async-done | bytes 7340048 | tf_op jit(solution)/shard_map/all_gather | solution.py:180
  56.4 31.7 %shard_map.118 = (f32[2,640,1]{2,1,0:T(8,128)}, f32[2,640,1]{2,1,0:T(8,128)}, f32[2,640,128]{2,1,0:T(8,128)}) custom-call(s32[14]{0:T(128)} %compare_convert_fusion.flags_ref, s32[56]{0:T(128)} %select_reduce_fusion.3.order_ref, bf16[128,1280]{1,0:T(8,128)(2,1)} %q_ref.3, f32[128,7168]{1,0:T(8,128)} %multiply_select_fusion.refs_0_.refs_1_.refs_2_.refs_3_, ...), custom_call_target="tpu_custom_call" | custom-call | tf_op jit(solution)/shard_map/pallas_call | solution.py:150
  88.1 14.2 %all-gather.3.cloned.1.call-done.refs_1_ = bf16[2048,512]{1,0:T(8,128)(2,1)} async-done(((bf16[128,512]{1,0:T(8,128)(2,1)}), bf16[2048,512]{1,0:T(8,128)(2,1)}) %all-gather.3.cloned.1.call-update) | async-done | bytes 2097168 | tf_op jit(solution)/shard_map/all_gather | solution.py:215
  102.4 11.5 %shard_map.119 = bf16[128,1280]{1,0:T(8,128)(2,1)} custom-call(s32[4]{0:T(128)} %compare_convert_fusion.1.flags_ref, s32[1]{0:T(128)} %constant.56.clone.1.order_ref, bf16[128,1280]{1,0:T(8,128)(2,1)} %q_ref.3, f32[128,2048]{1,0:T(8,128)} %fusion.38.refs_0_, bf16[2048,512]{1,0:T(8,128)(2,1)} %all-gather.3.cloned.1.call-done.refs_1_, ...), custom_call_target="tpu_custom_call" | custom-call | tf_op jit(solution)/shard_map/pallas_call | solution.py:150
  113.8 4.0 fusion.22
  117.8 0.2 fusion.31
  118.1 0.1 broadcast_in_dim.136
  118.1 3.9 fusion.12
  122.1 11.5 %all-to-all-start = ((bf16[128,8,2560]{2,1,0:T(8,128)(2,1)}), bf16[128,8,2560]{2,1,0:T(8,128)(2,1)}, u32[]{:S(2)}, u32[]{:S(2)}) async-start(bf16[128,8,2560]{2,1,0:T(8,128)(2,1)} %fusion.12), calls=%async_computation | async-start | bytes 10485760 | tf_op jit(solution)/shard_map/all_to_all | solution.py:282
  133.6 3.9 fusion.13
  137.5 58.2 %all-to-all-done = bf16[128,8,2560]{2,1,0:T(8,128)(2,1)} async-done(((bf16[128,8,2560]{2,1,0:T(8,128)(2,1)}), bf16[128,8,2560]{2,1,0:T(8,128)(2,1)}, u32[]{:S(2)}, u32[]{:S(2)}) %all-to-all-start) | async-done | bytes 5242912 | tf_op jit(solution)/shard_map/all_to_all | solution.py:282
  195.7 6.5 %all-to-all-start.2 = ((bf16[128,8,2560]{2,1,0:T(8,128)(2,1)}), bf16[128,8,2560]{2,1,0:T(8,128)(2,1)}, u32[]{:S(2)}, u32[]{:S(2)}) async-start(bf16[128,8,2560]{2,1,0:T(8,128)(2,1)} %fusion.13), calls=%async_computation.2 | async-start | bytes 10485760 | tf_op jit(solution)/shard_map/all_to_all | solution.py:282
  202.3 7.5 %fusion.8 = f32[1024,768]{1,0:T(8,128)S(1)} fusion(bf16[128,8,2560]{2,1,0:T(8,128)(2,1)} %all-to-all-done, bf16[1,2560,768]{2,1,0:T(8,128)(2,1)} %param.22), kind=kOutput, calls=%fused_computation.12 | convolution fusion | flops 4026531840 | bytes 12320768 | tf_op jit(solution)/shard_map/dot_general | solution.py:285
  209.8 7.2 %multiply_convert_fusion.1 = bf16[1024,768]{1,0:T(8,128)(2,1)S(1)} fusion(f32[1024,768]{1,0:T(8,128)S(1)} %fusion.8, bf16[1,2560,768]{2,1,0:T(8,128)(2,1)S(1)} %copy-done.4, bf16[128,8,2560]{2,1,0:T(8,128)(2,1)} %all-to-all-done), kind=kOutput, calls=%fused_computation.30 | convolution fusion | flops 4031250432 | bytes 13893632 | tf_op jit(solution)/shard_map/dot_general | solution.py:284
  217.0 6.0 %fusion.14 = bf16[128,8,2560]{2,1,0:T(8,128)(2,1)} fusion(bf16[1024,768]{1,0:T(8,128)(2,1)S(1)} %multiply_convert_fusion.1, bf16[1,768,2560]{2,1,0:T(8,128)(2,1)S(1)} %copy-done.6), kind=kOutput, calls=%fused_computation.18 | convolution fusion | flops 4029153280 | bytes 10747904 | tf_op jit(solution)/shard_map/dot_general | solution.py:288
  223.0 41.4 %all-to-all-done.2 = bf16[128,8,2560]{2,1,0:T(8,128)(2,1)} async-done(((bf16[128,8,2560]{2,1,0:T(8,128)(2,1)}), bf16[128,8,2560]{2,1,0:T(8,128)(2,1)}, u32[]{:S(2)}, u32[]{:S(2)}) %all-to-all-start.2) | async-done | bytes 5242912 | tf_op jit(solution)/shard_map/all_to_all | solution.py:282
  264.4 6.6 %all-to-all-start.1 = ((bf16[128,8,2560]{2,1,0:T(8,128)(2,1)}), bf16[128,8,2560]{2,1,0:T(8,128)(2,1)}, u32[]{:S(2)}, u32[]{:S(2)}) async-start(bf16[128,8,2560]{2,1,0:T(8,128)(2,1)} %fusion.14), calls=%async_computation.1 | async-start | bytes 10485760 | tf_op jit(solution)/shard_map/all_to_all | solution.py:287
  271.0 7.5 %fusion.2 = f32[1024,768]{1,0:T(8,128)S(1)} fusion(bf16[128,8,2560]{2,1,0:T(8,128)(2,1)} %all-to-all-done.2, bf16[1,2560,768]{2,1,0:T(8,128)(2,1)} %param.22), kind=kOutput, calls=%fused_computation.6 | convolution fusion | flops 4026531840 | bytes 12320768 | tf_op jit(solution)/shard_map/dot_general | solution.py:285
  278.5 7.2 %multiply_convert_fusion = bf16[1024,768]{1,0:T(8,128)(2,1)S(1)} fusion(f32[1024,768]{1,0:T(8,128)S(1)} %fusion.2, bf16[1,2560,768]{2,1,0:T(8,128)(2,1)S(1)} %copy-done.5, bf16[128,8,2560]{2,1,0:T(8,128)(2,1)} %all-to-all-done.2), kind=kOutput, calls=%fused_computation.29 | convolution fusion | flops 4031250432 | bytes 13893632 | tf_op jit(solution)/shard_map/dot_general | solution.py:284
  285.7 6.0 %fusion.15 = bf16[128,8,2560]{2,1,0:T(8,128)(2,1)} fusion(bf16[1024,768]{1,0:T(8,128)(2,1)S(1)} %multiply_convert_fusion, bf16[1,768,2560]{2,1,0:T(8,128)(2,1)S(1)} %copy-done.7), kind=kOutput, calls=%fused_computation.19 | convolution fusion | flops 4029153280 | bytes 10747904 | tf_op jit(solution)/shard_map/dot_general | solution.py:288
  291.7 41.4 %all-to-all-done.1 = bf16[128,8,2560]{2,1,0:T(8,128)(2,1)} async-done(((bf16[128,8,2560]{2,1,0:T(8,128)(2,1)}), bf16[128,8,2560]{2,1,0:T(8,128)(2,1)}, u32[]{:S(2)}, u32[]{:S(2)}) %all-to-all-start.1) | async-done | bytes 5242912 | tf_op jit(solution)/shard_map/all_to_all | solution.py:287
  333.1 6.5 %all-to-all-start.3 = ((bf16[128,8,2560]{2,1,0:T(8,128)(2,1)}), bf16[128,8,2560]{2,1,0:T(8,128)(2,1)}, u32[]{:S(2)}, u32[]{:S(2)}) async-start(bf16[128,8,2560]{2,1,0:T(8,128)(2,1)} %fusion.15), calls=%async_computation.3 | async-start | bytes 10485760 | tf_op jit(solution)/shard_map/all_to_all | solution.py:287
  339.6 0.4 fusion.68
  340.2 0.1 fusion.49
  340.5 5.5 %fusion.6 = f32[256,2560]{1,0:T(8,128)} fusion(bf16[128,8,2560]{2,1,0:T(8,128)(2,1)} %all-to-all-done.1, bf16[128,1024]{0,1:T(8,128)(2,1)S(1)} %fusion.40, bf16[128,1024]{0,1:T(8,128)(2,1)S(1)} %bitcast_convert_fusion.1), kind=kOutput, calls=%fused_computation.10 | convolution fusion | flops 1343225856 | bytes 8388608 | tf_op jit(solution)/shard_map/dot_general | solution.py:299
  346.0 55.8 %all-to-all-done.3 = bf16[128,8,2560]{2,1,0:T(8,128)(2,1)} async-done(((bf16[128,8,2560]{2,1,0:T(8,128)(2,1)}), bf16[128,8,2560]{2,1,0:T(8,128)(2,1)}, u32[]{:S(2)}, u32[]{:S(2)}) %all-to-all-start.3) | async-done | bytes 5242912 | tf_op jit(solution)/shard_map/all_to_all | solution.py:287
  401.8 4.2 %fusion = f32[256,2560]{1,0:T(8,128)S(1)} fusion(bf16[128,8,2560]{2,1,0:T(8,128)(2,1)} %all-to-all-done.3, bf16[128,1024]{0,1:T(8,128)(2,1)S(1)} %fusion.41, bf16[128,1024]{0,1:T(8,128)(2,1)S(1)} %bitcast_convert_fusion), kind=kOutput, calls=%fused_computation.4 | convolution fusion | flops 1343225856 | bytes 8388608 | tf_op jit(solution)/shard_map/dot_general | solution.py:299
  406.0 1.3 fusion.36
  (41 shorter events, 0.4 us)
Async XLA Ops:
  6.5 333.1 %copy-start = (bf16[2560,64]{0,1:T(8,128)(2,1)S(1)}, bf16[2560,64]{0,1:T(8,128)(2,1)}, u32[]{:S(2)}) copy-start(bf16[2560,64]{0,1:T(8,128)(2,1)} %param.19) | copy-start | bytes 983044
  6.5 9.8 %copy-start.8 = (s32[1,4]{1,0:T(1,128)S(1)}, s32[1,4]{1,0:T(1,128)}, u32[]{:S(2)}) copy-start(s32[1,4]{1,0:T(1,128)} %param.15) | copy-start | bytes 52
  6.5 9.9 %copy-start.3 = (s32[128,6]{0,1:T(8,128)S(1)}, s32[128,6]{0,1:T(8,128)}, u32[]{:S(2)}) copy-start(s32[128,6]{0,1:T(8,128)} %param.20) | copy-start | bytes 9220
  6.5 49.9 %all-gather.5.cloned.1.call-start = ((), (), s32[]{:S(2)}) async-start(), calls=%async_computation.5 | async-start | bytes 8257536 | tf_op jit(solution)/shard_map/all_gather | solution.py:180
  7.3 95.1 %all-gather.3.cloned.1.call-start = ((), (), s32[]{:S(2)}) async-start(), calls=%async_computation.4 | async-start | bytes 2228224 | tf_op jit(solution)/shard_map/all_gather | solution.py:215
  88.1 25.7 %copy-start.2 = (bf16[128,2560]{1,0:T(8,128)(2,1)S(1)}, bf16[128,2560]{1,0:T(8,128)(2,1)}, u32[]{:S(2)}) copy-start(bf16[128,2560]{1,0:T(8,128)(2,1)} %param.12) | copy-start | bytes 1966084
  122.1 73.6 %all-to-all-start = ((bf16[128,8,2560]{2,1,0:T(8,128)(2,1)}), bf16[128,8,2560]{2,1,0:T(8,128)(2,1)}, u32[]{:S(2)}, u32[]{:S(2)}) async-start(bf16[128,8,2560]{2,1,0:T(8,128)(2,1)} %fusion.12), calls=%async_computation | async-start | bytes 10485760 | tf_op jit(solution)/shard_map/all_to_all | solution.py:282
  195.7 68.7 %all-to-all-start.2 = ((bf16[128,8,2560]{2,1,0:T(8,128)(2,1)}), bf16[128,8,2560]{2,1,0:T(8,128)(2,1)}, u32[]{:S(2)}, u32[]{:S(2)}) async-start(bf16[128,8,2560]{2,1,0:T(8,128)(2,1)} %fusion.13), calls=%async_computation.2 | async-start | bytes 10485760 | tf_op jit(solution)/shard_map/all_to_all | solution.py:282
  202.3 7.5 %copy-start.4 = (bf16[1,2560,768]{2,1,0:T(8,128)(2,1)S(1)}, bf16[1,2560,768]{2,1,0:T(8,128)(2,1)}, u32[]{:S(2)}) copy-start(bf16[1,2560,768]{2,1,0:T(8,128)(2,1)} %param.21) | copy-start | bytes 11796484
  209.8 7.2 %copy-start.6 = (bf16[1,768,2560]{2,1,0:T(8,128)(2,1)S(1)}, bf16[1,768,2560]{2,1,0:T(8,128)(2,1)}, u32[]{:S(2)}) copy-start(bf16[1,768,2560]{2,1,0:T(8,128)(2,1)} %param.23) | copy-start | bytes 11796484
  264.4 68.7 %all-to-all-start.1 = ((bf16[128,8,2560]{2,1,0:T(8,128)(2,1)}), bf16[128,8,2560]{2,1,0:T(8,128)(2,1)}, u32[]{:S(2)}, u32[]{:S(2)}) async-start(bf16[128,8,2560]{2,1,0:T(8,128)(2,1)} %fusion.14), calls=%async_computation.1 | async-start | bytes 10485760 | tf_op jit(solution)/shard_map/all_to_all | solution.py:287
  271.0 7.5 %copy-start.5 = (bf16[1,2560,768]{2,1,0:T(8,128)(2,1)S(1)}, bf16[1,2560,768]{2,1,0:T(8,128)(2,1)}, u32[]{:S(2)}) copy-start(bf16[1,2560,768]{2,1,0:T(8,128)(2,1)} %param.21) | copy-start | bytes 11796484
  278.5 7.2 %copy-start.7 = (bf16[1,768,2560]{2,1,0:T(8,128)(2,1)S(1)}, bf16[1,768,2560]{2,1,0:T(8,128)(2,1)}, u32[]{:S(2)}) copy-start(bf16[1,768,2560]{2,1,0:T(8,128)(2,1)} %param.23) | copy-start | bytes 11796484
  333.1 68.7 %all-to-all-start.3 = ((bf16[128,8,2560]{2,1,0:T(8,128)(2,1)}), bf16[128,8,2560]{2,1,0:T(8,128)(2,1)}, u32[]{:S(2)}, u32[]{:S(2)}) async-start(bf16[128,8,2560]{2,1,0:T(8,128)(2,1)} %fusion.15), calls=%async_computation.3 | async-start | bytes 10485760 | tf_op jit(solution)/shard_map/all_to_all | solution.py:287
  401.8 4.2 %copy-start.1 = (f32[256,2560]{1,0:T(8,128)S(1)}, f32[256,2560]{1,0:T(8,128)}, u32[]{:S(2)}) copy-start(f32[256,2560]{1,0:T(8,128)} %fusion.6) | copy-start | bytes 7864324
Sparse Core Ops, SparseCore 0:
  9.1 47.3 all-gather.4
  58.5 43.7 all-gather.2

commit v14 on v13

--- a/solution.py
+++ b/solution.py
@@ -223,7 +223,7 @@
         KEY_VALUE_HEADS,
         HEAD_SIZE,
         (order, live_count),
-        KEY_BLOCK // PAGE_TOKENS,
+        2 * KEY_BLOCK // PAGE_TOKENS,
     )
     attended = flash(
         queries,

time: 416 us -> 415 us (level)
  Pallas kernels: 43.2 us -> 31.1 us
  waiting for transfers between devices: 249 us -> 261 us
    pallas_call x2, Pallas kernels: 43.2 us -> 31.1 us  [flash(): pl.pallas_call(kern, grid_spec=grid_spec, out_shape=out_shape)]
    all_gather x1, waiting for transfers between devices: 14.2 us -> 26.3 us  [on_device(): segment = lax.all_gather(suffix_after, 'exp', axis=0, tiled=True)]
  transfers between devices with their start and end apart: 6 -> 6, of which waited for: 6 -> 6; matrix products, arithmetic and copies ran while one was open for 15% -> 15% of each run, Pallas kernels for 8% -> 5%
where the time goes in v14:
time: 415 us; the launch traced here: 413 us
  waiting for transfers between devices  261 us (63%)
  matrix products  67 us (16%)
  Pallas kernels  31.1 us (7%)
  starting transfers between devices  30 us (7%)
  between operations  13.7 us (3%)
  other arithmetic  9.58 us (2%)
    all_to_all x2, waiting for transfers between devices, on_device(): lax.all_to_all(outgoing, ('req', 'exp'), split_axis=0, concat_axis=0, til...  99.7 us
    all_to_all x2, waiting for transfers between devices, on_device(): lax.all_to_all(jnp.dot(inner, w_down[0], preferred_element_type=jnp.float...  97.1 us
    all_gather x1, waiting for transfers between devices, on_device(): lax.all_gather(page_pool, 'req', axis=0, tiled=True)  37.4 us
    pallas_call x2, Pallas kernels, flash(): pl.pallas_call(kern, grid_spec=grid_spec, out_shape=out_shape)  31.1 us
    all_gather x1, waiting for transfers between devices, on_device(): segment = lax.all_gather(suffix_after, 'exp', axis=0, tiled=True)  26.3 us
    all_to_all x2, starting transfers between devices, on_device(): lax.all_to_all(outgoing, ('req', 'exp'), split_axis=0, concat_axis=0, til...  16.9 us
    dot_general x2, matrix products, on_device(): up_part = jnp.dot(flat_rows, w_up[0], preferred_element_type=jnp.float32)  14.9 us
    dot_general x2, matrix products, on_device(): jnp.dot(flat_rows, w_gate[0], preferred_element_type=jnp.float32)  14.4 us
  transfers between devices with their start and end apart: 6, of which 6 were waited for; matrix products, arithmetic and copies ran while one was open for 15% of the time, Pallas kernels for 5%

profile of v14, /device:TPU:34, one launch (start us, length us, event | category | flops | bytes accessed | tf_op | source)
XLA Modules:
  0.0 413.0 jit_solution(6269763543914466124)
XLA Ops:
  6.5 0.7 all-gather.5.cloned.1.call-update
  7.3 0.8 reduce-window.21
  8.1 0.1 convert_reduce_fusion.1
  8.2 0.8 convert_reduce_fusion
  9.0 0.3 fusion.71
  9.3 0.1 copy.27
  9.4 0.1 reduce-window.22
  9.5 0.1 copy.28
  9.6 0.1 reduce-window.23
  9.7 0.6 fusion.61
  10.4 0.8 add_reduce_fusion
  11.1 0.6 select_reduce_fusion.3.order_ref
  11.8 3.3 multiply_select_fusion.refs_0_.refs_1_.refs_2_.refs_3_.refs_4_.refs_5_.refs_6_.refs_7_
  15.1 1.2 compare_convert_fusion.flags_ref
  16.3 0.1 select_reduce_fusion.4
  16.4 0.3 select_reduce_fusion
  16.8 0.5 compare_convert_fusion.1.flags_ref
  17.3 0.1 convolution_convert_fusion.4
  17.5 0.1 fusion.50
  17.6 1.4 fusion.38.refs_0_
  19.0 37.4 %all-gather.5.cloned.1.call-done = bf16[56,128,512]{2,1,0:T(8,128)(2,1)} async-done(((bf16[7,128,512]{2,1,0:T(8,128)(2,1)}), bf16[56,128,512]{2,1,0:T(8,128)(2,1)}) %all-gather.5.cloned.1.call-update) | async-done | bytes 7340048 | tf_op jit(solution)/shard_map/all_gather | solution.py:180
  56.4 19.6 %shard_map.118 = (f32[2,640,1]{2,1,0:T(8,128)}, f32[2,640,1]{2,1,0:T(8,128)}, f32[2,640,128]{2,1,0:T(8,128)}) custom-call(s32[7]{0:T(128)} %compare_convert_fusion.flags_ref, s32[56]{0:T(128)} %select_reduce_fusion.3.order_ref, bf16[128,1280]{1,0:T(8,128)(2,1)} %q_ref.3, ...), custom_call_target="tpu_custom_call" | custom-call | tf_op jit(solution)/shard_map/pallas_call | solution.py:150
  76.1 26.3 %all-gather.3.cloned.1.call-done.refs_1_ = bf16[2048,512]{1,0:T(8,128)(2,1)} async-done(((bf16[128,512]{1,0:T(8,128)(2,1)}), bf16[2048,512]{1,0:T(8,128)(2,1)}) %all-gather.3.cloned.1.call-update) | async-done | bytes 2097168 | tf_op jit(solution)/shard_map/all_gather | solution.py:215
  102.4 11.5 %shard_map.119 = bf16[128,1280]{1,0:T(8,128)(2,1)} custom-call(s32[4]{0:T(128)} %compare_convert_fusion.1.flags_ref, s32[1]{0:T(128)} %constant.56.clone.1.order_ref, bf16[128,1280]{1,0:T(8,128)(2,1)} %q_ref.3, f32[128,2048]{1,0:T(8,128)} %fusion.38.refs_0_, bf16[2048,512]{1,0:T(8,128)(2,1)} %all-gather.3.cloned.1.call-done.refs_1_, ...), custom_call_target="tpu_custom_call" | custom-call | tf_op jit(solution)/shard_map/pallas_call | solution.py:150
  113.8 4.0 fusion.22
  117.8 0.2 fusion.31
  118.1 0.1 broadcast_in_dim.136
  118.1 3.9 fusion.12
  122.1 10.3 %all-to-all-start = ((bf16[128,8,2560]{2,1,0:T(8,128)(2,1)}), bf16[128,8,2560]{2,1,0:T(8,128)(2,1)}, u32[]{:S(2)}, u32[]{:S(2)}) async-start(bf16[128,8,2560]{2,1,0:T(8,128)(2,1)} %fusion.12), calls=%async_computation | async-start | bytes 10485760 | tf_op jit(solution)/shard_map/all_to_all | solution.py:282
  132.4 3.9 fusion.13
  136.3 58.2 %all-to-all-done = bf16[128,8,2560]{2,1,0:T(8,128)(2,1)} async-done(((bf16[128,8,2560]{2,1,0:T(8,128)(2,1)}), bf16[128,8,2560]{2,1,0:T(8,128)(2,1)}, u32[]{:S(2)}, u32[]{:S(2)}) %all-to-all-start) | async-done | bytes 5242912 | tf_op jit(solution)/shard_map/all_to_all | solution.py:282
  194.5 6.6 %all-to-all-start.2 = ((bf16[128,8,2560]{2,1,0:T(8,128)(2,1)}), bf16[128,8,2560]{2,1,0:T(8,128)(2,1)}, u32[]{:S(2)}, u32[]{:S(2)}) async-start(bf16[128,8,2560]{2,1,0:T(8,128)(2,1)} %fusion.13), calls=%async_computation.2 | async-start | bytes 10485760 | tf_op jit(solution)/shard_map/all_to_all | solution.py:282
  201.1 7.5 %fusion.8 = f32[1024,768]{1,0:T(8,128)S(1)} fusion(bf16[128,8,2560]{2,1,0:T(8,128)(2,1)} %all-to-all-done, bf16[1,2560,768]{2,1,0:T(8,128)(2,1)} %param.22), kind=kOutput, calls=%fused_computation.12 | convolution fusion | flops 4026531840 | bytes 12320768 | tf_op jit(solution)/shard_map/dot_general | solution.py:285
  208.6 7.2 %multiply_convert_fusion.1 = bf16[1024,768]{1,0:T(8,128)(2,1)S(1)} fusion(f32[1024,768]{1,0:T(8,128)S(1)} %fusion.8, bf16[1,2560,768]{2,1,0:T(8,128)(2,1)S(1)} %copy-done.4, bf16[128,8,2560]{2,1,0:T(8,128)(2,1)} %all-to-all-done), kind=kOutput, calls=%fused_computation.30 | convolution fusion | flops 4031250432 | bytes 13893632 | tf_op jit(solution)/shard_map/dot_general | solution.py:284
  215.8 6.0 %fusion.14 = bf16[128,8,2560]{2,1,0:T(8,128)(2,1)} fusion(bf16[1024,768]{1,0:T(8,128)(2,1)S(1)} %multiply_convert_fusion.1, bf16[1,768,2560]{2,1,0:T(8,128)(2,1)S(1)} %copy-done.6), kind=kOutput, calls=%fused_computation.18 | convolution fusion | flops 4029153280 | bytes 10747904 | tf_op jit(solution)/shard_map/dot_general | solution.py:288
  221.8 41.4 %all-to-all-done.2 = bf16[128,8,2560]{2,1,0:T(8,128)(2,1)} async-done(((bf16[128,8,2560]{2,1,0:T(8,128)(2,1)}), bf16[128,8,2560]{2,1,0:T(8,128)(2,1)}, u32[]{:S(2)}, u32[]{:S(2)}) %all-to-all-start.2) | async-done | bytes 5242912 | tf_op jit(solution)/shard_map/all_to_all | solution.py:282
  263.2 6.6 %all-to-all-start.1 = ((bf16[128,8,2560]{2,1,0:T(8,128)(2,1)}), bf16[128,8,2560]{2,1,0:T(8,128)(2,1)}, u32[]{:S(2)}, u32[]{:S(2)}) async-start(bf16[128,8,2560]{2,1,0:T(8,128)(2,1)} %fusion.14), calls=%async_computation.1 | async-start | bytes 10485760 | tf_op jit(solution)/shard_map/all_to_all | solution.py:287
  269.8 7.5 %fusion.2 = f32[1024,768]{1,0:T(8,128)S(1)} fusion(bf16[128,8,2560]{2,1,0:T(8,128)(2,1)} %all-to-all-done.2, bf16[1,2560,768]{2,1,0:T(8,128)(2,1)} %param.22), kind=kOutput, calls=%fused_computation.6 | convolution fusion | flops 4026531840 | bytes 12320768 | tf_op jit(solution)/shard_map/dot_general | solution.py:285
  277.3 7.2 %multiply_convert_fusion = bf16[1024,768]{1,0:T(8,128)(2,1)S(1)} fusion(f32[1024,768]{1,0:T(8,128)S(1)} %fusion.2, bf16[1,2560,768]{2,1,0:T(8,128)(2,1)S(1)} %copy-done.5, bf16[128,8,2560]{2,1,0:T(8,128)(2,1)} %all-to-all-done.2), kind=kOutput, calls=%fused_computation.29 | convolution fusion | flops 4031250432 | bytes 13893632 | tf_op jit(solution)/shard_map/dot_general | solution.py:284
  284.6 6.0 %fusion.15 = bf16[128,8,2560]{2,1,0:T(8,128)(2,1)} fusion(bf16[1024,768]{1,0:T(8,128)(2,1)S(1)} %multiply_convert_fusion, bf16[1,768,2560]{2,1,0:T(8,128)(2,1)S(1)} %copy-done.7), kind=kOutput, calls=%fused_computation.19 | convolution fusion | flops 4029153280 | bytes 10747904 | tf_op jit(solution)/shard_map/dot_general | solution.py:288
  290.6 41.4 %all-to-all-done.1 = bf16[128,8,2560]{2,1,0:T(8,128)(2,1)} async-done(((bf16[128,8,2560]{2,1,0:T(8,128)(2,1)}), bf16[128,8,2560]{2,1,0:T(8,128)(2,1)}, u32[]{:S(2)}, u32[]{:S(2)}) %all-to-all-start.1) | async-done | bytes 5242912 | tf_op jit(solution)/shard_map/all_to_all | solution.py:287
  332.0 6.5 %all-to-all-start.3 = ((bf16[128,8,2560]{2,1,0:T(8,128)(2,1)}), bf16[128,8,2560]{2,1,0:T(8,128)(2,1)}, u32[]{:S(2)}, u32[]{:S(2)}) async-start(bf16[128,8,2560]{2,1,0:T(8,128)(2,1)} %fusion.15), calls=%async_computation.3 | async-start | bytes 10485760 | tf_op jit(solution)/shard_map/all_to_all | solution.py:287
  338.5 0.4 fusion.68
  339.0 0.1 fusion.49
  339.3 5.5 %fusion.6 = f32[256,2560]{1,0:T(8,128)} fusion(bf16[128,8,2560]{2,1,0:T(8,128)(2,1)} %all-to-all-done.1, bf16[128,1024]{0,1:T(8,128)(2,1)S(1)} %fusion.40, bf16[128,1024]{0,1:T(8,128)(2,1)S(1)} %bitcast_convert_fusion.1), kind=kOutput, calls=%fused_computation.10 | convolution fusion | flops 1343225856 | bytes 8388608 | tf_op jit(solution)/shard_map/dot_general | solution.py:299
  344.9 55.8 %all-to-all-done.3 = bf16[128,8,2560]{2,1,0:T(8,128)(2,1)} async-done(((bf16[128,8,2560]{2,1,0:T(8,128)(2,1)}), bf16[128,8,2560]{2,1,0:T(8,128)(2,1)}, u32[]{:S(2)}, u32[]{:S(2)}) %all-to-all-start.3) | async-done | bytes 5242912 | tf_op jit(solution)/shard_map/all_to_all | solution.py:287
  400.6 4.2 %fusion = f32[256,2560]{1,0:T(8,128)S(1)} fusion(bf16[128,8,2560]{2,1,0:T(8,128)(2,1)} %all-to-all-done.3, bf16[128,1024]{0,1:T(8,128)(2,1)S(1)} %fusion.41, bf16[128,1024]{0,1:T(8,128)(2,1)S(1)} %bitcast_convert_fusion), kind=kOutput, calls=%fused_computation.4 | convolution fusion | flops 1343225856 | bytes 8388608 | tf_op jit(solution)/shard_map/dot_general | solution.py:299
  404.8 1.3 fusion.36
  (41 shorter events, 0.4 us)
Async XLA Ops:
  6.5 332.0 %copy-start = (bf16[2560,64]{0,1:T(8,128)(2,1)S(1)}, bf16[2560,64]{0,1:T(8,128)(2,1)}, u32[]{:S(2)}) copy-start(bf16[2560,64]{0,1:T(8,128)(2,1)} %param.19) | copy-start | bytes 983044
  6.5 9.8 %copy-start.8 = (s32[1,4]{1,0:T(1,128)S(1)}, s32[1,4]{1,0:T(1,128)}, u32[]{:S(2)}) copy-start(s32[1,4]{1,0:T(1,128)} %param.15) | copy-start | bytes 52
  6.5 9.9 %copy-start.3 = (s32[128,6]{0,1:T(8,128)S(1)}, s32[128,6]{0,1:T(8,128)}, u32[]{:S(2)}) copy-start(s32[128,6]{0,1:T(8,128)} %param.20) | copy-start | bytes 9220
  6.5 49.9 %all-gather.5.cloned.1.call-start = ((), (), s32[]{:S(2)}) async-start(), calls=%async_computation.5 | async-start | bytes 8257536 | tf_op jit(solution)/shard_map/all_gather | solution.py:180
  7.3 95.1 %all-gather.3.cloned.1.call-start = ((), (), s32[]{:S(2)}) async-start(), calls=%async_computation.4 | async-start | bytes 2228224 | tf_op jit(solution)/shard_map/all_gather | solution.py:215
  76.1 37.8 %copy-start.2 = (bf16[128,2560]{1,0:T(8,128)(2,1)S(1)}, bf16[128,2560]{1,0:T(8,128)(2,1)}, u32[]{:S(2)}) copy-start(bf16[128,2560]{1,0:T(8,128)(2,1)} %param.12) | copy-start | bytes 1966084
  122.1 72.4 %all-to-all-start = ((bf16[128,8,2560]{2,1,0:T(8,128)(2,1)}), bf16[128,8,2560]{2,1,0:T(8,128)(2,1)}, u32[]{:S(2)}, u32[]{:S(2)}) async-start(bf16[128,8,2560]{2,1,0:T(8,128)(2,1)} %fusion.12), calls=%async_computation | async-start | bytes 10485760 | tf_op jit(solution)/shard_map/all_to_all | solution.py:282
  194.5 68.7 %all-to-all-start.2 = ((bf16[128,8,2560]{2,1,0:T(8,128)(2,1)}), bf16[128,8,2560]{2,1,0:T(8,128)(2,1)}, u32[]{:S(2)}, u32[]{:S(2)}) async-start(bf16[128,8,2560]{2,1,0:T(8,128)(2,1)} %fusion.13), calls=%async_computation.2 | async-start | bytes 10485760 | tf_op jit(solution)/shard_map/all_to_all | solution.py:282
  201.1 7.5 %copy-start.4 = (bf16[1,2560,768]{2,1,0:T(8,128)(2,1)S(1)}, bf16[1,2560,768]{2,1,0:T(8,128)(2,1)}, u32[]{:S(2)}) copy-start(bf16[1,2560,768]{2,1,0:T(8,128)(2,1)} %param.21) | copy-start | bytes 11796484
  208.6 7.2 %copy-start.6 = (bf16[1,768,2560]{2,1,0:T(8,128)(2,1)S(1)}, bf16[1,768,2560]{2,1,0:T(8,128)(2,1)}, u32[]{:S(2)}) copy-start(bf16[1,768,2560]{2,1,0:T(8,128)(2,1)} %param.23) | copy-start | bytes 11796484
  263.2 68.7 %all-to-all-start.1 = ((bf16[128,8,2560]{2,1,0:T(8,128)(2,1)}), bf16[128,8,2560]{2,1,0:T(8,128)(2,1)}, u32[]{:S(2)}, u32[]{:S(2)}) async-start(bf16[128,8,2560]{2,1,0:T(8,128)(2,1)} %fusion.14), calls=%async_computation.1 | async-start | bytes 10485760 | tf_op jit(solution)/shard_map/all_to_all | solution.py:287
  269.8 7.5 %copy-start.5 = (bf16[1,2560,768]{2,1,0:T(8,128)(2,1)S(1)}, bf16[1,2560,768]{2,1,0:T(8,128)(2,1)}, u32[]{:S(2)}) copy-start(bf16[1,2560,768]{2,1,0:T(8,128)(2,1)} %param.21) | copy-start | bytes 11796484
  277.3 7.2 %copy-start.7 = (bf16[1,768,2560]{2,1,0:T(8,128)(2,1)S(1)}, bf16[1,768,2560]{2,1,0:T(8,128)(2,1)}, u32[]{:S(2)}) copy-start(bf16[1,768,2560]{2,1,0:T(8,128)(2,1)} %param.23) | copy-start | bytes 11796484
  332.0 68.7 %all-to-all-start.3 = ((bf16[128,8,2560]{2,1,0:T(8,128)(2,1)}), bf16[128,8,2560]{2,1,0:T(8,128)(2,1)}, u32[]{:S(2)}, u32[]{:S(2)}) async-start(bf16[128,8,2560]{2,1,0:T(8,128)(2,1)} %fusion.15), calls=%async_computation.3 | async-start | bytes 10485760 | tf_op jit(solution)/shard_map/all_to_all | solution.py:287
  400.6 4.2 %copy-start.1 = (f32[256,2560]{1,0:T(8,128)S(1)}, f32[256,2560]{1,0:T(8,128)}, u32[]{:S(2)}) copy-start(f32[256,2560]{1,0:T(8,128)} %fusion.6) | copy-start | bytes 7864324
Sparse Core Ops, SparseCore 0:
  9.1 47.3 all-gather.4
  58.5 43.7 all-gather.2

commit v15 on v13

--- a/solution.py
+++ b/solution.py
@@ -92,7 +92,7 @@
     t, width = queries.shape
     reps = width // hs // groups
     if order is None:
-        block = KEY_BLOCK
+        block = KEY_BLOCK // 2
         n_blocks = kv_rows.shape[0] // block
         flags = (
             jnp.max(bias.reshape(t, n_blocks, block), axis=(0, 2)) > 0.5 * NEGATIVE_MASK

time: 416 us -> 420 us (level)
  transfers between devices with their start and end apart: 6 -> 6, of which waited for: 6 -> 6; matrix products, arithmetic and copies ran while one was open for 15% -> 15% of each run, Pallas kernels for 8% -> 7%
where the time goes in v15:
time: 420 us; the launch traced here: 418 us
  waiting for transfers between devices  252 us (60%)
  matrix products  67 us (16%)
  Pallas kernels  42.5 us (10%)
  starting transfers between devices  32.9 us (8%)
  between operations  13.7 us (3%)
  other arithmetic  9.69 us (2%)
    all_to_all x2, waiting for transfers between devices, on_device(): lax.all_to_all(outgoing, ('req', 'exp'), split_axis=0, concat_axis=0, til...  99.6 us
    all_to_all x2, waiting for transfers between devices, on_device(): lax.all_to_all(jnp.dot(inner, w_down[0], preferred_element_type=jnp.float...  97.1 us
    pallas_call x2, Pallas kernels, flash(): pl.pallas_call(kern, grid_spec=grid_spec, out_shape=out_shape)  42.5 us
    all_gather x1, waiting for transfers between devices, on_device(): lax.all_gather(page_pool, 'req', axis=0, tiled=True)  37.3 us
    all_to_all x2, starting transfers between devices, on_device(): lax.all_to_all(outgoing, ('req', 'exp'), split_axis=0, concat_axis=0, til...  19.7 us
    all_gather x1, waiting for transfers between devices, on_device(): segment = lax.all_gather(suffix_after, 'exp', axis=0, tiled=True)  16.8 us
    dot_general x2, matrix products, on_device(): up_part = jnp.dot(flat_rows, w_up[0], preferred_element_type=jnp.float32)  14.9 us
    dot_general x2, matrix products, on_device(): jnp.dot(flat_rows, w_gate[0], preferred_element_type=jnp.float32)  14.4 us
  transfers between devices with their start and end apart: 6, of which 6 were waited for; matrix products, arithmetic and copies ran while one was open for 15% of the time, Pallas kernels for 7%

profile of v15, /device:TPU:34, one launch (start us, length us, event | category | flops | bytes accessed | tf_op | source)
XLA Modules:
  0.0 417.8 jit_solution(16545196375972266793)
XLA Ops:
  6.5 0.7 all-gather.5.cloned.1.call-update
  7.3 0.8 reduce-window.21
  8.1 0.1 convert_reduce_fusion.1
  8.2 0.8 convert_reduce_fusion
  9.0 0.3 fusion.71
  9.3 0.1 copy.27
  9.4 0.1 reduce-window.22
  9.5 0.1 copy.28
  9.6 0.1 reduce-window.23
  9.7 0.6 fusion.61
  10.4 0.8 add_reduce_fusion
  11.1 0.6 select_reduce_fusion.3.order_ref
  11.8 3.3 multiply_select_fusion.refs_0_.refs_1_.refs_2_.refs_3_
  15.1 1.2 compare_convert_fusion.flags_ref
  16.3 0.1 select_reduce_fusion.4
  16.4 0.4 select_reduce_fusion
  16.9 0.5 compare_convert_fusion.1.flags_ref
  17.4 0.1 convolution_convert_fusion.4
  17.6 0.1 fusion.50
  17.7 1.4 fusion.38.refs_0_
  19.1 37.3 %all-gather.5.cloned.1.call-done = bf16[56,128,512]{2,1,0:T(8,128)(2,1)} async-done(((bf16[7,128,512]{2,1,0:T(8,128)(2,1)}), bf16[56,128,512]{2,1,0:T(8,128)(2,1)}) %all-gather.5.cloned.1.call-update) | async-done | bytes 7340048 | tf_op jit(solution)/shard_map/all_gather | solution.py:180
  56.4 29.1 %shard_map.118 = (f32[2,640,1]{2,1,0:T(8,128)}, f32[2,640,1]{2,1,0:T(8,128)}, f32[2,640,128]{2,1,0:T(8,128)}) custom-call(s32[14]{0:T(128)} %compare_convert_fusion.flags_ref, s32[56]{0:T(128)} %select_reduce_fusion.3.order_ref, bf16[128,1280]{1,0:T(8,128)(2,1)} %q_ref.3, f32[128,7168]{1,0:T(8,128)} %multiply_select_fusion.refs_0_.refs_1_.refs_2_.refs_3_, ...), custom_call_target="tpu_custom_call" | custom-call | tf_op jit(solution)/shard_map/pallas_call | solution.py:150
  85.5 16.8 %all-gather.3.cloned.1.call-done.refs_1_ = bf16[2048,512]{1,0:T(8,128)(2,1)} async-done(((bf16[128,512]{1,0:T(8,128)(2,1)}), bf16[2048,512]{1,0:T(8,128)(2,1)}) %all-gather.3.cloned.1.call-update) | async-done | bytes 2097168 | tf_op jit(solution)/shard_map/all_gather | solution.py:215
  102.4 13.4 %shard_map.119 = bf16[128,1280]{1,0:T(8,128)(2,1)} custom-call(s32[8]{0:T(128)} %compare_convert_fusion.1.flags_ref, s32[1]{0:T(128)} %constant.56.clone.1.order_ref, bf16[128,1280]{1,0:T(8,128)(2,1)} %q_ref.3, f32[128,2048]{1,0:T(8,128)} %fusion.38.refs_0_, bf16[2048,512]{1,0:T(8,128)(2,1)} %all-gather.3.cloned.1.call-done.refs_1_, ...), custom_call_target="tpu_custom_call" | custom-call | tf_op jit(solution)/shard_map/pallas_call | solution.py:150
  115.8 4.0 fusion.22
  119.8 0.2 fusion.31
  120.0 0.1 broadcast_in_dim.136
  120.1 3.9 fusion.12
  124.0 13.2 %all-to-all-start = ((bf16[128,8,2560]{2,1,0:T(8,128)(2,1)}), bf16[128,8,2560]{2,1,0:T(8,128)(2,1)}, u32[]{:S(2)}, u32[]{:S(2)}) async-start(bf16[128,8,2560]{2,1,0:T(8,128)(2,1)} %fusion.12), calls=%async_computation | async-start | bytes 10485760 | tf_op jit(solution)/shard_map/all_to_all | solution.py:282
  137.2 3.9 fusion.13
  141.1 58.2 %all-to-all-done = bf16[128,8,2560]{2,1,0:T(8,128)(2,1)} async-done(((bf16[128,8,2560]{2,1,0:T(8,128)(2,1)}), bf16[128,8,2560]{2,1,0:T(8,128)(2,1)}, u32[]{:S(2)}, u32[]{:S(2)}) %all-to-all-start) | async-done | bytes 5242912 | tf_op jit(solution)/shard_map/all_to_all | solution.py:282
  199.4 6.5 %all-to-all-start.2 = ((bf16[128,8,2560]{2,1,0:T(8,128)(2,1)}), bf16[128,8,2560]{2,1,0:T(8,128)(2,1)}, u32[]{:S(2)}, u32[]{:S(2)}) async-start(bf16[128,8,2560]{2,1,0:T(8,128)(2,1)} %fusion.13), calls=%async_computation.2 | async-start | bytes 10485760 | tf_op jit(solution)/shard_map/all_to_all | solution.py:282
  205.9 7.5 %fusion.8 = f32[1024,768]{1,0:T(8,128)S(1)} fusion(bf16[128,8,2560]{2,1,0:T(8,128)(2,1)} %all-to-all-done, bf16[1,2560,768]{2,1,0:T(8,128)(2,1)} %param.22), kind=kOutput, calls=%fused_computation.12 | convolution fusion | flops 4026531840 | bytes 12320768 | tf_op jit(solution)/shard_map/dot_general | solution.py:285
  213.4 7.2 %multiply_convert_fusion.1 = bf16[1024,768]{1,0:T(8,128)(2,1)S(1)} fusion(f32[1024,768]{1,0:T(8,128)S(1)} %fusion.8, bf16[1,2560,768]{2,1,0:T(8,128)(2,1)S(1)} %copy-done.4, bf16[128,8,2560]{2,1,0:T(8,128)(2,1)} %all-to-all-done), kind=kOutput, calls=%fused_computation.30 | convolution fusion | flops 4031250432 | bytes 13893632 | tf_op jit(solution)/shard_map/dot_general | solution.py:284
  220.6 6.0 %fusion.14 = bf16[128,8,2560]{2,1,0:T(8,128)(2,1)} fusion(bf16[1024,768]{1,0:T(8,128)(2,1)S(1)} %multiply_convert_fusion.1, bf16[1,768,2560]{2,1,0:T(8,128)(2,1)S(1)} %copy-done.6), kind=kOutput, calls=%fused_computation.18 | convolution fusion | flops 4029153280 | bytes 10747904 | tf_op jit(solution)/shard_map/dot_general | solution.py:288
  226.6 41.4 %all-to-all-done.2 = bf16[128,8,2560]{2,1,0:T(8,128)(2,1)} async-done(((bf16[128,8,2560]{2,1,0:T(8,128)(2,1)}), bf16[128,8,2560]{2,1,0:T(8,128)(2,1)}, u32[]{:S(2)}, u32[]{:S(2)}) %all-to-all-start.2) | async-done | bytes 5242912 | tf_op jit(solution)/shard_map/all_to_all | solution.py:282
  268.0 6.6 %all-to-all-start.1 = ((bf16[128,8,2560]{2,1,0:T(8,128)(2,1)}), bf16[128,8,2560]{2,1,0:T(8,128)(2,1)}, u32[]{:S(2)}, u32[]{:S(2)}) async-start(bf16[128,8,2560]{2,1,0:T(8,128)(2,1)} %fusion.14), calls=%async_computation.1 | async-start | bytes 10485760 | tf_op jit(solution)/shard_map/all_to_all | solution.py:287
  274.6 7.5 %fusion.2 = f32[1024,768]{1,0:T(8,128)S(1)} fusion(bf16[128,8,2560]{2,1,0:T(8,128)(2,1)} %all-to-all-done.2, bf16[1,2560,768]{2,1,0:T(8,128)(2,1)} %param.22), kind=kOutput, calls=%fused_computation.6 | convolution fusion | flops 4026531840 | bytes 12320768 | tf_op jit(solution)/shard_map/dot_general | solution.py:285
  282.1 7.2 %multiply_convert_fusion = bf16[1024,768]{1,0:T(8,128)(2,1)S(1)} fusion(f32[1024,768]{1,0:T(8,128)S(1)} %fusion.2, bf16[1,2560,768]{2,1,0:T(8,128)(2,1)S(1)} %copy-done.5, bf16[128,8,2560]{2,1,0:T(8,128)(2,1)} %all-to-all-done.2), kind=kOutput, calls=%fused_computation.29 | convolution fusion | flops 4031250432 | bytes 13893632 | tf_op jit(solution)/shard_map/dot_general | solution.py:284
  289.3 6.0 %fusion.15 = bf16[128,8,2560]{2,1,0:T(8,128)(2,1)} fusion(bf16[1024,768]{1,0:T(8,128)(2,1)S(1)} %multiply_convert_fusion, bf16[1,768,2560]{2,1,0:T(8,128)(2,1)S(1)} %copy-done.7), kind=kOutput, calls=%fused_computation.19 | convolution fusion | flops 4029153280 | bytes 10747904 | tf_op jit(solution)/shard_map/dot_general | solution.py:288
  295.4 41.4 %all-to-all-done.1 = bf16[128,8,2560]{2,1,0:T(8,128)(2,1)} async-done(((bf16[128,8,2560]{2,1,0:T(8,128)(2,1)}), bf16[128,8,2560]{2,1,0:T(8,128)(2,1)}, u32[]{:S(2)}, u32[]{:S(2)}) %all-to-all-start.1) | async-done | bytes 5242912 | tf_op jit(solution)/shard_map/all_to_all | solution.py:287
  336.7 6.5 %all-to-all-start.3 = ((bf16[128,8,2560]{2,1,0:T(8,128)(2,1)}), bf16[128,8,2560]{2,1,0:T(8,128)(2,1)}, u32[]{:S(2)}, u32[]{:S(2)}) async-start(bf16[128,8,2560]{2,1,0:T(8,128)(2,1)} %fusion.15), calls=%async_computation.3 | async-start | bytes 10485760 | tf_op jit(solution)/shard_map/all_to_all | solution.py:287
  343.3 0.4 fusion.68
  343.8 0.1 fusion.49
  344.1 5.5 %fusion.6 = f32[256,2560]{1,0:T(8,128)} fusion(bf16[128,8,2560]{2,1,0:T(8,128)(2,1)} %all-to-all-done.1, bf16[128,1024]{0,1:T(8,128)(2,1)S(1)} %fusion.40, bf16[128,1024]{0,1:T(8,128)(2,1)S(1)} %bitcast_convert_fusion.1), kind=kOutput, calls=%fused_computation.10 | convolution fusion | flops 1343225856 | bytes 8388608 | tf_op jit(solution)/shard_map/dot_general | solution.py:299
  349.6 55.8 %all-to-all-done.3 = bf16[128,8,2560]{2,1,0:T(8,128)(2,1)} async-done(((bf16[128,8,2560]{2,1,0:T(8,128)(2,1)}), bf16[128,8,2560]{2,1,0:T(8,128)(2,1)}, u32[]{:S(2)}, u32[]{:S(2)}) %all-to-all-start.3) | async-done | bytes 5242912 | tf_op jit(solution)/shard_map/all_to_all | solution.py:287
  405.4 4.2 %fusion = f32[256,2560]{1,0:T(8,128)S(1)} fusion(bf16[128,8,2560]{2,1,0:T(8,128)(2,1)} %all-to-all-done.3, bf16[128,1024]{0,1:T(8,128)(2,1)S(1)} %fusion.41, bf16[128,1024]{0,1:T(8,128)(2,1)S(1)} %bitcast_convert_fusion), kind=kOutput, calls=%fused_computation.4 | convolution fusion | flops 1343225856 | bytes 8388608 | tf_op jit(solution)/shard_map/dot_general | solution.py:299
  409.6 1.3 fusion.36
  (41 shorter events, 0.4 us)
Async XLA Ops:
  6.5 336.7 %copy-start = (bf16[2560,64]{0,1:T(8,128)(2,1)S(1)}, bf16[2560,64]{0,1:T(8,128)(2,1)}, u32[]{:S(2)}) copy-start(bf16[2560,64]{0,1:T(8,128)(2,1)} %param.19) | copy-start | bytes 983044
  6.5 9.8 %copy-start.8 = (s32[1,4]{1,0:T(1,128)S(1)}, s32[1,4]{1,0:T(1,128)}, u32[]{:S(2)}) copy-start(s32[1,4]{1,0:T(1,128)} %param.15) | copy-start | bytes 52
  6.5 9.9 %copy-start.3 = (s32[128,6]{0,1:T(8,128)S(1)}, s32[128,6]{0,1:T(8,128)}, u32[]{:S(2)}) copy-start(s32[128,6]{0,1:T(8,128)} %param.20) | copy-start | bytes 9220
  6.5 49.9 %all-gather.5.cloned.1.call-start = ((), (), s32[]{:S(2)}) async-start(), calls=%async_computation.5 | async-start | bytes 8257536 | tf_op jit(solution)/shard_map/all_gather | solution.py:180
  7.3 95.1 %all-gather.3.cloned.1.call-start = ((), (), s32[]{:S(2)}) async-start(), calls=%async_computation.4 | async-start | bytes 2228224 | tf_op jit(solution)/shard_map/all_gather | solution.py:215
  85.5 30.3 %copy-start.2 = (bf16[128,2560]{1,0:T(8,128)(2,1)S(1)}, bf16[128,2560]{1,0:T(8,128)(2,1)}, u32[]{:S(2)}) copy-start(bf16[128,2560]{1,0:T(8,128)(2,1)} %param.12) | copy-start | bytes 1966084
  124.0 75.3 %all-to-all-start = ((bf16[128,8,2560]{2,1,0:T(8,128)(2,1)}), bf16[128,8,2560]{2,1,0:T(8,128)(2,1)}, u32[]{:S(2)}, u32[]{:S(2)}) async-start(bf16[128,8,2560]{2,1,0:T(8,128)(2,1)} %fusion.12), calls=%async_computation | async-start | bytes 10485760 | tf_op jit(solution)/shard_map/all_to_all | solution.py:282
  199.4 68.7 %all-to-all-start.2 = ((bf16[128,8,2560]{2,1,0:T(8,128)(2,1)}), bf16[128,8,2560]{2,1,0:T(8,128)(2,1)}, u32[]{:S(2)}, u32[]{:S(2)}) async-start(bf16[128,8,2560]{2,1,0:T(8,128)(2,1)} %fusion.13), calls=%async_computation.2 | async-start | bytes 10485760 | tf_op jit(solution)/shard_map/all_to_all | solution.py:282
  205.9 7.5 %copy-start.4 = (bf16[1,2560,768]{2,1,0:T(8,128)(2,1)S(1)}, bf16[1,2560,768]{2,1,0:T(8,128)(2,1)}, u32[]{:S(2)}) copy-start(bf16[1,2560,768]{2,1,0:T(8,128)(2,1)} %param.21) | copy-start | bytes 11796484
  213.4 7.2 %copy-start.6 = (bf16[1,768,2560]{2,1,0:T(8,128)(2,1)S(1)}, bf16[1,768,2560]{2,1,0:T(8,128)(2,1)}, u32[]{:S(2)}) copy-start(bf16[1,768,2560]{2,1,0:T(8,128)(2,1)} %param.23) | copy-start | bytes 11796484
  268.0 68.7 %all-to-all-start.1 = ((bf16[128,8,2560]{2,1,0:T(8,128)(2,1)}), bf16[128,8,2560]{2,1,0:T(8,128)(2,1)}, u32[]{:S(2)}, u32[]{:S(2)}) async-start(bf16[128,8,2560]{2,1,0:T(8,128)(2,1)} %fusion.14), calls=%async_computation.1 | async-start | bytes 10485760 | tf_op jit(solution)/shard_map/all_to_all | solution.py:287
  274.6 7.5 %copy-start.5 = (bf16[1,2560,768]{2,1,0:T(8,128)(2,1)S(1)}, bf16[1,2560,768]{2,1,0:T(8,128)(2,1)}, u32[]{:S(2)}) copy-start(bf16[1,2560,768]{2,1,0:T(8,128)(2,1)} %param.21) | copy-start | bytes 11796484
  282.1 7.2 %copy-start.7 = (bf16[1,768,2560]{2,1,0:T(8,128)(2,1)S(1)}, bf16[1,768,2560]{2,1,0:T(8,128)(2,1)}, u32[]{:S(2)}) copy-start(bf16[1,768,2560]{2,1,0:T(8,128)(2,1)} %param.23) | copy-start | bytes 11796484
  336.7 68.7 %all-to-all-start.3 = ((bf16[128,8,2560]{2,1,0:T(8,128)(2,1)}), bf16[128,8,2560]{2,1,0:T(8,128)(2,1)}, u32[]{:S(2)}, u32[]{:S(2)}) async-start(bf16[128,8,2560]{2,1,0:T(8,128)(2,1)} %fusion.15), calls=%async_computation.3 | async-start | bytes 10485760 | tf_op jit(solution)/shard_map/all_to_all | solution.py:287
  405.4 4.2 %copy-start.1 = (f32[256,2560]{1,0:T(8,128)S(1)}, f32[256,2560]{1,0:T(8,128)}, u32[]{:S(2)}) copy-start(f32[256,2560]{1,0:T(8,128)} %fusion.6) | copy-start | bytes 7864324
Sparse Core Ops, SparseCore 0:
  9.1 47.3 all-gather.4
  58.5 43.7 all-gather.2
